TPU v7x, 256 devices: a whole 4x4x8 slice. The times are simulated.
256 devices in a mesh: req: 4 (over x), tp: 64 (over z, y, core).
Axes of the slice: x: 4, y: 4, z: 8, core: 2. Of those that a mesh axis runs over, the one named last changes fastest.
Arguments:
- hidden: bfloat16 [256, 4096], P('req', 'tp'), may hold values from -6 to 6
- norm_gain: bfloat16 [4096], P('tp'), may hold values from 0.099609375 to 1.8984375
- w_qkv: bfloat16 [4096, 5120], P('tp'), may hold values from -0.1875 to 0.1875
- w_out: bfloat16 [4096, 4096], P('tp'), may hold values from -0.09375 to 0.09375
- cache_keys: bfloat16 [4, 65536, 512], P('req', 'tp')
- cache_values: bfloat16 [4, 65536, 512], P('req', 'tp'), may hold values from -6 to 6
- parents: int32 [4, 64], P('req'), may hold values from -1 to 62, as said below
- draft_counts: int32 [4], P('req'), may hold values from 1 to 64, as said below
- cache_lengths: int32 [4], P('req'), may hold values from 1 to 65536, as said below
Outputs:
- updated: bfloat16 [256, 4096], P('req', 'tp')
Inputs may be any that keep to these rules, and one draw needn't show every extreme that they name: parents[r, 0] = -1 and 0 <= parents[r, i] < i for i >= 1. `draft_counts`: some request has all 64 tree tokens live. `cache_lengths`: some request has a full cache of 65536 positions.
All inputs are finite; a program needn't handle non-finite values.
Results may differ from a plain program's by a relative error of at most 0.0065.
The roundings to bfloat16 on the way count: a program that leaves them out, or rounds other values in their place, can miss the bound.
Values may be sent and summed in bfloat16 or wider, within the bound.
No kernel may reach another device: no remote copies, remote signals or barrier semaphores. Data moves between devices by JAX's collectives and lax.ppermute only.
A program may use at most 64 MiB of HBM per device.

v0:
```python
import jax
import jax.numpy as jnp
from jax import lax
from jax.sharding import PartitionSpec as P

HEADS = 32
KV_HEADS = 4
HEAD = 128


NEGATIVE = -1e30


def tree_reach(parents):
    width = parents.shape[1]
    places = jnp.arange(width, dtype=jnp.int32)
    parent_link = (parents[:, :, None] == places[None, None, :]).astype(jnp.float32)
    identity = (places[:, None] == places[None, :]).astype(jnp.float32)
    reached = jnp.minimum(parent_link + identity[None], 1.0)
    for rounds in range(width.bit_length()):
        reached = jnp.minimum(
            jnp.einsum("rij,rjk->rik", reached, reached, precision=lax.Precision.HIGHEST), 1.0
        )
    return reached


def on_device(
    hidden, norm_gain, w_qkv, w_out, cache_keys, cache_values, parents, draft_counts, cache_lengths
):
    tp_count = lax.axis_size("tp")
    tp_rank = lax.axis_index("tp")
    model_width = w_out.shape[1]
    kv_width = KV_HEADS * HEAD
    groups = HEADS // KV_HEADS
    tree = parents.shape[1]
    requests = cache_keys.shape[0]
    places_dev = cache_keys.shape[1]
    inputs = hidden.astype(jnp.float32)
    all_rows = inputs.shape[0]
    own_count = all_rows // tp_count
    scaled = (inputs * norm_gain.astype(jnp.float32)[None, :]).astype(jnp.bfloat16)
    local_squares = jnp.sum(inputs * inputs, axis=1)
    raw, square_sum = lax.psum(
        (jnp.dot(scaled, w_qkv, preferred_element_type=jnp.float32), local_squares), "tp"
    )
    qkv = (raw * lax.rsqrt(square_sum / model_width + 1e-05)[:, None]).astype(jnp.bfloat16)
    query = qkv[:, :model_width]
    own_tokens = lax.dynamic_slice_in_dim(qkv, tp_rank * own_count, own_count, 0)[:, model_width:]
    own_keys = own_tokens[:, :kv_width].reshape(own_count, KV_HEADS, HEAD)
    own_values = own_tokens[:, kv_width:].reshape(own_count, KV_HEADS, HEAD)
    scale = HEAD ** (-0.5)
    key_index = tp_rank * own_count + jnp.arange(own_count, dtype=jnp.int32)
    key_request = key_index // tree
    key_place = key_index % tree
    query_request = jnp.arange(all_rows, dtype=jnp.int32) // tree
    reached = tree_reach(parents).reshape(all_rows, tree)
    column_pick = (jnp.arange(tree, dtype=jnp.int32)[:, None] == key_place[None, :]).astype(
        jnp.float32
    )
    on_path = jnp.dot(reached, column_pick, precision=lax.Precision.HIGHEST) > 0.5
    request_pick = jnp.arange(requests, dtype=jnp.int32)[:, None] == key_request[None, :]
    key_count = jnp.sum(jnp.where(request_pick, draft_counts[:, None], 0), axis=0)
    tree_mask = (
        on_path
        & (query_request[:, None] == key_request[None, :])
        & (key_place < key_count)[None, :]
    )
    query_heads = query.reshape(all_rows, KV_HEADS, groups, HEAD)
    query_blocks = query.reshape(requests, tree, KV_HEADS, groups, HEAD)
    first_place = tp_rank * places_dev
    positions = first_place + jnp.arange(places_dev, dtype=jnp.int32)

    def cache_scores(items):
        queries, keys, length = items
        scores = (
            jnp.einsum(
                "tkgd,pkd->tkgp",
                queries,
                keys.reshape(places_dev, KV_HEADS, HEAD),
                preferred_element_type=jnp.float32,
            )
            * scale
        )
        return jnp.where((positions < length)[None, None, None, :], scores, NEGATIVE)

    stored_scores = lax.map(cache_scores, (query_blocks, cache_keys, cache_lengths))
    tree_scores = (
        jnp.einsum("tkgd,ukd->tkgu", query_heads, own_keys, preferred_element_type=jnp.float32)
        * scale
    )
    tree_scores = jnp.where(tree_mask[:, None, None, :], tree_scores, NEGATIVE)
    local_top = jnp.maximum(
        jnp.max(stored_scores, axis=-1).reshape(all_rows, KV_HEADS, groups),
        jnp.max(tree_scores, axis=-1),
    )
    top = lax.pmax(local_top, "tp")
    top_blocks = top.reshape(requests, tree, KV_HEADS, groups)

    def cache_mix(items):
        block_scores, block_top, values = items
        exponent = jnp.exp(block_scores - block_top[..., None])
        block_totals = jnp.sum(exponent, axis=-1)
        block_mixed = jnp.einsum(
            "tkgp,pkd->tkgd",
            exponent.astype(jnp.bfloat16),
            values.reshape(places_dev, KV_HEADS, HEAD),
            preferred_element_type=jnp.float32,
        )
        return (block_mixed, block_totals)

    mixed, totals = lax.map(cache_mix, (stored_scores, top_blocks, cache_values))
    tree_exp = jnp.exp(tree_scores - top[..., None])
    mixed = mixed.reshape(all_rows, KV_HEADS, groups, HEAD) + jnp.einsum(
        "tkgu,ukd->tkgd",
        tree_exp.astype(jnp.bfloat16),
        own_values,
        preferred_element_type=jnp.float32,
    )
    totals = totals.reshape(all_rows, KV_HEADS, groups) + jnp.sum(tree_exp, axis=-1)
    totals_all = lax.psum(totals.reshape(all_rows, HEADS), "tp")
    mixed_cols = lax.psum_scatter(
        mixed.reshape(all_rows, model_width), "tp", scatter_dimension=1, tiled=True
    )
    columns = w_out.shape[0]
    column_head = (tp_rank * columns + jnp.arange(columns, dtype=jnp.int32)) // HEAD
    head_pick = (jnp.arange(HEADS, dtype=jnp.int32)[:, None] == column_head[None, :]).astype(
        jnp.float32
    )
    column_totals = jnp.dot(totals_all, head_pick, precision=lax.Precision.HIGHEST)
    attended = (mixed_cols / column_totals).astype(jnp.bfloat16)
    partial_terms = jnp.dot(attended, w_out, preferred_element_type=jnp.float32)
    projected = lax.psum_scatter(partial_terms, "tp", scatter_dimension=1, tiled=True)
    return (inputs + projected).astype(jnp.bfloat16)


def solution(mesh):
    placed = (
        P("req", "tp"),
        P("tp"),
        P("tp", None),
        P("tp", None),
        P("req", "tp", None),
        P("req", "tp", None),
        P("req", None),
        P("req"),
        P("req"),
    )
    return jax.shard_map(
        on_device, mesh=mesh, in_specs=placed, out_specs=P("req", "tp"), check_vma=False
    )
```

profile of v0, /device:TPU:1, one launch (start us, length us, event | category | flops | bytes accessed | tf_op | source)
XLA Modules:
  0.0 864.5 jit_solution(1173911116524621926)
XLA Ops:
  6.5 0.7 convert_element_type.75
  7.3 0.4 copy-done
  7.6 2.1 fusion.28
  9.8 0.8 fusion.24
  11.3 0.8 fusion.27
  13.1 128.3 %psum.22 = f32[64]{0:T(128)S(1)} all-reduce(f32[64]{0:T(128)S(1)} %fusion.24), channel_id=1, replica_groups=mesh['req'=4,'tp'=64] {'tp'}, use_global_device_ids=true, to_apply=%region_2.0 | all-reduce | flops 64 | bytes 512 | tf_op jit(solution)/shard_map/psum | solution.py:43
  142.1 1.3 reshape.297
  143.5 1.3 reshape.299
  145.2 56.7 %all-reduce.2.cloned.1.call-done = f32[64,5120]{1,0:T(8,128)} async-done(((f32[64,5120]{1,0:T(8,128)}), f32[64,5120]{1,0:T(8,128)}) %all-reduce.2.cloned.1.call-update) | async-done | bytes 1310736 | tf_op jit(solution)/shard_map/psum | solution.py:43
  201.9 1.5 multiply_convert_fusion
  203.5 2.4 fusion.19
  205.9 4.7 bitcast_reduce_fusion
  210.7 245.7 %pmax.7 = f32[64,4,8]{2,0,1:T(8,128)S(1)} all-reduce(f32[64,4,8]{2,0,1:T(8,128)S(1)} %bitcast_maximum_fusion), channel_id=1, replica_groups=mesh['req'=4,'tp'=64] {'tp'}, use_global_device_ids=true, to_apply=%region_4.5 | all-reduce | flops 2048 | bytes 16384 | tf_op jit(solution)/shard_map/pmax | solution.py:96
  456.4 0.7 convert_bitcast_fusion
  457.2 4.6 fusion.9
  461.9 2.0 copy.38
  464.0 4.5 fusion.1
  468.7 246.3 %psum.23 = f32[64,32]{0,1:T(8,128)S(1)} all-reduce(f32[64,32]{0,1:T(8,128)S(1)} %bitcast_add_fusion), channel_id=1, replica_groups=mesh['req'=4,'tp'=64] {'tp'}, use_global_device_ids=true, to_apply=%region_7.8 | all-reduce | flops 2048 | bytes 16384 | tf_op jit(solution)/shard_map/psum | solution.py:120
  714.9 0.8 copy.35
  715.8 0.2 fusion.12
  716.0 1.9 convolution_bitcast_fusion
  717.9 138.6 %reduce-scatter.9.cloned.1.call-done = f32[64,64]{1,0:T(8,128)} async-done(((f32[4096,64]{1,0:T(8,128)}), f32[64,64]{1,0:T(8,128)}) %reduce-scatter.9.cloned.1.call-update) | async-done | bytes 16400
  856.6 0.8 copy.37
  857.4 0.6 fusion.25
  (32 shorter events, 1.9 us)
Async XLA Ops:
  6.5 1.1 copy-start
  6.5 195.3 %all-reduce.2.cloned.1.call-start = ((), (), s32[]{:S(2)}) async-start(), calls=%async_computation.2 | async-start | bytes 2621440 | tf_op jit(solution)/shard_map/psum | solution.py:43
  9.8 705.2 %reduce-scatter.7.cloned.1.call-start = ((), (), s32[]{:S(2)}) async-start(), calls=%async_computation.3 | async-start | bytes 2129920
  461.9 6.7 copy-start.2
  461.9 254.1 %copy-start.1 = (bf16[64,4096]{1,0:T(8,128)(2,1)S(1)}, bf16[64,4096]{1,0:T(8,128)(2,1)}, u32[]{:S(2)}) copy-start(bf16[64,4096]{1,0:T(8,128)(2,1)} %param.12) | copy-start | bytes 1572868
  463.9 393.5 %copy-start.3 = (bf16[64,64]{1,0:T(8,128)(2,1)S(1)}, bf16[64,64]{1,0:T(8,128)(2,1)}, u32[]{:S(2)}) copy-start(bf16[64,64]{1,0:T(8,128)(2,1)} %param.9) | copy-start | bytes 24580
  463.9 392.6 %reduce-scatter.9.cloned.1.call-start = ((), (), s32[]{:S(2)}) async-start(), calls=%async_computation.4 | async-start | bytes 2129920
Sparse Core Ops, SparseCore 0:
  10.8 191.0 all-reduce.1
  464.1 138.9 reduce-scatter.6
  718.0 138.4 reduce-scatter.8
where the time goes:
time: 869 us; the launch traced here: 865 us
  blocking collectives  620 us (71%)
  waiting for transfers between devices  195 us (22%)
  matrix products  17.3 us (2%)
  between operations  14.6 us (2%)
  other arithmetic  9.83 us (1%)
    psum x1, blocking collectives, on_device(): totals_all = lax.psum(totals.reshape(all_rows, HEADS), 'tp')  246 us
    pmax x1, blocking collectives, on_device(): top = lax.pmax(local_top, 'tp')  246 us
    unnamed x5, waiting for transfers between devices  139 us
    psum x1, blocking collectives, on_device(): lax.psum((jnp.dot(scaled, w_qkv, preferred_element_type=jnp.float32), loc...  128 us
    psum x1, waiting for transfers between devices, on_device(): lax.psum((jnp.dot(scaled, w_qkv, preferred_element_type=jnp.float32), loc...  56.7 us
  transfers between devices with their start and end apart: 3, of which 2 were waited for; matrix products, arithmetic and copies ran while one was open for 1% of the time, Pallas kernels for 0%

commit v1 on v0

v1 whole, which is shorter than its diff:
```python
import jax
import jax.numpy as jnp
from jax import lax
from jax.sharding import PartitionSpec as P

HEADS = 32
KV_HEADS = 4
HEAD = 128


NEGATIVE = -1e30


def tree_reach(parents):
    width = parents.shape[1]
    places = jnp.arange(width, dtype=jnp.int32)
    parent_link = (parents[:, :, None] == places[None, None, :]).astype(jnp.float32)
    identity = (places[:, None] == places[None, :]).astype(jnp.float32)
    reached = jnp.minimum(parent_link + identity[None], 1.0)
    for rounds in range(width.bit_length()):
        reached = jnp.minimum(
            jnp.einsum("rij,rjk->rik", reached, reached, precision=lax.Precision.HIGHEST), 1.0
        )
    return reached


def spread(pieces):
    return lax.all_to_all(pieces, "tp", 0, 0, tiled=True)


def on_device(
    hidden, norm_gain, w_qkv, w_out, cache_keys, cache_values, parents, draft_counts, cache_lengths
):
    tp_count = lax.axis_size("tp")
    tp_rank = lax.axis_index("tp")
    model_width = w_out.shape[1]
    kv_width = KV_HEADS * HEAD
    groups = HEADS // KV_HEADS
    tree = parents.shape[1]
    places_dev = cache_keys.shape[1]
    inputs = hidden.astype(jnp.float32)
    all_rows = inputs.shape[0]
    own_count = all_rows // tp_count
    proj_width = w_qkv.shape[1]

    scaled = (inputs * norm_gain.astype(jnp.float32)[None, :]).astype(jnp.bfloat16)
    local_squares = jnp.sum(inputs * inputs, axis=1)
    partial = jnp.dot(scaled, w_qkv, preferred_element_type=jnp.float32)
    extended = jnp.concatenate(
        [partial, jnp.broadcast_to(local_squares[:, None], (all_rows, 128))], axis=1
    )
    gathered = spread(extended.reshape(tp_count, own_count, proj_width + 128))
    own_sum = jnp.sum(gathered, axis=0)
    square_sum = own_sum[:, proj_width]
    own_qkv = (
        own_sum[:, :proj_width] * lax.rsqrt(square_sum / model_width + 1e-05)[:, None]
    ).astype(jnp.bfloat16)
    own_queries = own_qkv[:, :model_width]
    query = spread(
        jnp.broadcast_to(own_queries[None], (tp_count, own_count, model_width))
    ).reshape(all_rows, model_width)
    own_tokens = own_qkv[:, model_width:]
    own_keys = own_tokens[:, :kv_width].reshape(own_count, KV_HEADS, HEAD)
    own_values = own_tokens[:, kv_width:].reshape(own_count, KV_HEADS, HEAD)

    scale = HEAD ** (-0.5)
    key_index = tp_rank * own_count + jnp.arange(own_count, dtype=jnp.int32)
    key_place = key_index % tree
    reached = tree_reach(parents).reshape(all_rows, tree)
    column_pick = (jnp.arange(tree, dtype=jnp.int32)[:, None] == key_place[None, :]).astype(
        jnp.float32
    )
    on_path = jnp.dot(reached, column_pick, precision=lax.Precision.HIGHEST) > 0.5
    tree_mask = on_path & (key_place < draft_counts[0])[None, :]

    query_heads = query.reshape(all_rows, KV_HEADS, groups, HEAD)
    positions = tp_rank * places_dev + jnp.arange(places_dev, dtype=jnp.int32)
    valid = positions < cache_lengths[0]
    cache_scores = (
        jnp.einsum(
            "tkgd,pkd->tkgp",
            query_heads,
            cache_keys[0].reshape(places_dev, KV_HEADS, HEAD),
            preferred_element_type=jnp.float32,
        )
        * scale
    )
    cache_scores = jnp.where(valid[None, None, None, :], cache_scores, NEGATIVE)
    tree_scores = (
        jnp.einsum("tkgd,ukd->tkgu", query_heads, own_keys, preferred_element_type=jnp.float32)
        * scale
    )
    tree_scores = jnp.where(tree_mask[:, None, None, :], tree_scores, NEGATIVE)
    local_top = jnp.maximum(jnp.max(cache_scores, axis=-1), jnp.max(tree_scores, axis=-1))
    cache_exp = jnp.where(
        valid[None, None, None, :], jnp.exp(cache_scores - local_top[..., None]), 0.0
    )
    tree_exp = jnp.where(
        tree_mask[:, None, None, :], jnp.exp(tree_scores - local_top[..., None]), 0.0
    )
    totals = jnp.sum(cache_exp, axis=-1) + jnp.sum(tree_exp, axis=-1)
    mixed = jnp.einsum(
        "tkgp,pkd->tkgd",
        cache_exp.astype(jnp.bfloat16),
        cache_values[0].reshape(places_dev, KV_HEADS, HEAD),
        preferred_element_type=jnp.float32,
    ) + jnp.einsum(
        "tkgu,ukd->tkgd",
        tree_exp.astype(jnp.bfloat16),
        own_values,
        preferred_element_type=jnp.float32,
    )

    columns = w_out.shape[0]
    per_head = HEAD // columns
    owner_mixed = jnp.swapaxes(mixed.reshape(all_rows, tp_count, columns), 0, 1)
    owner_top = jnp.repeat(jnp.swapaxes(local_top.reshape(all_rows, HEADS), 0, 1), per_head, 0)
    owner_totals = jnp.repeat(jnp.swapaxes(totals.reshape(all_rows, HEADS), 0, 1), per_head, 0)
    packed = jnp.concatenate(
        [owner_mixed, owner_top[..., None], owner_totals[..., None]], axis=2
    )
    got = spread(packed)
    source_top = got[:, :, columns]
    top = jnp.max(source_top, axis=0)
    rescale = jnp.exp(source_top - top[None])
    total = jnp.sum(rescale * got[:, :, columns + 1], axis=0)
    mixed_cols = jnp.sum(rescale[..., None] * got[:, :, :columns], axis=0)
    attended = (mixed_cols / total[:, None]).astype(jnp.bfloat16)

    partial_terms = jnp.dot(attended, w_out, preferred_element_type=jnp.float32)
    out_cols = model_width // tp_count
    terms = spread(jnp.swapaxes(partial_terms.reshape(all_rows, tp_count, out_cols), 0, 1))
    projected = jnp.sum(terms, axis=0)
    return (inputs + projected).astype(jnp.bfloat16)


def solution(mesh):
    placed = (
        P("req", "tp"),
        P("tp"),
        P("tp", None),
        P("tp", None),
        P("req", "tp", None),
        P("req", "tp", None),
        P("req", None),
        P("req"),
        P("req"),
    )
    return jax.shard_map(
        on_device, mesh=mesh, in_specs=placed, out_specs=P("req", "tp"), check_vma=False
    )
```

time: 869 us -> 235 us (0.27)
  blocking collectives: 620 us -> 90.1 us
  waiting for transfers between devices: 195 us -> 46.6 us
  local copies, waits for them, and re-layouts: 7.06 us -> 33.7 us
  starting transfers between devices: 0.09 us -> 19.6 us
  other arithmetic: 9.83 us -> 26.9 us
  between operations: 14.6 us -> 2.33 us
    psum x2 -> x0, blocking collectives: 375 us -> none  [the longest x1 246 us: on_device(): totals_all = lax.psum(totals.reshape(all_rows, HEADS), 'tp')]
    pmax x1 -> x0, blocking collectives: 246 us -> none  [on_device(): top = lax.pmax(local_top, 'tp')]
    unnamed x5 -> x0, waiting for transfers between devices: 139 us -> none
    all_to_all x0 -> x2, blocking collectives: none -> 90.1 us  [spread(): return lax.all_to_all(pieces, 'tp', 0, 0, tiled=True)]
    psum x1 -> x0, waiting for transfers between devices: 56.7 us -> none  [on_device(): lax.psum((jnp.dot(scaled, w_qkv, preferred_element_type=jnp.float32), loc...]
    all_to_all x0 -> x2, waiting for transfers between devices: none -> 46.6 us  [spread(): return lax.all_to_all(pieces, 'tp', 0, 0, tiled=True)]
    all_to_all x0 -> x2, starting transfers between devices: none -> 19.6 us  [spread(): return lax.all_to_all(pieces, 'tp', 0, 0, tiled=True)]
  transfers between devices with their start and end apart: 3 -> 2, of which waited for: 2 -> 2; matrix products, arithmetic and copies ran while one was open for 1% -> 2% of each run, Pallas kernels for 0% -> 0%
where the time goes in v1:
time: 235 us
  blocking collectives  90.1 us (38%)
  waiting for transfers between devices  46.6 us (20%)
  local copies, waits for them, and re-layouts  33.7 us (14%)
  other arithmetic  26.9 us (11%)
  starting transfers between devices  19.6 us (8%)
  matrix products  15.4 us (7%)
    all_to_all x2, blocking collectives, spread(): return lax.all_to_all(pieces, 'tp', 0, 0, tiled=True)  90.1 us
    all_to_all x2, waiting for transfers between devices, spread(): return lax.all_to_all(pieces, 'tp', 0, 0, tiled=True)  46.6 us
    all_to_all x2, starting transfers between devices, spread(): return lax.all_to_all(pieces, 'tp', 0, 0, tiled=True)  19.6 us
    unnamed x19, local copies, waits for them, and re-layouts  11.1 us
    all_to_all x2, other arithmetic, spread(): return lax.all_to_all(pieces, 'tp', 0, 0, tiled=True)  7.6 us
    reduce_sum x1, other arithmetic, on_device(): totals = jnp.sum(cache_exp, axis=-1) + jnp.sum(tree_exp, axis=-1)  4.71 us
  transfers between devices with their start and end apart: 2, of which 2 were waited for; matrix products, arithmetic and copies ran while one was open for 2% of the time, Pallas kernels for 0%

profile of v1, /device:TPU:1, one launch (start us, length us, event | category | flops | bytes accessed | tf_op | source)
XLA Modules:
  0.0 234.7 jit_solution(16008979579413713506)
XLA Ops:
  2.8 2.5 %copy.35 = f32[64,1,5248]{2,1,0:T(1,128)} copy(f32[64,1,5248]{2,0,1:T(8,128)S(1)} %maximum_bitcast_fusion) | data formatting | bytes 2686976 | tf_op jit(solution)/shard_map/reshape | solution.py:52
  5.2 13.1 %all-to-all-start = ((f32[64,1,5248]{2,1,0:T(1,128)}), f32[64,1,5248]{2,1,0:T(1,128)S(1)}, u32[]{:S(2)}, u32[]{:S(2)}) async-start(f32[64,1,5248]{2,1,0:T(1,128)} %copy.35), calls=%async_computation | async-start | bytes 2686976 | tf_op jit(solution)/shard_map/all_to_all | solution.py:28
  19.2 33.5 %all-to-all-done = f32[64,1,5248]{2,1,0:T(1,128)S(1)} async-done(((f32[64,1,5248]{2,1,0:T(1,128)}), f32[64,1,5248]{2,1,0:T(1,128)S(1)}, u32[]{:S(2)}, u32[]{:S(2)}) %all-to-all-start) | async-done | bytes 1343520 | tf_op jit(solution)/shard_map/all_to_all | solution.py:28
  56.3 3.8 %reduce.5 = bf16[64,4096]{1,0:T(8,128)(2,1)S(1)} reduce(bf16[64,1,4096]{2,1,0:T(2,128)(2,1)S(1)} %broadcast_in_dim.83, bf16[]{:T(256)} %broadcast.135), dimensions={1}, to_apply=%broadcast_in_dim.83.reduce_sub_computation | reduce | bytes 1048578 | tf_op jit(solution)/shard_map/broadcast_in_dim | solution.py:60
  61.3 6.5 %all-to-all-start.1 = ((bf16[64,2,2048]{2,1,0:T(2,128)(2,1)}), bf16[64,2,2048]{2,1,0:T(2,128)(2,1)S(1)}, u32[]{:S(2)}, u32[]{:S(2)}) async-start(bf16[64,2,2048]{2,1,0:T(2,128)(2,1)} %reshape.283), calls=%async_computation.1 | async-start | bytes 1048576 | tf_op jit(solution)/shard_map/all_to_all | solution.py:28
  72.3 13.1 %all-to-all-done.1 = bf16[64,2,2048]{2,1,0:T(2,128)(2,1)S(1)} async-done(((bf16[64,2,2048]{2,1,0:T(2,128)(2,1)}), bf16[64,2,2048]{2,1,0:T(2,128)(2,1)S(1)}, u32[]{:S(2)}, u32[]{:S(2)}) %all-to-all-start.1) | async-done | bytes 524320 | tf_op jit(solution)/shard_map/all_to_all | solution.py:28
  86.0 3.1 %reduce.3 = bf16[64,4096]{1,0:T(8,128)(2,1)S(1)} reduce(bf16[64,1,4096]{2,1,0:T(2,128)(2,1)S(1)} %reshape.284, bf16[]{:T(256)} %constant.50), dimensions={1}, to_apply=%all_to_all.13.reduce_sub_computation | reduce | bytes 1048578 | tf_op jit(solution)/shard_map/all_to_all | solution.py:28
  89.2 2.4 %fusion.20 = f32[4,1,64,8]{3,1,2,0:T(1,128)S(1)} fusion(bf16[64,4,8,128]{3,2,1,0:T(8,128)(2,1)S(1)} %bitcast.130, bf16[1,5120]{1,0:T(2,128)(2,1)S(1)} %fusion.32), kind=kOutput, calls=%fused_computation.30 | convolution fusion | flops 524288 | bytes 534528 | tf_op jit(solution)/shard_map/tkgd,ukd->tkgu/dot_general | solution.py:90
  91.6 4.7 %bitcast_reduce_fusion = (f32[64,4,8]{2,0,1:T(8,128)S(1)}, f32[4,64,8,1024]{3,2,1,0:T(8,128)}) fusion(pred[1024]{0:T(1024)(128)(4,1)S(1)} %add_compare_fusion, bf16[1024,4,128,1]{2,1,0,3:T(4,128)(2,1)S(1)} %bitcast.129, bf16[64,4,8,128]{3,2,1,0:T(8,128)(2,1)S(1)} %bitcast.131), kind=kOutput, calls=%fused_computation.1 | convolution fusion | flops 543160320 | bytes 9970688 | tf_op jit(solution)/shard_map/tkgd,pkd->tkgp/dot_general | solution.py:80
  96.6 4.7 %fusion.2 = f32[64,4,8]{2,0,1:T(8,128)S(1)} fusion(f32[4,64,8,1024]{3,2,1,0:T(8,128)} %get-tuple-element.12, f32[64,4,8]{2,0,1:T(8,128)S(1)} %fusion.24, pred[1024]{0:T(1024)(128)(4,1)S(1)} %add_compare_fusion), kind=kLoop, calls=%fused_computation.5 | loop fusion | flops 10483712 | bytes 8406016 | tf_op jit(solution)/shard_map/reduce_sum | solution.py:101
  101.4 4.6 %fusion.12 = f32[64,4,8,128]{3,2,0,1:T(8,128)S(1)} fusion(f32[4,64,8,1024]{3,2,1,0:T(8,128)} %get-tuple-element.12, f32[64,4,8]{2,0,1:T(8,128)S(1)} %fusion.24, pred[1024]{0:T(1024)(128)(4,1)S(1)} %add_compare_fusion, bf16[1024,4,128,1]{2,1,0,3:T(4,128)(2,1)S(1)} %bitcast.133, f32[4,64,8]{2,1,0:T(8,128)S(1)} %get-tuple-element.5, f32[4,128]{1,0:T(4,128)S(1)} %bitcast.138), kind=kOutput, calls=%fused_computation.16 | convolution fusion | flops 547880960 | bytes 10505216 | tf_op jit(solution)/shard_map/tkgp,pkd->tkgd/dot_general | solution.py:102
  109.1 2.9 %copy.44 = f32[64,64,1]{2,0,1:T(8,128)} copy(f32[64,64,1]{1,0,2:T(8,128)S(1)} %bitcast.136) | data formatting | bytes 32768 | tf_op jit(solution)/shard_map/broadcast_in_dim;reshape | solution.py:120
  112.0 2.9 %copy.45 = f32[64,64,1]{2,0,1:T(8,128)} copy(f32[64,64,1]{1,0,2:T(8,128)S(1)} %bitcast.137) | data formatting | bytes 32768 | tf_op jit(solution)/shard_map/broadcast_in_dim;reshape | solution.py:120
  114.9 3.4 %pad_maximum_fusion = f32[64,64,66]{2,0,1:T(8,128)S(1)} fusion(f32[64,64,1]{2,0,1:T(8,128)} %copy.45, f32[64,64,1]{2,0,1:T(8,128)} %copy.44, f32[64,64,64]{2,0,1:T(8,128)S(1)} %bitcast.128), kind=kLoop, calls=%fused_computation.12 | loop fusion | flops 540672 | bytes 2162688 | tf_op jit(solution)/shard_map/concatenate | solution.py:119
  119.5 55.2 %all_to_all.20 = f32[64,64,66]{2,1,0:T(8,128)S(1)} all-to-all(f32[64,64,66]{2,1,0:T(8,128)S(1)} %copy.46), channel_id=1, replica_groups=mesh['req'=4,'tp'=64] {'tp'}, dimensions={0} | all-to-all | bytes 2162688 | tf_op jit(solution)/shard_map/all_to_all | solution.py:28
  174.7 3.2 %fusion.48 = (f32[64,64,1]{2,1,0:T(8,128)}, f32[64]{0:T(128)S(1)}, f32[64,64,1]{2,1,0:T(8,128)}) fusion(f32[64,64,66]{2,1,0:T(8,128)S(1)} %all_to_all.20), kind=kLoop, calls=%fused_computation.77 | loop fusion | flops 4032 | bytes 65792 | tf_op jit(solution)/shard_map/slice | solution.py:126
  177.9 2.3 copy.59
  180.2 2.3 copy.58
  184.7 2.0 reshape.271
  186.7 2.6 %copy.75 = f32[64,64,64]{2,0,1:T(8,128)} copy(f32[64,64,64]{2,1,0:T(8,128)S(1)} %reshape.271) | data formatting | bytes 2097152 | tf_op jit(solution)/shard_map/reshape | solution.py:132
  189.2 2.7 %reshape.285 = f32[64,1,4096]{2,1,0:T(1,128)S(1)} reshape(f32[64,64,64]{2,1,0:T(8,128)} %bitcast.127) | data formatting | bytes 2097152
  191.9 34.9 %all_to_all.21 = f32[64,1,4096]{2,1,0:T(1,128)S(1)} all-to-all(f32[64,1,4096]{2,1,0:T(1,128)S(1)} %reshape.285), channel_id=1, replica_groups=mesh['req'=4,'tp'=64] {'tp'}, dimensions={0} | all-to-all | bytes 2097152 | tf_op jit(solution)/shard_map/all_to_all | solution.py:28
  227.4 4.5 %reduce.6 = f32[64,4096]{1,0:T(8,128)} reduce(f32[64,1,4096]{2,1,0:T(1,128)S(1)} %all_to_all.21, f32[]{:T(128)} %broadcast.136), dimensions={1}, to_apply=%all_to_all.15.reduce_sub_computation | reduce | bytes 2097156 | tf_op jit(solution)/shard_map/all_to_all | solution.py:28
  231.8 2.0 reshape.286
  (60 shorter events, 19.4 us)
Async XLA Ops:
  0.0 1.6 copy-start
  2.8 15.6 %copy-start.5 = (s32[1,64]{1,0:T(1,128)S(1)}, s32[1,64]{1,0:T(1,128)}, u32[]{:S(2)}) copy-start(s32[1,64]{1,0:T(1,128)} %param.15) | copy-start | bytes 772
  5.2 47.5 %all-to-all-start = ((f32[64,1,5248]{2,1,0:T(1,128)}), f32[64,1,5248]{2,1,0:T(1,128)S(1)}, u32[]{:S(2)}, u32[]{:S(2)}) async-start(f32[64,1,5248]{2,1,0:T(1,128)} %copy.35), calls=%async_computation | async-start | bytes 2686976 | tf_op jit(solution)/shard_map/all_to_all | solution.py:28
  61.3 9.3 %copy-start.1 = (bf16[1,1024,512]{2,1,0:T(8,128)(2,1)S(1)}, bf16[1,1024,512]{2,1,0:T(8,128)(2,1)}, u32[]{:S(2)}) copy-start(bf16[1,1024,512]{2,1,0:T(8,128)(2,1)} %param.14) | copy-start | bytes 3145732
  61.3 24.2 %all-to-all-start.1 = ((bf16[64,2,2048]{2,1,0:T(2,128)(2,1)}), bf16[64,2,2048]{2,1,0:T(2,128)(2,1)S(1)}, u32[]{:S(2)}, u32[]{:S(2)}) async-start(bf16[64,2,2048]{2,1,0:T(2,128)(2,1)} %reshape.283), calls=%async_computation.1 | async-start | bytes 1048576 | tf_op jit(solution)/shard_map/all_to_all | solution.py:28
  96.6 4.8 %copy-start.2 = (bf16[1024,4,128]{2,1,0:T(4,128)(2,1)S(1)}, bf16[1024,4,128]{2,1,0:T(4,128)(2,1)}, u32[]{:S(2)}) copy-start(bf16[1024,4,128]{2,1,0:T(4,128)(2,1)} %reshape_squeeze.7) | copy-start | bytes 3145732
  180.2 3.1 %copy-start.3 = (bf16[64,4096]{1,0:T(8,128)(2,1)S(1)}, bf16[64,4096]{1,0:T(8,128)(2,1)}, u32[]{:S(2)}) copy-start(bf16[64,4096]{1,0:T(8,128)(2,1)} %param.12) | copy-start | bytes 1572868
  231.8 2.2 copy-start.4

commit v2 on v1

--- a/solution.py
+++ b/solution.py
@@ -117,20 +117,23 @@
     owner_top = jnp.repeat(jnp.swapaxes(local_top.reshape(all_rows, HEADS), 0, 1), per_head, 0)
     owner_totals = jnp.repeat(jnp.swapaxes(totals.reshape(all_rows, HEADS), 0, 1), per_head, 0)
     packed = jnp.concatenate(
-        [owner_mixed, owner_top[..., None], owner_totals[..., None]], axis=2
+        [owner_mixed.reshape(tp_count, all_rows * columns), owner_top, owner_totals], axis=1
     )
     got = spread(packed)
-    source_top = got[:, :, columns]
+    flat = all_rows * columns
+    source_top = got[:, flat : flat + all_rows]
     top = jnp.max(source_top, axis=0)
     rescale = jnp.exp(source_top - top[None])
-    total = jnp.sum(rescale * got[:, :, columns + 1], axis=0)
-    mixed_cols = jnp.sum(rescale[..., None] * got[:, :, :columns], axis=0)
+    total = jnp.sum(rescale * got[:, flat + all_rows :], axis=0)
+    source_mixed = got[:, :flat].reshape(tp_count, all_rows, columns)
+    mixed_cols = jnp.sum(rescale[..., None] * source_mixed, axis=0)
     attended = (mixed_cols / total[:, None]).astype(jnp.bfloat16)
 
     partial_terms = jnp.dot(attended, w_out, preferred_element_type=jnp.float32)
     out_cols = model_width // tp_count
-    terms = spread(jnp.swapaxes(partial_terms.reshape(all_rows, tp_count, out_cols), 0, 1))
-    projected = jnp.sum(terms, axis=0)
+    owner_terms = jnp.swapaxes(partial_terms.reshape(all_rows, tp_count, out_cols), 0, 1)
+    terms = spread(owner_terms.reshape(tp_count, all_rows * out_cols))
+    projected = jnp.sum(terms, axis=0).reshape(all_rows, out_cols)
     return (inputs + projected).astype(jnp.bfloat16)
 
 

time: 235 us -> 197 us (0.84)
  blocking collectives: 90.1 us -> 34.5 us
  waiting for transfers between devices: 46.6 us -> 73 us
  other arithmetic: 26.9 us -> 17.6 us
  local copies, waits for them, and re-layouts: 33.7 us -> 27.5 us
  starting transfers between devices: 19.6 us -> 25.2 us
    all_to_all x2 -> x1, blocking collectives: 90.1 us -> 34.5 us  [spread(): return lax.all_to_all(pieces, 'tp', 0, 0, tiled=True)]
    all_to_all x2 -> x3, waiting for transfers between devices: 46.6 us -> 73 us  [spread(): return lax.all_to_all(pieces, 'tp', 0, 0, tiled=True)]
    unnamed x19 -> x16, local copies, waits for them, and re-layouts: 11.1 us -> 2.73 us
    another operation x2 -> x0, local copies, waits for them, and re-layouts: 5.79 us -> none  [the longest x1 2.92 us: on_device(): owner_totals[..., None]]
    all_to_all x2 -> x3, starting transfers between devices: 19.6 us -> 25.2 us  [spread(): return lax.all_to_all(pieces, 'tp', 0, 0, tiled=True)]
    all_to_all x2 -> x1, other arithmetic: 7.6 us -> 3.15 us  [spread(): return lax.all_to_all(pieces, 'tp', 0, 0, tiled=True)]
    all_to_all x1 -> x2, local copies, waits for them, and re-layouts: 0.51 us -> 4.4 us  [spread(): return lax.all_to_all(pieces, 'tp', 0, 0, tiled=True)]
    concatenate x1 -> x0, other arithmetic: 3.37 us -> none  [on_device(): jnp.concatenate([owner_mixed, owner_top[..., None], owner_totals[..., Non...]
  transfers between devices with their start and end apart: 2 -> 3, of which waited for: 2 -> 3; matrix products, arithmetic and copies ran while one was open for 2% -> 3% of each run, Pallas kernels for 0% -> 0%
where the time goes in v2:
time: 197 us
  waiting for transfers between devices  73 us (37%)
  blocking collectives  34.5 us (18%)
  local copies, waits for them, and re-layouts  27.5 us (14%)
  starting transfers between devices  25.2 us (13%)
  other arithmetic  17.6 us (9%)
  matrix products  16.4 us (8%)
  between operations  2.33 us (1%)
    all_to_all x3, waiting for transfers between devices, spread(): return lax.all_to_all(pieces, 'tp', 0, 0, tiled=True)  73 us
    all_to_all x1, blocking collectives, spread(): return lax.all_to_all(pieces, 'tp', 0, 0, tiled=True)  34.5 us
    all_to_all x3, starting transfers between devices, spread(): return lax.all_to_all(pieces, 'tp', 0, 0, tiled=True)  25.2 us
    reduce_sum x1, other arithmetic, on_device(): totals = jnp.sum(cache_exp, axis=-1) + jnp.sum(tree_exp, axis=-1)  4.71 us
    dot_general x1, matrix products, on_device(): jnp.einsum('tkgd,pkd->tkgp', query_heads, cache_keys[0].reshape(places_de...  4.7 us
    dot_general x1, matrix products, on_device(): jnp.einsum('tkgp,pkd->tkgd', cache_exp.astype(jnp.bfloat16), cache_values...  4.64 us
    all_to_all x2, local copies, waits for them, and re-layouts, spread(): return lax.all_to_all(pieces, 'tp', 0, 0, tiled=True)  4.4 us
  transfers between devices with their start and end apart: 3, of which 3 were waited for; matrix products, arithmetic and copies ran while one was open for 3% of the time, Pallas kernels for 0%

profile of v2, /device:TPU:1, one launch (start us, length us, event | category | flops | bytes accessed | tf_op | source)
XLA Modules:
  0.0 196.5 jit_solution(15402171979142976559)
XLA Ops:
  2.8 2.5 %copy.33 = f32[64,1,5248]{2,1,0:T(1,128)} copy(f32[64,1,5248]{2,0,1:T(8,128)S(1)} %maximum_bitcast_fusion) | data formatting | bytes 2686976 | tf_op jit(solution)/shard_map/reshape | solution.py:52
  5.2 13.1 %all-to-all-start = ((f32[64,1,5248]{2,1,0:T(1,128)}), f32[64,1,5248]{2,1,0:T(1,128)S(1)}, u32[]{:S(2)}, u32[]{:S(2)}) async-start(f32[64,1,5248]{2,1,0:T(1,128)} %copy.33), calls=%async_computation | async-start | bytes 2686976 | tf_op jit(solution)/shard_map/all_to_all | solution.py:28
  19.2 33.5 %all-to-all-done = f32[64,1,5248]{2,1,0:T(1,128)S(1)} async-done(((f32[64,1,5248]{2,1,0:T(1,128)}), f32[64,1,5248]{2,1,0:T(1,128)S(1)}, u32[]{:S(2)}, u32[]{:S(2)}) %all-to-all-start) | async-done | bytes 1343520 | tf_op jit(solution)/shard_map/all_to_all | solution.py:28
  56.3 3.8 %reduce.6 = bf16[64,4096]{1,0:T(8,128)(2,1)S(1)} reduce(bf16[64,1,4096]{2,1,0:T(2,128)(2,1)S(1)} %broadcast_in_dim.83, bf16[]{:T(256)} %broadcast.138), dimensions={1}, to_apply=%broadcast_in_dim.83.reduce_sub_computation | reduce | bytes 1048578 | tf_op jit(solution)/shard_map/broadcast_in_dim | solution.py:60
  61.3 6.3 %all-to-all-start.1 = ((bf16[64,2,2048]{2,1,0:T(2,128)(2,1)}), bf16[64,2,2048]{2,1,0:T(2,128)(2,1)S(1)}, u32[]{:S(2)}, u32[]{:S(2)}) async-start(bf16[64,2,2048]{2,1,0:T(2,128)(2,1)} %reshape.312), calls=%async_computation.1 | async-start | bytes 1048576 | tf_op jit(solution)/shard_map/all_to_all | solution.py:28
  70.5 2.2 %reshape_squeeze.7 = bf16[1024,4,128]{2,1,0:T(4,128)(2,1)} reshape(bf16[1,1024,512]{2,1,0:T(8,128)(2,1)} %param.14) | data formatting | bytes 2097152 | tf_op jit(solution)/shard_map/reshape;squeeze | solution.py:105
  73.2 12.1 %all-to-all-done.1 = bf16[64,2,2048]{2,1,0:T(2,128)(2,1)S(1)} async-done(((bf16[64,2,2048]{2,1,0:T(2,128)(2,1)}), bf16[64,2,2048]{2,1,0:T(2,128)(2,1)S(1)}, u32[]{:S(2)}, u32[]{:S(2)}) %all-to-all-start.1) | async-done | bytes 524320 | tf_op jit(solution)/shard_map/all_to_all | solution.py:28
  85.8 3.1 %reduce.4 = bf16[64,4096]{1,0:T(8,128)(2,1)S(1)} reduce(bf16[64,1,4096]{2,1,0:T(2,128)(2,1)S(1)} %reshape.313, bf16[]{:T(256)} %constant.50), dimensions={1}, to_apply=%all_to_all.21.reduce_sub_computation | reduce | bytes 1048578 | tf_op jit(solution)/shard_map/all_to_all | solution.py:28
  89.1 2.4 %fusion.20 = f32[4,1,64,8]{3,1,2,0:T(1,128)S(1)} fusion(bf16[64,4,8,128]{3,2,1,0:T(8,128)(2,1)S(1)} %bitcast.123, bf16[1,5120]{1,0:T(2,128)(2,1)S(1)} %fusion.31), kind=kOutput, calls=%fused_computation.30 | convolution fusion | flops 524288 | bytes 534528 | tf_op jit(solution)/shard_map/tkgd,ukd->tkgu/dot_general | solution.py:90
  91.5 4.7 %bitcast_reduce_fusion = (f32[64,4,8]{2,0,1:T(8,128)S(1)}, f32[4,64,8,1024]{3,2,1,0:T(8,128)}) fusion(pred[1024]{0:T(1024)(128)(4,1)S(1)} %add_compare_fusion, bf16[1024,4,128,1]{2,1,0,3:T(4,128)(2,1)S(1)} %bitcast.122, bf16[64,4,8,128]{3,2,1,0:T(8,128)(2,1)S(1)} %bitcast.124), kind=kOutput, calls=%fused_computation.1 | convolution fusion | flops 543160320 | bytes 9970688 | tf_op jit(solution)/shard_map/tkgd,pkd->tkgp/dot_general | solution.py:80
  96.5 4.7 %fusion.2 = f32[64,4,8]{2,0,1:T(8,128)S(1)} fusion(f32[4,64,8,1024]{3,2,1,0:T(8,128)} %get-tuple-element.11, f32[64,4,8]{2,0,1:T(8,128)S(1)} %fusion.24, pred[1024]{0:T(1024)(128)(4,1)S(1)} %add_compare_fusion), kind=kLoop, calls=%fused_computation.5 | loop fusion | flops 10483712 | bytes 8406016 | tf_op jit(solution)/shard_map/reduce_sum | solution.py:101
  101.4 4.6 %fusion.11 = f32[64,4,8,128]{3,2,0,1:T(8,128)S(1)} fusion(f32[4,64,8,1024]{3,2,1,0:T(8,128)} %get-tuple-element.11, f32[64,4,8]{2,0,1:T(8,128)S(1)} %fusion.24, pred[1024]{0:T(1024)(128)(4,1)S(1)} %add_compare_fusion, bf16[1024,4,128,1]{2,1,0,3:T(4,128)(2,1)S(1)} %bitcast.131, f32[4,64,8]{2,1,0:T(8,128)S(1)} %get-tuple-element.7, f32[4,128]{1,0:T(4,128)S(1)} %bitcast.137), kind=kOutput, calls=%fused_computation.13 | convolution fusion | flops 547880960 | bytes 10505216 | tf_op jit(solution)/shard_map/tkgp,pkd->tkgd/dot_general | solution.py:102
  107.2 1.6 reshape.294
  108.7 2.6 %copy.38 = f32[64,64,64]{2,1,0:T(8,128)} copy(f32[64,64,64]{2,0,1:T(8,128)S(1)} %bitcast.121) | data formatting | bytes 2097152 | tf_op jit(solution)/shard_map/transpose | solution.py:116
  111.3 2.2 %reshape.295 = f32[64,4096]{1,0:T(8,128)S(1)} reshape(f32[64,64,64]{2,1,0:T(8,128)} %copy.38) | data formatting | bytes 2097152 | tf_op jit(solution)/shard_map/reshape | solution.py:120
  114.0 2.1 %copy.43 = f32[64,1,4224]{2,1,0:T(1,128)} copy(f32[64,1,4224]{2,0,1:T(8,128)S(1)} %bitcast.128) | data formatting | bytes 2162688 | tf_op jit(solution)/shard_map/all_to_all | solution.py:28
  116.1 5.7 %all-to-all-start.2 = ((f32[64,1,4224]{2,1,0:T(1,128)}), f32[64,1,4224]{2,1,0:T(1,128)S(1)}, u32[]{:S(2)}, u32[]{:S(2)}) async-start(f32[64,1,4224]{2,1,0:T(1,128)} %copy.43), calls=%async_computation.2 | async-start | bytes 2162688 | tf_op jit(solution)/shard_map/all_to_all | solution.py:28
  121.8 1.4 copy.54
  123.2 27.4 %all-to-all-done.2 = f32[64,1,4224]{2,1,0:T(1,128)S(1)} async-done(((f32[64,1,4224]{2,1,0:T(1,128)}), f32[64,1,4224]{2,1,0:T(1,128)S(1)}, u32[]{:S(2)}, u32[]{:S(2)}) %all-to-all-start.2) | async-done | bytes 1081376 | tf_op jit(solution)/shard_map/all_to_all | solution.py:28
  152.3 1.6 mul.68
  154.0 1.7 fusion.16
  155.9 2.3 %convolution_bitcast_fusion = f32[64,64,64]{2,1,0:T(8,128)S(1)} fusion(bf16[64,64,1]{1,0,2:T(8,128)(2,1)S(1)} %reshape.307, bf16[64,64,64]{2,1,0:T(8,128)(2,1)} %bitcast.129), kind=kOutput, calls=%fused_computation.10 | convolution fusion | flops 33554432 | bytes 1581056 | tf_op jit(solution)/shard_map/dot_general | solution.py:132
  158.2 2.3 %all_to_all.27 = f32[64,1,4096]{2,1,0:T(1,128)} reshape(f32[64,64,64]{2,1,0:T(8,128)S(1)} %convolution_bitcast_fusion) | data formatting | bytes 2097152 | tf_op jit(solution)/shard_map/all_to_all | solution.py:28
  160.5 34.5 %all_to_all.32 = f32[64,1,4096]{2,1,0:T(1,128)S(1)} all-to-all(f32[64,1,4096]{2,1,0:T(1,128)} %all_to_all.27), channel_id=1, replica_groups=mesh['req'=4,'tp'=64] {'tp'}, dimensions={0} | all-to-all | bytes 2097152 | tf_op jit(solution)/shard_map/all_to_all | solution.py:28
  (62 shorter events, 15.7 us)
Async XLA Ops:
  0.0 1.6 copy-start
  2.6 15.8 %copy-start.5 = (s32[1,64]{1,0:T(1,128)S(1)}, s32[1,64]{1,0:T(1,128)}, u32[]{:S(2)}) copy-start(s32[1,64]{1,0:T(1,128)} %param.15) | copy-start | bytes 772
  5.2 47.5 %all-to-all-start = ((f32[64,1,5248]{2,1,0:T(1,128)}), f32[64,1,5248]{2,1,0:T(1,128)S(1)}, u32[]{:S(2)}, u32[]{:S(2)}) async-start(f32[64,1,5248]{2,1,0:T(1,128)} %copy.33), calls=%async_computation | async-start | bytes 2686976 | tf_op jit(solution)/shard_map/all_to_all | solution.py:28
  61.3 24.0 %all-to-all-start.1 = ((bf16[64,2,2048]{2,1,0:T(2,128)(2,1)}), bf16[64,2,2048]{2,1,0:T(2,128)(2,1)S(1)}, u32[]{:S(2)}, u32[]{:S(2)}) async-start(bf16[64,2,2048]{2,1,0:T(2,128)(2,1)} %reshape.312), calls=%async_computation.1 | async-start | bytes 1048576 | tf_op jit(solution)/shard_map/all_to_all | solution.py:28
  96.5 4.9 %copy-start.2 = (bf16[1024,4,128]{2,1,0:T(4,128)(2,1)S(1)}, bf16[1024,4,128]{2,1,0:T(4,128)(2,1)}, u32[]{:S(2)}) copy-start(bf16[1024,4,128]{2,1,0:T(4,128)(2,1)} %reshape_squeeze.7) | copy-start | bytes 3145732
  111.3 10.5 %copy-start.3 = (bf16[64,4096]{1,0:T(8,128)(2,1)S(1)}, bf16[64,4096]{1,0:T(8,128)(2,1)}, u32[]{:S(2)}) copy-start(bf16[64,4096]{1,0:T(8,128)(2,1)} %param.12) | copy-start | bytes 1572868
  116.1 34.5 %all-to-all-start.2 = ((f32[64,1,4224]{2,1,0:T(1,128)}), f32[64,1,4224]{2,1,0:T(1,128)S(1)}, u32[]{:S(2)}, u32[]{:S(2)}) async-start(f32[64,1,4224]{2,1,0:T(1,128)} %copy.43), calls=%async_computation.2 | async-start | bytes 2162688 | tf_op jit(solution)/shard_map/all_to_all | solution.py:28
  150.7 1.0 copy-start.1
  155.9 40.1 %copy-start.4 = (bf16[64,64]{1,0:T(8,128)(2,1)S(1)}, bf16[64,64]{1,0:T(8,128)(2,1)}, u32[]{:S(2)}) copy-start(bf16[64,64]{1,0:T(8,128)(2,1)} %param.9) | copy-start | bytes 24580

commit v3 on v2

--- a/solution.py
+++ b/solution.py
@@ -1,6 +1,8 @@
 import jax
 import jax.numpy as jnp
 from jax import lax
+from jax.experimental import pallas as pl
+from jax.experimental.pallas import tpu as pltpu
 from jax.sharding import PartitionSpec as P
 
 HEADS = 32
@@ -22,6 +24,70 @@
             jnp.einsum("rij,rjk->rik", reached, reached, precision=lax.Precision.HIGHEST), 1.0
         )
     return reached
+
+
+def attention_kernel(limit_ref, q_ref, k_ref, v_ref, ts_ref, tv_ref, o_ref, m_ref, l_ref):
+    rows, places = q_ref.shape[1], k_ref.shape[0]
+    scale = HEAD ** (-0.5)
+    scores = (
+        lax.dot_general(
+            q_ref[0], k_ref[...], (((1,), (1,)), ((), ())), preferred_element_type=jnp.float32
+        )
+        * scale
+    )
+    valid = lax.broadcasted_iota(jnp.int32, (rows, places), 1) < limit_ref[0]
+    scores = jnp.where(valid, scores, NEGATIVE)
+    tree_score = ts_ref[0]
+    top = jnp.maximum(jnp.max(scores, axis=1, keepdims=True), tree_score)
+    shift = jnp.where(top > 0.5 * NEGATIVE, top, 0.0)
+    weights = jnp.exp(scores - shift)
+    tree_weight = jnp.exp(tree_score - shift)
+    m_ref[0] = top
+    l_ref[0] = jnp.sum(weights, axis=1, keepdims=True) + tree_weight
+    o_ref[0] = jnp.dot(
+        weights.astype(jnp.bfloat16), v_ref[...], preferred_element_type=jnp.float32
+    ) + tree_weight.astype(jnp.bfloat16).astype(jnp.float32) * tv_ref[0].astype(jnp.float32)
+
+
+def local_attention(limit, query, keys, values, tree_scores, own_values):
+    rows = query.shape[1]
+    places = keys.shape[0]
+    return pl.pallas_call(
+        attention_kernel,
+        grid_spec=pltpu.PrefetchScalarGridSpec(
+            num_scalar_prefetch=1,
+            grid=(KV_HEADS,),
+            in_specs=[
+                pl.BlockSpec((1, rows, HEAD), lambda k, lim: (k, 0, 0)),
+                pl.BlockSpec((places, HEAD), lambda k, lim: (0, k)),
+                pl.BlockSpec((places, HEAD), lambda k, lim: (0, k)),
+                pl.BlockSpec((1, rows, 1), lambda k, lim: (k, 0, 0)),
+                pl.BlockSpec((1, 1, HEAD), lambda k, lim: (k, 0, 0)),
+            ],
+            out_specs=[
+                pl.BlockSpec((1, rows, HEAD), lambda k, lim: (k, 0, 0)),
+                pl.BlockSpec((1, rows, 1), lambda k, lim: (k, 0, 0)),
+                pl.BlockSpec((1, rows, 1), lambda k, lim: (k, 0, 0)),
+            ],
+        ),
+        out_shape=[
+            jax.ShapeDtypeStruct((KV_HEADS, rows, HEAD), jnp.float32),
+            jax.ShapeDtypeStruct((KV_HEADS, rows, 1), jnp.float32),
+            jax.ShapeDtypeStruct((KV_HEADS, rows, 1), jnp.float32),
+        ],
+    )(limit, query, keys, values, tree_scores, own_values)
+
+
+def split3(values):
+    high = lax.reduce_precision(values, exponent_bits=8, mantissa_bits=7)
+    rest = values - high
+    middle = lax.reduce_precision(rest, exponent_bits=8, mantissa_bits=7)
+    low = rest - middle
+    return [high.astype(jnp.bfloat16), middle.astype(jnp.bfloat16), low.astype(jnp.bfloat16)]
+
+
+def join3(high, middle, low):
+    return high.astype(jnp.float32) + middle.astype(jnp.float32) + low.astype(jnp.float32)
 
 
 def spread(pieces):
@@ -56,8 +122,9 @@
         own_sum[:, :proj_width] * lax.rsqrt(square_sum / model_width + 1e-05)[:, None]
     ).astype(jnp.bfloat16)
     own_queries = own_qkv[:, :model_width]
+    lanes = own_count * model_width // 128
     query = spread(
-        jnp.broadcast_to(own_queries[None], (tp_count, own_count, model_width))
+        jnp.broadcast_to(own_queries.reshape(1, lanes, 128), (tp_count, lanes, 128))
     ).reshape(all_rows, model_width)
     own_tokens = own_qkv[:, model_width:]
     own_keys = own_tokens[:, :kv_width].reshape(own_count, KV_HEADS, HEAD)
@@ -74,66 +141,57 @@
     tree_mask = on_path & (key_place < draft_counts[0])[None, :]
 
     query_heads = query.reshape(all_rows, KV_HEADS, groups, HEAD)
-    positions = tp_rank * places_dev + jnp.arange(places_dev, dtype=jnp.int32)
-    valid = positions < cache_lengths[0]
-    cache_scores = (
-        jnp.einsum(
-            "tkgd,pkd->tkgp",
-            query_heads,
-            cache_keys[0].reshape(places_dev, KV_HEADS, HEAD),
-            preferred_element_type=jnp.float32,
-        )
-        * scale
-    )
-    cache_scores = jnp.where(valid[None, None, None, :], cache_scores, NEGATIVE)
     tree_scores = (
         jnp.einsum("tkgd,ukd->tkgu", query_heads, own_keys, preferred_element_type=jnp.float32)
         * scale
     )
     tree_scores = jnp.where(tree_mask[:, None, None, :], tree_scores, NEGATIVE)
-    local_top = jnp.maximum(jnp.max(cache_scores, axis=-1), jnp.max(tree_scores, axis=-1))
-    cache_exp = jnp.where(
-        valid[None, None, None, :], jnp.exp(cache_scores - local_top[..., None]), 0.0
-    )
-    tree_exp = jnp.where(
-        tree_mask[:, None, None, :], jnp.exp(tree_scores - local_top[..., None]), 0.0
-    )
-    totals = jnp.sum(cache_exp, axis=-1) + jnp.sum(tree_exp, axis=-1)
-    mixed = jnp.einsum(
-        "tkgp,pkd->tkgd",
-        cache_exp.astype(jnp.bfloat16),
-        cache_values[0].reshape(places_dev, KV_HEADS, HEAD),
-        preferred_element_type=jnp.float32,
-    ) + jnp.einsum(
-        "tkgu,ukd->tkgd",
-        tree_exp.astype(jnp.bfloat16),
-        own_values,
-        preferred_element_type=jnp.float32,
-    )
+    limit = (cache_lengths[:1] - tp_rank * places_dev).astype(jnp.int32)
+    head_rows = jnp.transpose(query_heads, (1, 2, 0, 3)).reshape(KV_HEADS, groups * all_rows, HEAD)
+    head_mixed, top_parts, total_parts = local_attention(
+        limit,
+        head_rows,
+        cache_keys[0],
+        cache_values[0],
+        jnp.transpose(tree_scores[..., 0], (1, 2, 0)).reshape(KV_HEADS, groups * all_rows, 1),
+        own_values[0].reshape(KV_HEADS, 1, HEAD),
+    )
+    local_top = top_parts.reshape(HEADS, all_rows)
+    totals = total_parts.reshape(HEADS, all_rows)
 
     columns = w_out.shape[0]
     per_head = HEAD // columns
-    owner_mixed = jnp.swapaxes(mixed.reshape(all_rows, tp_count, columns), 0, 1)
-    owner_top = jnp.repeat(jnp.swapaxes(local_top.reshape(all_rows, HEADS), 0, 1), per_head, 0)
-    owner_totals = jnp.repeat(jnp.swapaxes(totals.reshape(all_rows, HEADS), 0, 1), per_head, 0)
+    halves = HEAD // columns
+    owner_mixed = jnp.swapaxes(
+        head_mixed.reshape(HEADS, all_rows, halves, columns), 1, 2
+    ).reshape(tp_count, all_rows * columns)
+    owner_top = jnp.repeat(local_top, per_head, 0)
+    owner_totals = jnp.repeat(totals, per_head, 0)
     packed = jnp.concatenate(
-        [owner_mixed.reshape(tp_count, all_rows * columns), owner_top, owner_totals], axis=1
-    )
-    got = spread(packed)
+        [owner_mixed.astype(jnp.bfloat16)]
+        + split3(owner_top)
+        + split3(owner_totals)
+        + [jnp.zeros((tp_count, 128 - (6 * all_rows) % 128), jnp.bfloat16)],
+        axis=1,
+    )
+    got = spread(packed.reshape(tp_count, -1, 128)).reshape(tp_count, -1)
     flat = all_rows * columns
-    source_top = got[:, flat : flat + all_rows]
+    piece = [got[:, flat + i * all_rows : flat + (i + 1) * all_rows] for i in range(6)]
+    source_top = join3(*piece[:3])
     top = jnp.max(source_top, axis=0)
     rescale = jnp.exp(source_top - top[None])
-    total = jnp.sum(rescale * got[:, flat + all_rows :], axis=0)
-    source_mixed = got[:, :flat].reshape(tp_count, all_rows, columns)
+    total = jnp.sum(rescale * join3(*piece[3:]), axis=0)
+    source_mixed = got[:, :flat].reshape(tp_count, all_rows, columns).astype(jnp.float32)
     mixed_cols = jnp.sum(rescale[..., None] * source_mixed, axis=0)
     attended = (mixed_cols / total[:, None]).astype(jnp.bfloat16)
 
     partial_terms = jnp.dot(attended, w_out, preferred_element_type=jnp.float32)
     out_cols = model_width // tp_count
     owner_terms = jnp.swapaxes(partial_terms.reshape(all_rows, tp_count, out_cols), 0, 1)
-    terms = spread(owner_terms.reshape(tp_count, all_rows * out_cols))
-    projected = jnp.sum(terms, axis=0).reshape(all_rows, out_cols)
+    terms = spread(
+        owner_terms.reshape(tp_count, all_rows * out_cols // 128, 128).astype(jnp.bfloat16)
+    )
+    projected = jnp.sum(terms.astype(jnp.float32), axis=0).reshape(all_rows, out_cols)
     return (inputs + projected).astype(jnp.bfloat16)
 
 

time: 197 us -> 157 us (0.80)
  local copies, waits for them, and re-layouts: 27.5 us -> 15.3 us
  blocking collectives: 34.5 us -> 23.3 us
  matrix products: 16.4 us -> 5.81 us
  other arithmetic: 17.6 us -> 8.28 us
  Pallas kernels: 0 us -> 8.67 us
  waiting for transfers between devices: 73 us -> 67.6 us
    all_to_all x1, blocking collectives: 34.5 us -> 23.3 us  [spread(): return lax.all_to_all(pieces, 'tp', 0, 0, tiled=True)]
    dot_general x2 -> x0, matrix products: 9.34 us -> none  [the longest x1 4.7 us: on_device(): jnp.einsum('tkgd,pkd->tkgp', query_heads, cache_keys[0].reshape(places_de...]
    pallas_call x0 -> x1, Pallas kernels: none -> 8.67 us  [local_attention(): pl.pallas_call(attention_kernel, grid_spec=pltpu.PrefetchScalarGridSpec(n...]
    reduce_sum x3 -> x2, other arithmetic: 5.67 us -> 0.21 us  [the longest x1 0.11 us: on_device(): total = jnp.sum(rescale * join3(*piece[3:]), axis=0)]
    all_to_all x3, waiting for transfers between devices: 73 us -> 67.6 us  [spread(): return lax.all_to_all(pieces, 'tp', 0, 0, tiled=True)]
    all_to_all x2 -> x0, local copies, waits for them, and re-layouts: 4.4 us -> none  [spread(): return lax.all_to_all(pieces, 'tp', 0, 0, tiled=True)]
    broadcast_in_dim x1 -> x0, other arithmetic: 3.79 us -> none  [on_device(): jnp.broadcast_to(own_queries[None], (tp_count, own_count, model_width))]
    pallas_call x0 -> x2, other arithmetic: none -> 3.24 us  [local_attention(): pl.pallas_call(attention_kernel, grid_spec=pltpu.PrefetchScalarGridSpec(n...]
  transfers between devices with their start and end apart: 3 -> 3, of which waited for: 3 -> 3; matrix products, arithmetic and copies ran while one was open for 3% -> 2% of each run, Pallas kernels for 0% -> 0%
where the time goes in v3:
time: 157 us
  waiting for transfers between devices  67.6 us (43%)
  starting transfers between devices  25.3 us (16%)
  blocking collectives  23.3 us (15%)
  local copies, waits for them, and re-layouts  15.3 us (10%)
  Pallas kernels  8.67 us (6%)
  other arithmetic  8.28 us (5%)
  matrix products  5.81 us (4%)
  between operations  2.28 us (1%)
    all_to_all x3, waiting for transfers between devices, spread(): return lax.all_to_all(pieces, 'tp', 0, 0, tiled=True)  67.6 us
    all_to_all x3, starting transfers between devices, spread(): return lax.all_to_all(pieces, 'tp', 0, 0, tiled=True)  25.3 us
    all_to_all x1, blocking collectives, spread(): return lax.all_to_all(pieces, 'tp', 0, 0, tiled=True)  23.3 us
    pallas_call x1, Pallas kernels, local_attention(): pl.pallas_call(attention_kernel, grid_spec=pltpu.PrefetchScalarGridSpec(n...  8.67 us
    pallas_call x2, other arithmetic, local_attention(): pl.pallas_call(attention_kernel, grid_spec=pltpu.PrefetchScalarGridSpec(n...  3.24 us
  transfers between devices with their start and end apart: 3, of which 3 were waited for; matrix products, arithmetic and copies ran while one was open for 2% of the time, Pallas kernels for 0%

profile of v3, /device:TPU:1, one launch (start us, length us, event | category | flops | bytes accessed | tf_op | source)
XLA Modules:
  0.0 156.5 jit_solution(13493225326244860020)
XLA Ops:
  0.7 0.8 fusion.8
  1.6 1.0 fusion.14
  2.8 2.5 %copy.14 = f32[64,1,5248]{2,1,0:T(1,128)} copy(f32[64,1,5248]{2,0,1:T(8,128)S(1)} %maximum_bitcast_fusion) | data formatting | bytes 2686976 | tf_op jit(solution)/shard_map/reshape | solution.py:118
  5.2 13.3 %all-to-all-start = ((f32[64,1,5248]{2,1,0:T(1,128)}), f32[64,1,5248]{2,1,0:T(1,128)S(1)}, u32[]{:S(2)}, u32[]{:S(2)}) async-start(f32[64,1,5248]{2,1,0:T(1,128)} %copy.14), calls=%async_computation | async-start | bytes 2686976 | tf_op jit(solution)/shard_map/all_to_all | solution.py:94
  20.7 32.2 %all-to-all-done = f32[64,1,5248]{2,1,0:T(1,128)S(1)} async-done(((f32[64,1,5248]{2,1,0:T(1,128)}), f32[64,1,5248]{2,1,0:T(1,128)S(1)}, u32[]{:S(2)}, u32[]{:S(2)}) %all-to-all-start) | async-done | bytes 1343520 | tf_op jit(solution)/shard_map/all_to_all | solution.py:94
  52.8 0.8 reduce_sum.48
  54.9 0.9 broadcast_in_dim.22
  55.8 6.3 %all-to-all-start.1 = ((bf16[64,32,128]{2,1,0:T(8,128)(2,1)}), bf16[64,32,128]{2,1,0:T(8,128)(2,1)S(1)}, u32[]{:S(2)}, u32[]{:S(2)}) async-start(bf16[64,32,128]{2,1,0:T(8,128)(2,1)} %broadcast_in_dim.22), calls=%async_computation.1 | async-start | bytes 1048576 | tf_op jit(solution)/shard_map/all_to_all | solution.py:94
  63.4 16.4 %all-to-all-done.1 = bf16[64,32,128]{2,1,0:T(8,128)(2,1)S(1)} async-done(((bf16[64,32,128]{2,1,0:T(8,128)(2,1)}), bf16[64,32,128]{2,1,0:T(8,128)(2,1)S(1)}, u32[]{:S(2)}, u32[]{:S(2)}) %all-to-all-start.1) | async-done | bytes 524320 | tf_op jit(solution)/shard_map/all_to_all | solution.py:94
  79.8 2.4 %fusion.3 = f32[4,1,64,8]{3,1,2,0:T(1,128)S(1)} fusion(bf16[1,5120]{1,0:T(2,128)(2,1)S(1)} %fusion.13, bf16[64,32,128]{2,1,0:T(8,128)(2,1)S(1)} %all-to-all-done.1), kind=kOutput, calls=%fused_computation.17 | convolution fusion | flops 524288 | bytes 534528 | tf_op jit(solution)/shard_map/tkgd,ukd->tkgu/dot_general | solution.py:145
  82.3 2.0 %reshape.292.ts_ref = f32[4,512,1]{2,1,0:T(8,128)} reshape(f32[4,8,64]{2,1,0:T(8,128)S(1)} %fusion.16) | data formatting | bytes 16384 | tf_op jit(solution)/shard_map/reshape | solution.py:156
  84.3 1.0 copy.15
  85.3 8.7 %shard_map.94 = (f32[4,512,128]{2,1,0:T(8,128)}, f32[4,512,1]{2,1,0:T(8,128)}, f32[4,512,1]{2,1,0:T(8,128)}) custom-call(s32[1]{0:T(128)S(6)} %sub.27.limit_ref, bf16[4,512,128]{2,1,0:T(8,128)(2,1)} %bitcast.87, bf16[1024,512]{1,0:T(8,128)(2,1)} %bitcast.88, bf16[1024,512]{1,0:T(8,128)(2,1)} %bitcast.89, f32[4,512,1]{2,1,0:T(8,128)} %reshape.292.ts_ref, ...), custom_call_target="tpu_custom_call" | custom-call | tf_op jit(solution)/shard_map/pallas_call | solution.py:55
  94.0 1.7 %reduce.3 = f32[4,512]{1,0:T(4,128)S(1)} reduce(f32[4,512,1]{2,1,0:T(8,128)} %get-tuple-element.9, f32[]{:T(128)} %constant.52), dimensions={2}, to_apply=%get-tuple-element.9.reduce_sub_computation | reduce | bytes 16388 | tf_op jit(solution)/shard_map/pallas_call | solution.py:55
  95.7 1.6 %reduce.4 = f32[4,512]{1,0:T(4,128)S(1)} reduce(f32[4,512,1]{2,1,0:T(8,128)} %get-tuple-element.10, f32[]{:T(128)} %constant.52), dimensions={2}, to_apply=%get-tuple-element.10.reduce_sub_computation | reduce | bytes 16388 | tf_op jit(solution)/shard_map/pallas_call | solution.py:55
  98.1 0.8 convert_element_type.146
  99.3 1.2 reshape.283
  100.5 5.7 %all-to-all-start.2 = ((bf16[64,36,128]{2,1,0:T(8,128)(2,1)}), bf16[64,36,128]{2,1,0:T(8,128)(2,1)S(1)}, u32[]{:S(2)}, u32[]{:S(2)}) async-start(bf16[64,36,128]{2,1,0:T(8,128)(2,1)} %reshape.283), calls=%async_computation.2 | async-start | bytes 1310720 | tf_op jit(solution)/shard_map/all_to_all | solution.py:94
  106.2 1.3 copy.22
  107.6 19.0 %all-to-all-done.2 = bf16[64,36,128]{2,1,0:T(8,128)(2,1)S(1)} async-done(((bf16[64,36,128]{2,1,0:T(8,128)(2,1)}), bf16[64,36,128]{2,1,0:T(8,128)(2,1)S(1)}, u32[]{:S(2)}, u32[]{:S(2)}) %all-to-all-start.2) | async-done | bytes 589856 | tf_op jit(solution)/shard_map/all_to_all | solution.py:94
  127.4 1.7 %mul.59 = f32[64,4096]{1,0:T(8,128)} reshape(f32[64,64,64]{2,1,0:T(8,128)S(1)} %mul.58) | data formatting | bytes 2097152 | tf_op jit(solution)/shard_map/mul | solution.py:185
  129.1 1.4 multiply_reduce_fusion
  130.8 1.1 fusion
  132.5 23.3 %all_to_all.20 = bf16[64,32,128]{2,1,0:T(8,128)(2,1)S(1)} all-to-all(bf16[64,32,128]{2,1,0:T(8,128)(2,1)S(1)} %convert_element_type.164), channel_id=1, replica_groups=mesh['req'=4,'tp'=64] {'tp'}, dimensions={0} | all-to-all | bytes 1048576 | tf_op jit(solution)/shard_map/all_to_all | solution.py:94
  (53 shorter events, 7.2 us)
Async XLA Ops:
  0.0 1.6 copy-start
  5.2 14.6 %copy-start.5 = (s32[1,64]{1,0:T(1,128)S(1)}, s32[1,64]{1,0:T(1,128)}, u32[]{:S(2)}) copy-start(s32[1,64]{1,0:T(1,128)} %param.15) | copy-start | bytes 772
  5.2 47.6 %all-to-all-start = ((f32[64,1,5248]{2,1,0:T(1,128)}), f32[64,1,5248]{2,1,0:T(1,128)S(1)}, u32[]{:S(2)}, u32[]{:S(2)}) async-start(f32[64,1,5248]{2,1,0:T(1,128)} %copy.14), calls=%async_computation | async-start | bytes 2686976 | tf_op jit(solution)/shard_map/all_to_all | solution.py:94
  55.8 24.0 %all-to-all-start.1 = ((bf16[64,32,128]{2,1,0:T(8,128)(2,1)}), bf16[64,32,128]{2,1,0:T(8,128)(2,1)S(1)}, u32[]{:S(2)}, u32[]{:S(2)}) async-start(bf16[64,32,128]{2,1,0:T(8,128)(2,1)} %broadcast_in_dim.22), calls=%async_computation.1 | async-start | bytes 1048576 | tf_op jit(solution)/shard_map/all_to_all | solution.py:94
  94.0 3.4 %copy-start.2 = (f32[4,512,128]{2,1,0:T(8,128)S(1)}, f32[4,512,128]{2,1,0:T(8,128)}, u32[]{:S(2)}) copy-start(f32[4,512,128]{2,1,0:T(8,128)} %get-tuple-element.8) | copy-start | bytes 3145732
  99.3 6.9 %copy-start.3 = (bf16[64,4096]{1,0:T(8,128)(2,1)S(1)}, bf16[64,4096]{1,0:T(8,128)(2,1)}, u32[]{:S(2)}) copy-start(bf16[64,4096]{1,0:T(8,128)(2,1)} %param.12) | copy-start | bytes 1572868
  100.5 26.0 %all-to-all-start.2 = ((bf16[64,36,128]{2,1,0:T(8,128)(2,1)}), bf16[64,36,128]{2,1,0:T(8,128)(2,1)S(1)}, u32[]{:S(2)}, u32[]{:S(2)}) async-start(bf16[64,36,128]{2,1,0:T(8,128)(2,1)} %reshape.283), calls=%async_computation.2 | async-start | bytes 1310720 | tf_op jit(solution)/shard_map/all_to_all | solution.py:94
  129.1 1.7 %copy-start.1 = (bf16[4096,64]{1,0:T(8,128)(2,1)S(1)}, bf16[4096,64]{1,0:T(8,128)(2,1)}, u32[]{:S(2)}) copy-start(bf16[4096,64]{1,0:T(8,128)(2,1)} %copy.22) | copy-start | bytes 1572868
  132.0 24.0 %copy-start.4 = (bf16[64,64]{1,0:T(8,128)(2,1)S(1)}, bf16[64,64]{1,0:T(8,128)(2,1)}, u32[]{:S(2)}) copy-start(bf16[64,64]{1,0:T(8,128)(2,1)} %param.9) | copy-start | bytes 24580

commit v4 on v3

--- a/solution.py
+++ b/solution.py
@@ -26,30 +26,32 @@
     return reached
 
 
-def attention_kernel(limit_ref, q_ref, k_ref, v_ref, ts_ref, tv_ref, o_ref, m_ref, l_ref):
+def attention_kernel(limit_ref, q_ref, k_ref, v_ref, ts_ref, o_ref, m_ref, l_ref):
     rows, places = q_ref.shape[1], k_ref.shape[0]
     scale = HEAD ** (-0.5)
     scores = (
         lax.dot_general(
-            q_ref[0], k_ref[...], (((1,), (1,)), ((), ())), preferred_element_type=jnp.float32
+            k_ref[...], q_ref[0], (((1,), (1,)), ((), ())), preferred_element_type=jnp.float32
         )
         * scale
     )
-    valid = lax.broadcasted_iota(jnp.int32, (rows, places), 1) < limit_ref[0]
+    valid = lax.broadcasted_iota(jnp.int32, (places, rows), 0) < limit_ref[0]
     scores = jnp.where(valid, scores, NEGATIVE)
     tree_score = ts_ref[0]
-    top = jnp.maximum(jnp.max(scores, axis=1, keepdims=True), tree_score)
+    top = jnp.maximum(jnp.max(scores, axis=0, keepdims=True), tree_score)
     shift = jnp.where(top > 0.5 * NEGATIVE, top, 0.0)
     weights = jnp.exp(scores - shift)
-    tree_weight = jnp.exp(tree_score - shift)
     m_ref[0] = top
-    l_ref[0] = jnp.sum(weights, axis=1, keepdims=True) + tree_weight
-    o_ref[0] = jnp.dot(
-        weights.astype(jnp.bfloat16), v_ref[...], preferred_element_type=jnp.float32
-    ) + tree_weight.astype(jnp.bfloat16).astype(jnp.float32) * tv_ref[0].astype(jnp.float32)
-
-
-def local_attention(limit, query, keys, values, tree_scores, own_values):
+    l_ref[0] = jnp.sum(weights, axis=0, keepdims=True) + jnp.exp(tree_score - shift)
+    o_ref[0] = lax.dot_general(
+        weights.astype(jnp.bfloat16),
+        v_ref[...],
+        (((0,), (0,)), ((), ())),
+        preferred_element_type=jnp.float32,
+    )
+
+
+def local_attention(limit, query, keys, values, tree_scores):
     rows = query.shape[1]
     places = keys.shape[0]
     return pl.pallas_call(
@@ -61,21 +63,20 @@
                 pl.BlockSpec((1, rows, HEAD), lambda k, lim: (k, 0, 0)),
                 pl.BlockSpec((places, HEAD), lambda k, lim: (0, k)),
                 pl.BlockSpec((places, HEAD), lambda k, lim: (0, k)),
-                pl.BlockSpec((1, rows, 1), lambda k, lim: (k, 0, 0)),
-                pl.BlockSpec((1, 1, HEAD), lambda k, lim: (k, 0, 0)),
+                pl.BlockSpec((1, 1, rows), lambda k, lim: (k, 0, 0)),
             ],
             out_specs=[
                 pl.BlockSpec((1, rows, HEAD), lambda k, lim: (k, 0, 0)),
-                pl.BlockSpec((1, rows, 1), lambda k, lim: (k, 0, 0)),
-                pl.BlockSpec((1, rows, 1), lambda k, lim: (k, 0, 0)),
+                pl.BlockSpec((1, 1, rows), lambda k, lim: (k, 0, 0)),
+                pl.BlockSpec((1, 1, rows), lambda k, lim: (k, 0, 0)),
             ],
         ),
         out_shape=[
             jax.ShapeDtypeStruct((KV_HEADS, rows, HEAD), jnp.float32),
-            jax.ShapeDtypeStruct((KV_HEADS, rows, 1), jnp.float32),
-            jax.ShapeDtypeStruct((KV_HEADS, rows, 1), jnp.float32),
+            jax.ShapeDtypeStruct((KV_HEADS, 1, rows), jnp.float32),
+            jax.ShapeDtypeStruct((KV_HEADS, 1, rows), jnp.float32),
         ],
-    )(limit, query, keys, values, tree_scores, own_values)
+    )(limit, query, keys, values, tree_scores)
 
 
 def split3(values):
@@ -148,14 +149,15 @@
     tree_scores = jnp.where(tree_mask[:, None, None, :], tree_scores, NEGATIVE)
     limit = (cache_lengths[:1] - tp_rank * places_dev).astype(jnp.int32)
     head_rows = jnp.transpose(query_heads, (1, 2, 0, 3)).reshape(KV_HEADS, groups * all_rows, HEAD)
-    head_mixed, top_parts, total_parts = local_attention(
-        limit,
-        head_rows,
-        cache_keys[0],
-        cache_values[0],
-        jnp.transpose(tree_scores[..., 0], (1, 2, 0)).reshape(KV_HEADS, groups * all_rows, 1),
-        own_values[0].reshape(KV_HEADS, 1, HEAD),
-    )
+    head_tree = jnp.transpose(tree_scores[..., 0], (1, 2, 0)).reshape(KV_HEADS, 1, groups * all_rows)
+    cache_mixed, top_parts, total_parts = local_attention(
+        limit, head_rows, cache_keys[0], cache_values[0], head_tree
+    )
+    shift = jnp.where(top_parts > 0.5 * NEGATIVE, top_parts, 0.0)
+    tree_weight = lax.reduce_precision(jnp.exp(head_tree - shift), exponent_bits=8, mantissa_bits=7)
+    head_mixed = cache_mixed + jnp.swapaxes(tree_weight, 1, 2) * own_values[0].reshape(
+        KV_HEADS, 1, HEAD
+    ).astype(jnp.float32)
     local_top = top_parts.reshape(HEADS, all_rows)
     totals = total_parts.reshape(HEADS, all_rows)
 

time: 157 us -> 155 us (0.987)
  local copies, waits for them, and re-layouts: 15.3 us -> 13.4 us
    pallas_call x2, other arithmetic: 3.24 us -> 1.47 us  [local_attention(): pl.pallas_call(attention_kernel, grid_spec=pltpu.PrefetchScalarGridSpec(n...]
where the time goes in v4:
time: 155 us
  waiting for transfers between devices  68.2 us (44%)
  starting transfers between devices  25.3 us (16%)
  blocking collectives  23.3 us (15%)
  local copies, waits for them, and re-layouts  13.4 us (9%)
  Pallas kernels  8.29 us (5%)
  other arithmetic  8.01 us (5%)
  matrix products  5.81 us (4%)
  between operations  2.29 us (1%)
    all_to_all x3, waiting for transfers between devices, spread(): return lax.all_to_all(pieces, 'tp', 0, 0, tiled=True)  68.2 us
    all_to_all x3, starting transfers between devices, spread(): return lax.all_to_all(pieces, 'tp', 0, 0, tiled=True)  25.3 us
    all_to_all x1, blocking collectives, spread(): return lax.all_to_all(pieces, 'tp', 0, 0, tiled=True)  23.3 us
    pallas_call x1, Pallas kernels, local_attention(): pl.pallas_call(attention_kernel, grid_spec=pltpu.PrefetchScalarGridSpec(n...  8.29 us
  transfers between devices with their start and end apart: 3, of which 3 were waited for; matrix products, arithmetic and copies ran while one was open for 2% of the time, Pallas kernels for 0%

profile of v4, /device:TPU:1, one launch (start us, length us, event | category | flops | bytes accessed | tf_op | source)
XLA Modules:
  0.0 154.6 jit_solution(17770576274817384438)
XLA Ops:
  0.7 0.8 fusion.8
  1.6 1.0 fusion.14
  2.8 2.5 %copy.13 = f32[64,1,5248]{2,1,0:T(1,128)} copy(f32[64,1,5248]{2,0,1:T(8,128)S(1)} %maximum_bitcast_fusion) | data formatting | bytes 2686976 | tf_op jit(solution)/shard_map/reshape | solution.py:119
  5.2 13.3 %all-to-all-start = ((f32[64,1,5248]{2,1,0:T(1,128)}), f32[64,1,5248]{2,1,0:T(1,128)S(1)}, u32[]{:S(2)}, u32[]{:S(2)}) async-start(f32[64,1,5248]{2,1,0:T(1,128)} %copy.13), calls=%async_computation | async-start | bytes 2686976 | tf_op jit(solution)/shard_map/all_to_all | solution.py:95
  20.7 32.2 %all-to-all-done = f32[64,1,5248]{2,1,0:T(1,128)S(1)} async-done(((f32[64,1,5248]{2,1,0:T(1,128)}), f32[64,1,5248]{2,1,0:T(1,128)S(1)}, u32[]{:S(2)}, u32[]{:S(2)}) %all-to-all-start) | async-done | bytes 1343520 | tf_op jit(solution)/shard_map/all_to_all | solution.py:95
  52.8 0.8 reduce_sum.48
  54.9 0.9 broadcast_in_dim.30
  55.8 6.3 %all-to-all-start.1 = ((bf16[64,32,128]{2,1,0:T(8,128)(2,1)}), bf16[64,32,128]{2,1,0:T(8,128)(2,1)S(1)}, u32[]{:S(2)}, u32[]{:S(2)}) async-start(bf16[64,32,128]{2,1,0:T(8,128)(2,1)} %broadcast_in_dim.30), calls=%async_computation.1 | async-start | bytes 1048576 | tf_op jit(solution)/shard_map/all_to_all | solution.py:95
  62.8 17.0 %all-to-all-done.1 = bf16[64,32,128]{2,1,0:T(8,128)(2,1)S(1)} async-done(((bf16[64,32,128]{2,1,0:T(8,128)(2,1)}), bf16[64,32,128]{2,1,0:T(8,128)(2,1)S(1)}, u32[]{:S(2)}, u32[]{:S(2)}) %all-to-all-start.1) | async-done | bytes 524320 | tf_op jit(solution)/shard_map/all_to_all | solution.py:95
  79.8 2.4 %fusion.3 = f32[4,1,64,8]{3,1,2,0:T(1,128)S(1)} fusion(bf16[1,5120]{1,0:T(2,128)(2,1)S(1)} %fusion.13, bf16[64,32,128]{2,1,0:T(8,128)(2,1)S(1)} %all-to-all-done.1), kind=kOutput, calls=%fused_computation.18 | convolution fusion | flops 524288 | bytes 534528 | tf_op jit(solution)/shard_map/tkgd,ukd->tkgu/dot_general | solution.py:146
  83.0 1.0 copy.14
  84.0 8.3 %shard_map.94 = (f32[4,512,128]{2,1,0:T(8,128)}, f32[4,1,512]{2,1,0:T(1,128)}, f32[4,1,512]{2,1,0:T(1,128)}) custom-call(s32[1]{0:T(128)S(6)} %sub.30.limit_ref, bf16[4,512,128]{2,1,0:T(8,128)(2,1)} %bitcast.89, bf16[1024,512]{1,0:T(8,128)(2,1)} %bitcast.90, bf16[1024,512]{1,0:T(8,128)(2,1)} %bitcast.91, f32[4,1,512]{2,1,0:T(1,128)} %reshape.288.ts_ref), custom_call_target="tpu_custom_call" | custom-call | tf_op jit(solution)/shard_map/pallas_call | solution.py:57
  92.3 0.7 fusion.23
  93.1 0.7 reduce.4
  93.9 1.6 %add_convert_fusion = bf16[4,512,128]{2,1,0:T(8,128)(2,1)S(1)} fusion(f32[4,512,128]{2,1,0:T(8,128)} %get-tuple-element.8, f32[4,128]{1,0:T(4,128)S(1)} %bitcast.98, f32[4,512]{1,0:T(4,128)S(1)} %bitcast.97), kind=kLoop, calls=%fused_computation.16 | loop fusion | flops 786432 | bytes 1583104 | tf_op jit(solution)/shard_map/convert_element_type | solution.py:173
  96.2 0.8 convert_element_type.159
  97.4 1.2 reshape.293
  98.6 5.7 %all-to-all-start.2 = ((bf16[64,36,128]{2,1,0:T(8,128)(2,1)}), bf16[64,36,128]{2,1,0:T(8,128)(2,1)S(1)}, u32[]{:S(2)}, u32[]{:S(2)}) async-start(bf16[64,36,128]{2,1,0:T(8,128)(2,1)} %reshape.293), calls=%async_computation.2 | async-start | bytes 1310720 | tf_op jit(solution)/shard_map/all_to_all | solution.py:95
  104.3 1.3 copy.20
  105.6 19.0 %all-to-all-done.2 = bf16[64,36,128]{2,1,0:T(8,128)(2,1)S(1)} async-done(((bf16[64,36,128]{2,1,0:T(8,128)(2,1)}), bf16[64,36,128]{2,1,0:T(8,128)(2,1)S(1)}, u32[]{:S(2)}, u32[]{:S(2)}) %all-to-all-start.2) | async-done | bytes 589856 | tf_op jit(solution)/shard_map/all_to_all | solution.py:95
  125.5 1.7 %mul.78 = f32[64,4096]{1,0:T(8,128)} reshape(f32[64,64,64]{2,1,0:T(8,128)S(1)} %mul.77) | data formatting | bytes 2097152 | tf_op jit(solution)/shard_map/mul | solution.py:187
  127.2 1.4 multiply_reduce_fusion
  128.9 1.1 fusion
  130.5 23.3 %all_to_all.20 = bf16[64,32,128]{2,1,0:T(8,128)(2,1)S(1)} all-to-all(bf16[64,32,128]{2,1,0:T(8,128)(2,1)S(1)} %convert_element_type.177), channel_id=1, replica_groups=mesh['req'=4,'tp'=64] {'tp'}, dimensions={0} | all-to-all | bytes 1048576 | tf_op jit(solution)/shard_map/all_to_all | solution.py:95
  (54 shorter events, 7.2 us)
Async XLA Ops:
  0.0 1.6 %copy-start = (bf16[64,5120]{1,0:T(8,128)(2,1)S(1)}, bf16[64,5120]{1,0:T(8,128)(2,1)}, u32[]{:S(2)}) copy-start(bf16[64,5120]{1,0:T(8,128)(2,1)} %param.11) | copy-start | bytes 1966084
  5.2 14.6 %copy-start.5 = (s32[1,64]{1,0:T(1,128)S(1)}, s32[1,64]{1,0:T(1,128)}, u32[]{:S(2)}) copy-start(s32[1,64]{1,0:T(1,128)} %param.15) | copy-start | bytes 772
  5.2 47.6 %all-to-all-start = ((f32[64,1,5248]{2,1,0:T(1,128)}), f32[64,1,5248]{2,1,0:T(1,128)S(1)}, u32[]{:S(2)}, u32[]{:S(2)}) async-start(f32[64,1,5248]{2,1,0:T(1,128)} %copy.13), calls=%async_computation | async-start | bytes 2686976 | tf_op jit(solution)/shard_map/all_to_all | solution.py:95
  55.8 24.0 %all-to-all-start.1 = ((bf16[64,32,128]{2,1,0:T(8,128)(2,1)}), bf16[64,32,128]{2,1,0:T(8,128)(2,1)S(1)}, u32[]{:S(2)}, u32[]{:S(2)}) async-start(bf16[64,32,128]{2,1,0:T(8,128)(2,1)} %broadcast_in_dim.30), calls=%async_computation.1 | async-start | bytes 1048576 | tf_op jit(solution)/shard_map/all_to_all | solution.py:95
  84.0 8.3 %copy-start.4 = (f32[4,1,512]{2,1,0:T(1,128)S(1)}, f32[4,1,512]{2,1,0:T(1,128)}, u32[]{:S(2)}) copy-start(f32[4,1,512]{2,1,0:T(1,128)} %reshape.288.ts_ref) | copy-start | bytes 24580
  97.4 6.9 %copy-start.2 = (bf16[64,4096]{1,0:T(8,128)(2,1)S(1)}, bf16[64,4096]{1,0:T(8,128)(2,1)}, u32[]{:S(2)}) copy-start(bf16[64,4096]{1,0:T(8,128)(2,1)} %param.12) | copy-start | bytes 1572868
  98.6 26.0 %all-to-all-start.2 = ((bf16[64,36,128]{2,1,0:T(8,128)(2,1)}), bf16[64,36,128]{2,1,0:T(8,128)(2,1)S(1)}, u32[]{:S(2)}, u32[]{:S(2)}) async-start(bf16[64,36,128]{2,1,0:T(8,128)(2,1)} %reshape.293), calls=%async_computation.2 | async-start | bytes 1310720 | tf_op jit(solution)/shard_map/all_to_all | solution.py:95
  127.2 1.7 %copy-start.1 = (bf16[4096,64]{1,0:T(8,128)(2,1)S(1)}, bf16[4096,64]{1,0:T(8,128)(2,1)}, u32[]{:S(2)}) copy-start(bf16[4096,64]{1,0:T(8,128)(2,1)} %copy.20) | copy-start | bytes 1572868
  130.0 24.0 %copy-start.3 = (bf16[64,64]{1,0:T(8,128)(2,1)S(1)}, bf16[64,64]{1,0:T(8,128)(2,1)}, u32[]{:S(2)}) copy-start(bf16[64,64]{1,0:T(8,128)(2,1)} %param.9) | copy-start | bytes 24580

commit v5 on v4

--- a/solution.py
+++ b/solution.py
@@ -26,23 +26,29 @@
     return reached
 
 
-def attention_kernel(limit_ref, q_ref, k_ref, v_ref, ts_ref, o_ref, m_ref, l_ref):
+def attention_kernel(limit_ref, q_ref, k_ref, v_ref, tk_ref, tb_ref, o_ref, m_ref, l_ref, w_ref):
     rows, places = q_ref.shape[1], k_ref.shape[0]
     scale = HEAD ** (-0.5)
+    query = q_ref[0]
     scores = (
         lax.dot_general(
-            k_ref[...], q_ref[0], (((1,), (1,)), ((), ())), preferred_element_type=jnp.float32
+            k_ref[...], query, (((1,), (1,)), ((), ())), preferred_element_type=jnp.float32
         )
         * scale
     )
     valid = lax.broadcasted_iota(jnp.int32, (places, rows), 0) < limit_ref[0]
     scores = jnp.where(valid, scores, NEGATIVE)
-    tree_score = ts_ref[0]
+    own_scores = lax.dot_general(
+        tk_ref[0], query, (((1,), (1,)), ((), ())), preferred_element_type=jnp.float32
+    )
+    tree_score = jnp.where(tb_ref[0] > 0.5, own_scores[0:1, :] * scale, NEGATIVE)
     top = jnp.maximum(jnp.max(scores, axis=0, keepdims=True), tree_score)
     shift = jnp.where(top > 0.5 * NEGATIVE, top, 0.0)
     weights = jnp.exp(scores - shift)
+    tree_weight = jnp.exp(tree_score - shift)
     m_ref[0] = top
-    l_ref[0] = jnp.sum(weights, axis=0, keepdims=True) + jnp.exp(tree_score - shift)
+    l_ref[0] = jnp.sum(weights, axis=0, keepdims=True) + tree_weight
+    w_ref[0] = tree_weight.astype(jnp.bfloat16).astype(jnp.float32)
     o_ref[0] = lax.dot_general(
         weights.astype(jnp.bfloat16),
         v_ref[...],
@@ -51,9 +57,10 @@
     )
 
 
-def local_attention(limit, query, keys, values, tree_scores):
+def local_attention(limit, query, keys, values, tree_keys, tree_valid):
     rows = query.shape[1]
     places = keys.shape[0]
+    lane_row = pl.BlockSpec((1, 1, rows), lambda k, lim: (k, 0, 0))
     return pl.pallas_call(
         attention_kernel,
         grid_spec=pltpu.PrefetchScalarGridSpec(
@@ -63,20 +70,19 @@
                 pl.BlockSpec((1, rows, HEAD), lambda k, lim: (k, 0, 0)),
                 pl.BlockSpec((places, HEAD), lambda k, lim: (0, k)),
                 pl.BlockSpec((places, HEAD), lambda k, lim: (0, k)),
-                pl.BlockSpec((1, 1, rows), lambda k, lim: (k, 0, 0)),
+                pl.BlockSpec((1, 8, HEAD), lambda k, lim: (k, 0, 0)),
+                lane_row,
             ],
             out_specs=[
                 pl.BlockSpec((1, rows, HEAD), lambda k, lim: (k, 0, 0)),
-                pl.BlockSpec((1, 1, rows), lambda k, lim: (k, 0, 0)),
-                pl.BlockSpec((1, 1, rows), lambda k, lim: (k, 0, 0)),
+                lane_row,
+                lane_row,
+                lane_row,
             ],
         ),
-        out_shape=[
-            jax.ShapeDtypeStruct((KV_HEADS, rows, HEAD), jnp.float32),
-            jax.ShapeDtypeStruct((KV_HEADS, 1, rows), jnp.float32),
-            jax.ShapeDtypeStruct((KV_HEADS, 1, rows), jnp.float32),
-        ],
-    )(limit, query, keys, values, tree_scores)
+        out_shape=[jax.ShapeDtypeStruct((KV_HEADS, rows, HEAD), jnp.float32)]
+        + [jax.ShapeDtypeStruct((KV_HEADS, 1, rows), jnp.float32)] * 3,
+    )(limit, query, keys, values, tree_keys, tree_valid)
 
 
 def split3(values):
@@ -142,19 +148,19 @@
     tree_mask = on_path & (key_place < draft_counts[0])[None, :]
 
     query_heads = query.reshape(all_rows, KV_HEADS, groups, HEAD)
-    tree_scores = (
-        jnp.einsum("tkgd,ukd->tkgu", query_heads, own_keys, preferred_element_type=jnp.float32)
-        * scale
-    )
-    tree_scores = jnp.where(tree_mask[:, None, None, :], tree_scores, NEGATIVE)
     limit = (cache_lengths[:1] - tp_rank * places_dev).astype(jnp.int32)
     head_rows = jnp.transpose(query_heads, (1, 2, 0, 3)).reshape(KV_HEADS, groups * all_rows, HEAD)
-    head_tree = jnp.transpose(tree_scores[..., 0], (1, 2, 0)).reshape(KV_HEADS, 1, groups * all_rows)
-    cache_mixed, top_parts, total_parts = local_attention(
-        limit, head_rows, cache_keys[0], cache_values[0], head_tree
-    )
-    shift = jnp.where(top_parts > 0.5 * NEGATIVE, top_parts, 0.0)
-    tree_weight = lax.reduce_precision(jnp.exp(head_tree - shift), exponent_bits=8, mantissa_bits=7)
+    tree_valid = jnp.broadcast_to(
+        tree_mask[:, 0].astype(jnp.float32)[None, None, None, :], (KV_HEADS, 1, groups, all_rows)
+    ).reshape(KV_HEADS, 1, groups * all_rows)
+    cache_mixed, top_parts, total_parts, tree_weight = local_attention(
+        limit,
+        head_rows,
+        cache_keys[0],
+        cache_values[0],
+        jnp.broadcast_to(own_keys[0][:, None, :], (KV_HEADS, 8, HEAD)),
+        tree_valid,
+    )
     head_mixed = cache_mixed + jnp.swapaxes(tree_weight, 1, 2) * own_values[0].reshape(
         KV_HEADS, 1, HEAD
     ).astype(jnp.float32)

time: 155 us -> 155 us (level)
  matrix products: 5.81 us -> 3.41 us
    dot_general x1 -> x0, matrix products: 2.4 us -> none  [on_device(): jnp.einsum('tkgd,ukd->tkgu', query_heads, own_keys, preferred_element_typ...]
where the time goes in v5:
time: 155 us; the launch traced here: 154 us
  waiting for transfers between devices  68.1 us (44%)
  starting transfers between devices  25.3 us (16%)
  blocking collectives  23.3 us (15%)
  local copies, waits for them, and re-layouts  14.7 us (9%)
  Pallas kernels  9.09 us (6%)
  other arithmetic  8 us (5%)
  matrix products  3.41 us (2%)
  between operations  2.36 us (2%)
    all_to_all x3, waiting for transfers between devices, spread(): return lax.all_to_all(pieces, 'tp', 0, 0, tiled=True)  68.1 us
    all_to_all x3, starting transfers between devices, spread(): return lax.all_to_all(pieces, 'tp', 0, 0, tiled=True)  25.3 us
    all_to_all x1, blocking collectives, spread(): return lax.all_to_all(pieces, 'tp', 0, 0, tiled=True)  23.3 us
    pallas_call x1, Pallas kernels, local_attention(): pl.pallas_call(attention_kernel, grid_spec=pltpu.PrefetchScalarGridSpec(n...  9.09 us
  transfers between devices with their start and end apart: 3, of which 3 were waited for; matrix products, arithmetic and copies ran while one was open for 2% of the time, Pallas kernels for 0%

profile of v5, /device:TPU:1, one launch (start us, length us, event | category | flops | bytes accessed | tf_op | source)
XLA Modules:
  0.0 154.2 jit_solution(16695408056543003053)
XLA Ops:
  0.0 0.7 convert_element_type.154
  0.7 0.8 fusion.7
  1.6 1.0 fusion.13
  2.8 2.5 %copy.13 = f32[64,1,5248]{2,1,0:T(1,128)} copy(f32[64,1,5248]{2,0,1:T(8,128)S(1)} %maximum_bitcast_fusion) | data formatting | bytes 2686976 | tf_op jit(solution)/shard_map/reshape | solution.py:125
  5.2 13.3 %all-to-all-start = ((f32[64,1,5248]{2,1,0:T(1,128)}), f32[64,1,5248]{2,1,0:T(1,128)S(1)}, u32[]{:S(2)}, u32[]{:S(2)}) async-start(f32[64,1,5248]{2,1,0:T(1,128)} %copy.13), calls=%async_computation | async-start | bytes 2686976 | tf_op jit(solution)/shard_map/all_to_all | solution.py:101
  20.0 32.8 %all-to-all-done = f32[64,1,5248]{2,1,0:T(1,128)S(1)} async-done(((f32[64,1,5248]{2,1,0:T(1,128)}), f32[64,1,5248]{2,1,0:T(1,128)S(1)}, u32[]{:S(2)}, u32[]{:S(2)}) %all-to-all-start) | async-done | bytes 1343520 | tf_op jit(solution)/shard_map/all_to_all | solution.py:101
  52.8 0.8 reduce_sum.48
  55.0 0.9 broadcast_in_dim.24
  55.9 6.3 %all-to-all-start.1 = ((bf16[64,32,128]{2,1,0:T(8,128)(2,1)}), bf16[64,32,128]{2,1,0:T(8,128)(2,1)S(1)}, u32[]{:S(2)}, u32[]{:S(2)}) async-start(bf16[64,32,128]{2,1,0:T(8,128)(2,1)} %broadcast_in_dim.24), calls=%async_computation.1 | async-start | bytes 1048576 | tf_op jit(solution)/shard_map/all_to_all | solution.py:101
  63.7 16.3 %all-to-all-done.1 = bf16[64,32,128]{2,1,0:T(8,128)(2,1)S(1)} async-done(((bf16[64,32,128]{2,1,0:T(8,128)(2,1)}), bf16[64,32,128]{2,1,0:T(8,128)(2,1)S(1)}, u32[]{:S(2)}, u32[]{:S(2)}) %all-to-all-start.1) | async-done | bytes 524320 | tf_op jit(solution)/shard_map/all_to_all | solution.py:101
  79.9 1.0 copy.14
  82.1 9.1 %shard_map.94 = (f32[4,512,128]{2,1,0:T(8,128)}, f32[4,1,512]{2,1,0:T(1,128)}, f32[4,1,512]{2,1,0:T(1,128)}, f32[4,1,512]{2,1,0:T(1,128)}) custom-call(s32[1]{0:T(128)S(6)} %sub.27.limit_ref, bf16[4,512,128]{2,1,0:T(8,128)(2,1)} %bitcast.72, bf16[1024,512]{1,0:T(8,128)(2,1)} %bitcast.73, bf16[1024,512]{1,0:T(8,128)(2,1)} %bitcast.74, ...), custom_call_target="tpu_custom_call" | custom-call | tf_op jit(solution)/shard_map/pallas_call | solution.py:64
  91.2 0.7 reduce.4
  92.1 0.7 reduce.5
  93.6 1.6 %add_convert_fusion = bf16[4,512,128]{2,1,0:T(8,128)(2,1)S(1)} fusion(f32[4,512,128]{2,1,0:T(8,128)} %get-tuple-element.9, f32[4,128]{1,0:T(4,128)S(1)} %bitcast.81, f32[4,512]{1,0:T(4,128)S(1)} %bitcast.80), kind=kLoop, calls=%fused_computation.17 | loop fusion | flops 786432 | bytes 1583104 | tf_op jit(solution)/shard_map/convert_element_type | solution.py:179
  95.8 0.8 convert_element_type.165
  97.0 1.2 reshape.285
  98.2 5.7 %all-to-all-start.2 = ((bf16[64,36,128]{2,1,0:T(8,128)(2,1)}), bf16[64,36,128]{2,1,0:T(8,128)(2,1)S(1)}, u32[]{:S(2)}, u32[]{:S(2)}) async-start(bf16[64,36,128]{2,1,0:T(8,128)(2,1)} %reshape.285), calls=%async_computation.2 | async-start | bytes 1310720 | tf_op jit(solution)/shard_map/all_to_all | solution.py:101
  103.9 1.3 copy.17
  105.2 19.0 %all-to-all-done.2 = bf16[64,36,128]{2,1,0:T(8,128)(2,1)S(1)} async-done(((bf16[64,36,128]{2,1,0:T(8,128)(2,1)}), bf16[64,36,128]{2,1,0:T(8,128)(2,1)S(1)}, u32[]{:S(2)}, u32[]{:S(2)}) %all-to-all-start.2) | async-done | bytes 589856 | tf_op jit(solution)/shard_map/all_to_all | solution.py:101
  125.1 1.7 %mul.65 = f32[64,4096]{1,0:T(8,128)} reshape(f32[64,64,64]{2,1,0:T(8,128)S(1)} %mul.64) | data formatting | bytes 2097152 | tf_op jit(solution)/shard_map/mul | solution.py:193
  126.8 1.4 multiply_reduce_fusion
  128.5 1.1 fusion
  130.1 23.3 %all_to_all.20 = bf16[64,32,128]{2,1,0:T(8,128)(2,1)S(1)} all-to-all(bf16[64,32,128]{2,1,0:T(8,128)(2,1)S(1)} %convert_element_type.183), channel_id=1, replica_groups=mesh['req'=4,'tp'=64] {'tp'}, dimensions={0} | all-to-all | bytes 1048576 | tf_op jit(solution)/shard_map/all_to_all | solution.py:101
  (52 shorter events, 7.8 us)
Async XLA Ops:
  0.0 1.6 %copy-start = (bf16[64,5120]{1,0:T(8,128)(2,1)S(1)}, bf16[64,5120]{1,0:T(8,128)(2,1)}, u32[]{:S(2)}) copy-start(bf16[64,5120]{1,0:T(8,128)(2,1)} %param.11) | copy-start | bytes 1966084
  5.2 13.9 %copy-start.4 = (s32[1,64]{1,0:T(1,128)S(1)}, s32[1,64]{1,0:T(1,128)}, u32[]{:S(2)}) copy-start(s32[1,64]{1,0:T(1,128)} %param.15) | copy-start | bytes 772
  5.2 47.6 %all-to-all-start = ((f32[64,1,5248]{2,1,0:T(1,128)}), f32[64,1,5248]{2,1,0:T(1,128)S(1)}, u32[]{:S(2)}, u32[]{:S(2)}) async-start(f32[64,1,5248]{2,1,0:T(1,128)} %copy.13), calls=%async_computation | async-start | bytes 2686976 | tf_op jit(solution)/shard_map/all_to_all | solution.py:101
  55.9 24.0 %all-to-all-start.1 = ((bf16[64,32,128]{2,1,0:T(8,128)(2,1)}), bf16[64,32,128]{2,1,0:T(8,128)(2,1)S(1)}, u32[]{:S(2)}, u32[]{:S(2)}) async-start(bf16[64,32,128]{2,1,0:T(8,128)(2,1)} %broadcast_in_dim.24), calls=%async_computation.1 | async-start | bytes 1048576 | tf_op jit(solution)/shard_map/all_to_all | solution.py:101
  97.0 6.9 %copy-start.2 = (bf16[64,4096]{1,0:T(8,128)(2,1)S(1)}, bf16[64,4096]{1,0:T(8,128)(2,1)}, u32[]{:S(2)}) copy-start(bf16[64,4096]{1,0:T(8,128)(2,1)} %param.12) | copy-start | bytes 1572868
  98.2 26.0 %all-to-all-start.2 = ((bf16[64,36,128]{2,1,0:T(8,128)(2,1)}), bf16[64,36,128]{2,1,0:T(8,128)(2,1)S(1)}, u32[]{:S(2)}, u32[]{:S(2)}) async-start(bf16[64,36,128]{2,1,0:T(8,128)(2,1)} %reshape.285), calls=%async_computation.2 | async-start | bytes 1310720 | tf_op jit(solution)/shard_map/all_to_all | solution.py:101
  126.8 1.7 %copy-start.1 = (bf16[4096,64]{1,0:T(8,128)(2,1)S(1)}, bf16[4096,64]{1,0:T(8,128)(2,1)}, u32[]{:S(2)}) copy-start(bf16[4096,64]{1,0:T(8,128)(2,1)} %copy.17) | copy-start | bytes 1572868
  129.6 24.0 %copy-start.3 = (bf16[64,64]{1,0:T(8,128)(2,1)S(1)}, bf16[64,64]{1,0:T(8,128)(2,1)}, u32[]{:S(2)}) copy-start(bf16[64,64]{1,0:T(8,128)(2,1)} %param.9) | copy-start | bytes 24580

commit v6 on v5

--- a/solution.py
+++ b/solution.py
@@ -36,8 +36,8 @@
         )
         * scale
     )
-    valid = lax.broadcasted_iota(jnp.int32, (places, rows), 0) < limit_ref[0]
-    scores = jnp.where(valid, scores, NEGATIVE)
+    position = lax.broadcasted_iota(jnp.int32, (places, 1), 0)
+    scores = scores + jnp.where(position < limit_ref[0], 0.0, NEGATIVE)
     own_scores = lax.dot_general(
         tk_ref[0], query, (((1,), (1,)), ((), ())), preferred_element_type=jnp.float32
     )

time: 155 us -> 154 us (level)
  no operation moved by 1% of the time
where the time goes in v6:
time: 154 us
  waiting for transfers between devices  68.1 us (44%)
  starting transfers between devices  25.3 us (16%)
  blocking collectives  23.3 us (15%)
  local copies, waits for them, and re-layouts  14.7 us (10%)
  Pallas kernels  8.57 us (6%)
  other arithmetic  8 us (5%)
  matrix products  3.41 us (2%)
  between operations  2.36 us (2%)
    all_to_all x3, waiting for transfers between devices, spread(): return lax.all_to_all(pieces, 'tp', 0, 0, tiled=True)  68.1 us
    all_to_all x3, starting transfers between devices, spread(): return lax.all_to_all(pieces, 'tp', 0, 0, tiled=True)  25.3 us
    all_to_all x1, blocking collectives, spread(): return lax.all_to_all(pieces, 'tp', 0, 0, tiled=True)  23.3 us
    pallas_call x1, Pallas kernels, local_attention(): pl.pallas_call(attention_kernel, grid_spec=pltpu.PrefetchScalarGridSpec(n...  8.57 us
  transfers between devices with their start and end apart: 3, of which 3 were waited for; matrix products, arithmetic and copies ran while one was open for 2% of the time, Pallas kernels for 0%

profile of v6, /device:TPU:1, one launch (start us, length us, event | category | flops | bytes accessed | tf_op | source)
XLA Modules:
  0.0 153.7 jit_solution(9875182145701562185)
XLA Ops:
  0.0 0.7 convert_element_type.154
  0.7 0.8 fusion.7
  1.6 1.0 fusion.13
  2.8 2.5 %copy.13 = f32[64,1,5248]{2,1,0:T(1,128)} copy(f32[64,1,5248]{2,0,1:T(8,128)S(1)} %maximum_bitcast_fusion) | data formatting | bytes 2686976 | tf_op jit(solution)/shard_map/reshape | solution.py:125
  5.2 13.3 %all-to-all-start = ((f32[64,1,5248]{2,1,0:T(1,128)}), f32[64,1,5248]{2,1,0:T(1,128)S(1)}, u32[]{:S(2)}, u32[]{:S(2)}) async-start(f32[64,1,5248]{2,1,0:T(1,128)} %copy.13), calls=%async_computation | async-start | bytes 2686976 | tf_op jit(solution)/shard_map/all_to_all | solution.py:101
  20.0 32.8 %all-to-all-done = f32[64,1,5248]{2,1,0:T(1,128)S(1)} async-done(((f32[64,1,5248]{2,1,0:T(1,128)}), f32[64,1,5248]{2,1,0:T(1,128)S(1)}, u32[]{:S(2)}, u32[]{:S(2)}) %all-to-all-start) | async-done | bytes 1343520 | tf_op jit(solution)/shard_map/all_to_all | solution.py:101
  52.8 0.8 reduce_sum.48
  55.0 0.9 broadcast_in_dim.24
  55.9 6.3 %all-to-all-start.1 = ((bf16[64,32,128]{2,1,0:T(8,128)(2,1)}), bf16[64,32,128]{2,1,0:T(8,128)(2,1)S(1)}, u32[]{:S(2)}, u32[]{:S(2)}) async-start(bf16[64,32,128]{2,1,0:T(8,128)(2,1)} %broadcast_in_dim.24), calls=%async_computation.1 | async-start | bytes 1048576 | tf_op jit(solution)/shard_map/all_to_all | solution.py:101
  63.7 16.3 %all-to-all-done.1 = bf16[64,32,128]{2,1,0:T(8,128)(2,1)S(1)} async-done(((bf16[64,32,128]{2,1,0:T(8,128)(2,1)}), bf16[64,32,128]{2,1,0:T(8,128)(2,1)S(1)}, u32[]{:S(2)}, u32[]{:S(2)}) %all-to-all-start.1) | async-done | bytes 524320 | tf_op jit(solution)/shard_map/all_to_all | solution.py:101
  79.9 1.0 copy.14
  82.1 8.6 %shard_map.94 = (f32[4,512,128]{2,1,0:T(8,128)}, f32[4,1,512]{2,1,0:T(1,128)}, f32[4,1,512]{2,1,0:T(1,128)}, f32[4,1,512]{2,1,0:T(1,128)}) custom-call(s32[1]{0:T(128)S(6)} %sub.27.limit_ref, bf16[4,512,128]{2,1,0:T(8,128)(2,1)} %bitcast.72, bf16[1024,512]{1,0:T(8,128)(2,1)} %bitcast.73, bf16[1024,512]{1,0:T(8,128)(2,1)} %bitcast.74, ...), custom_call_target="tpu_custom_call" | custom-call | tf_op jit(solution)/shard_map/pallas_call | solution.py:64
  90.7 0.7 reduce.4
  91.5 0.7 reduce.5
  93.0 1.6 %add_convert_fusion = bf16[4,512,128]{2,1,0:T(8,128)(2,1)S(1)} fusion(f32[4,512,128]{2,1,0:T(8,128)} %get-tuple-element.9, f32[4,128]{1,0:T(4,128)S(1)} %bitcast.81, f32[4,512]{1,0:T(4,128)S(1)} %bitcast.80), kind=kLoop, calls=%fused_computation.17 | loop fusion | flops 786432 | bytes 1583104 | tf_op jit(solution)/shard_map/convert_element_type | solution.py:179
  95.3 0.8 convert_element_type.165
  96.5 1.2 reshape.285
  97.6 5.7 %all-to-all-start.2 = ((bf16[64,36,128]{2,1,0:T(8,128)(2,1)}), bf16[64,36,128]{2,1,0:T(8,128)(2,1)S(1)}, u32[]{:S(2)}, u32[]{:S(2)}) async-start(bf16[64,36,128]{2,1,0:T(8,128)(2,1)} %reshape.285), calls=%async_computation.2 | async-start | bytes 1310720 | tf_op jit(solution)/shard_map/all_to_all | solution.py:101
  103.4 1.3 copy.17
  104.7 19.0 %all-to-all-done.2 = bf16[64,36,128]{2,1,0:T(8,128)(2,1)S(1)} async-done(((bf16[64,36,128]{2,1,0:T(8,128)(2,1)}), bf16[64,36,128]{2,1,0:T(8,128)(2,1)S(1)}, u32[]{:S(2)}, u32[]{:S(2)}) %all-to-all-start.2) | async-done | bytes 589856 | tf_op jit(solution)/shard_map/all_to_all | solution.py:101
  124.6 1.7 %mul.65 = f32[64,4096]{1,0:T(8,128)} reshape(f32[64,64,64]{2,1,0:T(8,128)S(1)} %mul.64) | data formatting | bytes 2097152 | tf_op jit(solution)/shard_map/mul | solution.py:193
  126.3 1.4 multiply_reduce_fusion
  128.0 1.1 fusion
  129.6 23.3 %all_to_all.20 = bf16[64,32,128]{2,1,0:T(8,128)(2,1)S(1)} all-to-all(bf16[64,32,128]{2,1,0:T(8,128)(2,1)S(1)} %convert_element_type.183), channel_id=1, replica_groups=mesh['req'=4,'tp'=64] {'tp'}, dimensions={0} | all-to-all | bytes 1048576 | tf_op jit(solution)/shard_map/all_to_all | solution.py:101
  (52 shorter events, 7.8 us)
Async XLA Ops:
  0.0 1.6 %copy-start = (bf16[64,5120]{1,0:T(8,128)(2,1)S(1)}, bf16[64,5120]{1,0:T(8,128)(2,1)}, u32[]{:S(2)}) copy-start(bf16[64,5120]{1,0:T(8,128)(2,1)} %param.11) | copy-start | bytes 1966084
  5.2 13.9 %copy-start.4 = (s32[1,64]{1,0:T(1,128)S(1)}, s32[1,64]{1,0:T(1,128)}, u32[]{:S(2)}) copy-start(s32[1,64]{1,0:T(1,128)} %param.15) | copy-start | bytes 772
  5.2 47.6 %all-to-all-start = ((f32[64,1,5248]{2,1,0:T(1,128)}), f32[64,1,5248]{2,1,0:T(1,128)S(1)}, u32[]{:S(2)}, u32[]{:S(2)}) async-start(f32[64,1,5248]{2,1,0:T(1,128)} %copy.13), calls=%async_computation | async-start | bytes 2686976 | tf_op jit(solution)/shard_map/all_to_all | solution.py:101
  55.9 24.0 %all-to-all-start.1 = ((bf16[64,32,128]{2,1,0:T(8,128)(2,1)}), bf16[64,32,128]{2,1,0:T(8,128)(2,1)S(1)}, u32[]{:S(2)}, u32[]{:S(2)}) async-start(bf16[64,32,128]{2,1,0:T(8,128)(2,1)} %broadcast_in_dim.24), calls=%async_computation.1 | async-start | bytes 1048576 | tf_op jit(solution)/shard_map/all_to_all | solution.py:101
  96.5 6.9 %copy-start.2 = (bf16[64,4096]{1,0:T(8,128)(2,1)S(1)}, bf16[64,4096]{1,0:T(8,128)(2,1)}, u32[]{:S(2)}) copy-start(bf16[64,4096]{1,0:T(8,128)(2,1)} %param.12) | copy-start | bytes 1572868
  97.6 26.0 %all-to-all-start.2 = ((bf16[64,36,128]{2,1,0:T(8,128)(2,1)}), bf16[64,36,128]{2,1,0:T(8,128)(2,1)S(1)}, u32[]{:S(2)}, u32[]{:S(2)}) async-start(bf16[64,36,128]{2,1,0:T(8,128)(2,1)} %reshape.285), calls=%async_computation.2 | async-start | bytes 1310720 | tf_op jit(solution)/shard_map/all_to_all | solution.py:101
  126.3 1.7 %copy-start.1 = (bf16[4096,64]{1,0:T(8,128)(2,1)S(1)}, bf16[4096,64]{1,0:T(8,128)(2,1)}, u32[]{:S(2)}) copy-start(bf16[4096,64]{1,0:T(8,128)(2,1)} %copy.17) | copy-start | bytes 1572868
  129.1 24.0 %copy-start.3 = (bf16[64,64]{1,0:T(8,128)(2,1)S(1)}, bf16[64,64]{1,0:T(8,128)(2,1)}, u32[]{:S(2)}) copy-start(bf16[64,64]{1,0:T(8,128)(2,1)} %param.9) | copy-start | bytes 24580

commit v7 on v6

--- a/solution.py
+++ b/solution.py
@@ -190,7 +190,9 @@
     rescale = jnp.exp(source_top - top[None])
     total = jnp.sum(rescale * join3(*piece[3:]), axis=0)
     source_mixed = got[:, :flat].reshape(tp_count, all_rows, columns).astype(jnp.float32)
-    mixed_cols = jnp.sum(rescale[..., None] * source_mixed, axis=0)
+    mixed_cols = jnp.einsum(
+        "st,stc->tc", rescale, source_mixed, precision=lax.Precision.HIGHEST
+    )
     attended = (mixed_cols / total[:, None]).astype(jnp.bfloat16)
 
     partial_terms = jnp.dot(attended, w_out, preferred_element_type=jnp.float32)

time: 154 us -> 152 us (0.987)
  blocking collectives: 23.3 us -> 49.1 us
  waiting for transfers between devices: 68.1 us -> 49.1 us
  starting transfers between devices: 25.3 us -> 19.6 us
  other arithmetic: 8 us -> 5.18 us
  local copies, waits for them, and re-layouts: 14.7 us -> 13 us
    all_to_all x1 -> x2, blocking collectives: 23.3 us -> 49.1 us  [spread(): return lax.all_to_all(pieces, 'tp', 0, 0, tiled=True)]
    all_to_all x3 -> x2, waiting for transfers between devices: 68.1 us -> 49.1 us  [spread(): return lax.all_to_all(pieces, 'tp', 0, 0, tiled=True)]
    all_to_all x3 -> x2, starting transfers between devices: 25.3 us -> 19.6 us  [spread(): return lax.all_to_all(pieces, 'tp', 0, 0, tiled=True)]
    mul x2 -> x0, local copies, waits for them, and re-layouts: 2.3 us -> none  [on_device(): mixed_cols = jnp.sum(rescale[..., None] * source_mixed, axis=0)]
    convert_element_type x1 -> x3, local copies, waits for them, and re-layouts: 0.48 us -> 2.28 us  [on_device(): owner_terms.reshape(tp_count, all_rows * out_cols // 128, 128)]
    dot_general x0 -> x1, matrix products: none -> 1.59 us  [on_device(): jnp.einsum('st,stc->tc', rescale, source_mixed, precision=lax.Precision.H...]
  transfers between devices with their start and end apart: 3 -> 2, of which waited for: 3 -> 2; matrix products, arithmetic and copies ran while one was open for 2% -> 1% of each run, Pallas kernels for 0% -> 0%
where the time goes in v7:
time: 152 us; the launch traced here: 151 us
  waiting for transfers between devices  49.1 us (32%)
  blocking collectives  49.1 us (32%)
  starting transfers between devices  19.6 us (13%)
  local copies, waits for them, and re-layouts  13 us (9%)
  Pallas kernels  8.57 us (6%)
  other arithmetic  5.18 us (3%)
  matrix products  4.23 us (3%)
  between operations  2.35 us (2%)
    all_to_all x2, blocking collectives, spread(): return lax.all_to_all(pieces, 'tp', 0, 0, tiled=True)  49.1 us
    all_to_all x2, waiting for transfers between devices, spread(): return lax.all_to_all(pieces, 'tp', 0, 0, tiled=True)  49.1 us
    all_to_all x2, starting transfers between devices, spread(): return lax.all_to_all(pieces, 'tp', 0, 0, tiled=True)  19.6 us
    pallas_call x1, Pallas kernels, local_attention(): pl.pallas_call(attention_kernel, grid_spec=pltpu.PrefetchScalarGridSpec(n...  8.57 us
  transfers between devices with their start and end apart: 2, of which 2 were waited for; matrix products, arithmetic and copies ran while one was open for 1% of the time, Pallas kernels for 0%

profile of v7, /device:TPU:1, one launch (start us, length us, event | category | flops | bytes accessed | tf_op | source)
XLA Modules:
  0.0 151.2 jit_solution(10004209256527208361)
XLA Ops:
  0.0 0.9 fusion.8
  0.9 0.7 convert_element_type.147
  1.6 1.0 fusion.14
  2.8 2.5 %copy.12 = f32[64,1,5248]{2,1,0:T(1,128)} copy(f32[64,1,5248]{2,0,1:T(8,128)S(1)} %maximum_bitcast_fusion) | data formatting | bytes 2686976 | tf_op jit(solution)/shard_map/reshape | solution.py:125
  5.2 13.3 %all-to-all-start = ((f32[64,1,5248]{2,1,0:T(1,128)}), f32[64,1,5248]{2,1,0:T(1,128)S(1)}, u32[]{:S(2)}, u32[]{:S(2)}) async-start(f32[64,1,5248]{2,1,0:T(1,128)} %copy.12), calls=%async_computation | async-start | bytes 2686976 | tf_op jit(solution)/shard_map/all_to_all | solution.py:101
  20.6 32.2 %all-to-all-done = f32[64,1,5248]{2,1,0:T(1,128)S(1)} async-done(((f32[64,1,5248]{2,1,0:T(1,128)}), f32[64,1,5248]{2,1,0:T(1,128)S(1)}, u32[]{:S(2)}, u32[]{:S(2)}) %all-to-all-start) | async-done | bytes 1343520 | tf_op jit(solution)/shard_map/all_to_all | solution.py:101
  52.8 0.8 reduce_sum.39
  55.0 0.9 broadcast_in_dim.24
  55.9 6.3 %all-to-all-start.1 = ((bf16[64,32,128]{2,1,0:T(8,128)(2,1)}), bf16[64,32,128]{2,1,0:T(8,128)(2,1)S(1)}, u32[]{:S(2)}, u32[]{:S(2)}) async-start(bf16[64,32,128]{2,1,0:T(8,128)(2,1)} %broadcast_in_dim.24), calls=%async_computation.1 | async-start | bytes 1048576 | tf_op jit(solution)/shard_map/all_to_all | solution.py:101
  63.0 16.9 %all-to-all-done.1 = bf16[64,32,128]{2,1,0:T(8,128)(2,1)S(1)} async-done(((bf16[64,32,128]{2,1,0:T(8,128)(2,1)}), bf16[64,32,128]{2,1,0:T(8,128)(2,1)S(1)}, u32[]{:S(2)}, u32[]{:S(2)}) %all-to-all-start.1) | async-done | bytes 524320 | tf_op jit(solution)/shard_map/all_to_all | solution.py:101
  79.9 1.0 copy.13
  80.9 0.6 broadcast_in_dim.26.tk_ref
  81.5 0.6 broadcast_in_dim.58.tb_ref
  82.1 8.6 %shard_map.94 = (f32[4,512,128]{2,1,0:T(8,128)}, f32[4,1,512]{2,1,0:T(1,128)}, f32[4,1,512]{2,1,0:T(1,128)}, f32[4,1,512]{2,1,0:T(1,128)}) custom-call(s32[1]{0:T(128)S(6)} %sub.27.limit_ref, bf16[4,512,128]{2,1,0:T(8,128)(2,1)} %bitcast.75, bf16[1024,512]{1,0:T(8,128)(2,1)} %bitcast.76, bf16[1024,512]{1,0:T(8,128)(2,1)} %bitcast.77, ...), custom_call_target="tpu_custom_call" | custom-call | tf_op jit(solution)/shard_map/pallas_call | solution.py:64
  90.7 0.7 copy.30
  91.4 1.6 %add_convert_fusion = bf16[4,512,128]{2,1,0:T(8,128)(2,1)S(1)} fusion(f32[4,512,128]{2,1,0:T(8,128)} %get-tuple-element.9, f32[4,128]{1,0:T(4,128)S(1)} %bitcast.84, f32[4,512]{1,0:T(4,128)S(1)} %bitcast.82), kind=kLoop, calls=%fused_computation.18 | loop fusion | flops 786432 | bytes 1583104 | tf_op jit(solution)/shard_map/convert_element_type | solution.py:179
  93.7 0.8 convert_element_type.158
  95.4 25.8 %all_to_all.20 = bf16[64,36,128]{2,1,0:T(8,128)(2,1)S(1)} all-to-all(bf16[64,36,128]{2,1,0:T(8,128)(2,1)S(1)} %reshape.276), channel_id=1, replica_groups=mesh['req'=4,'tp'=64] {'tp'}, dimensions={0} | all-to-all | bytes 1179648 | tf_op jit(solution)/shard_map/all_to_all | solution.py:101
  121.7 1.1 reshape.278
  122.8 1.6 %fusion.3 = f32[64,1,64]{2,1,0:T(1,128)S(1)} fusion(f32[64,64,1]{0,2,1:T(1,128)S(1)} %copy.16, bf16[64,64,64]{2,1,0:T(8,128)(2,1)S(1)} %reshape.278), kind=kOutput, calls=%fused_computation.13 | convolution fusion | flops 3145728 | bytes 557056 | tf_op jit(solution)/shard_map/st,stc->tc/dot_general | solution.py:193
  124.8 1.1 convert_element_type.173
  125.9 0.7 copy.27
  127.1 23.3 %all_to_all.21 = bf16[64,32,128]{2,1,0:T(8,128)(2,1)S(1)} all-to-all(bf16[64,32,128]{2,1,0:T(8,128)(2,1)S(1)} %convert_element_type.175), channel_id=1, replica_groups=mesh['req'=4,'tp'=64] {'tp'}, dimensions={0} | all-to-all | bytes 1048576 | tf_op jit(solution)/shard_map/all_to_all | solution.py:101
  150.5 0.6 fusion.9
  (51 shorter events, 5.3 us)
Async XLA Ops:
  0.0 1.6 %copy-start = (bf16[64,5120]{1,0:T(8,128)(2,1)S(1)}, bf16[64,5120]{1,0:T(8,128)(2,1)}, u32[]{:S(2)}) copy-start(bf16[64,5120]{1,0:T(8,128)(2,1)} %param.11) | copy-start | bytes 1966084
  5.2 14.6 %copy-start.5 = (s32[1,64]{1,0:T(1,128)S(1)}, s32[1,64]{1,0:T(1,128)}, u32[]{:S(2)}) copy-start(s32[1,64]{1,0:T(1,128)} %param.15) | copy-start | bytes 772
  5.2 47.6 %all-to-all-start = ((f32[64,1,5248]{2,1,0:T(1,128)}), f32[64,1,5248]{2,1,0:T(1,128)S(1)}, u32[]{:S(2)}, u32[]{:S(2)}) async-start(f32[64,1,5248]{2,1,0:T(1,128)} %copy.12), calls=%async_computation | async-start | bytes 2686976 | tf_op jit(solution)/shard_map/all_to_all | solution.py:101
  55.9 24.0 %all-to-all-start.1 = ((bf16[64,32,128]{2,1,0:T(8,128)(2,1)}), bf16[64,32,128]{2,1,0:T(8,128)(2,1)S(1)}, u32[]{:S(2)}, u32[]{:S(2)}) async-start(bf16[64,32,128]{2,1,0:T(8,128)(2,1)} %broadcast_in_dim.24), calls=%async_computation.1 | async-start | bytes 1048576 | tf_op jit(solution)/shard_map/all_to_all | solution.py:101
  93.4 1.1 copy-start.4
  93.4 1.2 copy-start.3
  121.7 2.7 %copy-start.1 = (bf16[64,4096]{1,0:T(8,128)(2,1)S(1)}, bf16[64,4096]{1,0:T(8,128)(2,1)}, u32[]{:S(2)}) copy-start(bf16[64,4096]{1,0:T(8,128)(2,1)} %param.12) | copy-start | bytes 1572868
  126.6 24.0 %copy-start.2 = (bf16[64,64]{1,0:T(8,128)(2,1)S(1)}, bf16[64,64]{1,0:T(8,128)(2,1)}, u32[]{:S(2)}) copy-start(bf16[64,64]{1,0:T(8,128)(2,1)} %param.9) | copy-start | bytes 24580

commit v8 on v7

--- a/solution.py
+++ b/solution.py
@@ -3,11 +3,14 @@
 from jax import lax
 from jax.experimental import pallas as pl
 from jax.experimental.pallas import tpu as pltpu
+from jax.sharding import Mesh
 from jax.sharding import PartitionSpec as P
 
 HEADS = 32
 KV_HEADS = 4
 HEAD = 128
+TP = ("z", "y", "c")
+CHIP = ("z", "y")
 
 
 NEGATIVE = -1e30
@@ -98,14 +101,15 @@
 
 
 def spread(pieces):
-    return lax.all_to_all(pieces, "tp", 0, 0, tiled=True)
+    return lax.all_to_all(pieces, TP, 0, 0, tiled=True)
 
 
 def on_device(
     hidden, norm_gain, w_qkv, w_out, cache_keys, cache_values, parents, draft_counts, cache_lengths
 ):
-    tp_count = lax.axis_size("tp")
-    tp_rank = lax.axis_index("tp")
+    cores = lax.axis_size("c")
+    tp_count = lax.axis_size(CHIP) * cores
+    tp_rank = lax.axis_index(CHIP) * cores + lax.axis_index("c")
     model_width = w_out.shape[1]
     kv_width = KV_HEADS * HEAD
     groups = HEADS // KV_HEADS
@@ -122,7 +126,9 @@
     extended = jnp.concatenate(
         [partial, jnp.broadcast_to(local_squares[:, None], (all_rows, 128))], axis=1
     )
-    gathered = spread(extended.reshape(tp_count, own_count, proj_width + 128))
+    by_core = extended.reshape(tp_count // cores, cores, own_count, proj_width + 128)
+    chip_sum = jnp.sum(lax.all_to_all(by_core, "c", 1, 1, tiled=True), axis=1)
+    gathered = lax.all_to_all(chip_sum, CHIP, 0, 0, tiled=True)
     own_sum = jnp.sum(gathered, axis=0)
     square_sum = own_sum[:, proj_width]
     own_qkv = (
@@ -206,17 +212,19 @@
 
 
 def solution(mesh):
+    tp = mesh.shape["tp"]
+    split = Mesh(mesh.devices.reshape(mesh.shape["req"], tp // 8, 4, 2), ("req",) + TP)
     placed = (
-        P("req", "tp"),
-        P("tp"),
-        P("tp", None),
-        P("tp", None),
-        P("req", "tp", None),
-        P("req", "tp", None),
+        P("req", TP),
+        P(TP),
+        P(TP, None),
+        P(TP, None),
+        P("req", TP, None),
+        P("req", TP, None),
         P("req", None),
         P("req"),
         P("req"),
     )
     return jax.shard_map(
-        on_device, mesh=mesh, in_specs=placed, out_specs=P("req", "tp"), check_vma=False
-    )
+        on_device, mesh=split, in_specs=placed, out_specs=P("req", TP), check_vma=False
+    )

time: 152 us -> 141 us (0.928)
  waiting for transfers between devices: 49.1 us -> 34.1 us
  blocking collectives: 49.1 us -> 56.7 us
  starting transfers between devices: 19.6 us -> 16.8 us
    all_to_all x2, waiting for transfers between devices: 49.1 us -> 34.1 us  [the longest x1 17.2 us: on_device(): gathered = lax.all_to_all(chip_sum, CHIP, 0, 0, tiled=True)]
    all_to_all x2 -> x3, blocking collectives: 49.1 us -> 56.7 us  [the longest x2 49.1 us: spread(): return lax.all_to_all(pieces, TP, 0, 0, tiled=True)]
    all_to_all x2, starting transfers between devices: 19.6 us -> 16.8 us  [the longest x1 9.49 us: on_device(): gathered = lax.all_to_all(chip_sum, CHIP, 0, 0, tiled=True)]
    reshape x1 -> x2, local copies, waits for them, and re-layouts: 2.46 us -> 0.89 us  [on_device(): extended.reshape(tp_count // cores, cores, own_count, proj_width + 128)]
where the time goes in v8:
time: 141 us
  blocking collectives  56.7 us (40%)
  waiting for transfers between devices  34.1 us (24%)
  starting transfers between devices  16.8 us (12%)
  local copies, waits for them, and re-layouts  12.8 us (9%)
  Pallas kernels  8.57 us (6%)
  other arithmetic  4.92 us (3%)
  matrix products  4.23 us (3%)
  between operations  2.39 us (2%)
    all_to_all x2, blocking collectives, spread(): return lax.all_to_all(pieces, TP, 0, 0, tiled=True)  49.1 us
    all_to_all x1, waiting for transfers between devices, on_device(): gathered = lax.all_to_all(chip_sum, CHIP, 0, 0, tiled=True)  17.2 us
    all_to_all x1, waiting for transfers between devices, spread(): return lax.all_to_all(pieces, TP, 0, 0, tiled=True)  16.9 us
    all_to_all x1, starting transfers between devices, on_device(): gathered = lax.all_to_all(chip_sum, CHIP, 0, 0, tiled=True)  9.49 us
    pallas_call x1, Pallas kernels, local_attention(): pl.pallas_call(attention_kernel, grid_spec=pltpu.PrefetchScalarGridSpec(n...  8.57 us
    all_to_all x1, blocking collectives, on_device(): chip_sum = jnp.sum(lax.all_to_all(by_core, 'c', 1, 1, tiled=True), axis=1)  7.63 us
    all_to_all x1, starting transfers between devices, spread(): return lax.all_to_all(pieces, TP, 0, 0, tiled=True)  7.35 us
  transfers between devices with their start and end apart: 2, of which 2 were waited for; matrix products, arithmetic and copies ran while one was open for 1% of the time, Pallas kernels for 0%

profile of v8, /device:TPU:1, one launch (start us, length us, event | category | flops | bytes accessed | tf_op | source)
XLA Modules:
  0.0 140.6 jit_solution(16028623803386486533)
XLA Ops:
  0.0 0.9 fusion.8
  0.9 0.7 convert_element_type.147
  1.6 1.0 fusion.14
  2.8 0.8 reshape.271
  3.7 7.6 %all_to_all.25 = f32[32,2,1,5248]{3,0,2,1:T(8,128)S(1)} all-to-all(f32[32,2,1,5248]{3,0,2,1:T(8,128)S(1)} %copy.12), channel_id=1, replica_groups=mesh['req'=4,'z'=8,'y'=4,'c'=2] {'c'}, dimensions={1} | all-to-all | bytes 2686976 | tf_op jit(solution)/shard_map/all_to_all | solution.py:130
  11.4 1.3 reduce_sum.51
  12.8 9.5 %all-to-all-start.1 = ((f32[32,1,5248]{2,1,0:T(1,128)}), f32[32,1,5248]{2,1,0:T(1,128)S(1)}, u32[]{:S(2)}, u32[]{:S(2)}) async-start(f32[32,1,5248]{2,1,0:T(1,128)} %reduce_sum.51), calls=%async_computation.1 | async-start | bytes 1343488 | tf_op jit(solution)/shard_map/all_to_all | solution.py:131
  24.4 17.2 %all-to-all-done.1 = f32[32,1,5248]{2,1,0:T(1,128)S(1)} async-done(((f32[32,1,5248]{2,1,0:T(1,128)}), f32[32,1,5248]{2,1,0:T(1,128)S(1)}, u32[]{:S(2)}, u32[]{:S(2)}) %all-to-all-start.1) | async-done | bytes 671776 | tf_op jit(solution)/shard_map/all_to_all | solution.py:131
  43.4 0.9 broadcast_in_dim.24
  44.3 7.3 %all-to-all-start.2 = ((bf16[64,32,128]{2,1,0:T(8,128)(2,1)}), bf16[64,32,128]{2,1,0:T(8,128)(2,1)S(1)}, u32[]{:S(2)}, u32[]{:S(2)}) async-start(bf16[64,32,128]{2,1,0:T(8,128)(2,1)} %broadcast_in_dim.24), calls=%async_computation.2 | async-start | bytes 1048576 | tf_op jit(solution)/shard_map/all_to_all | solution.py:104
  52.4 16.9 %all-to-all-done.2 = bf16[64,32,128]{2,1,0:T(8,128)(2,1)S(1)} async-done(((bf16[64,32,128]{2,1,0:T(8,128)(2,1)}), bf16[64,32,128]{2,1,0:T(8,128)(2,1)S(1)}, u32[]{:S(2)}, u32[]{:S(2)}) %all-to-all-start.2) | async-done | bytes 524320 | tf_op jit(solution)/shard_map/all_to_all | solution.py:104
  69.3 1.0 copy.13
  70.3 0.6 broadcast_in_dim.26.tk_ref
  71.5 8.6 %shard_map.94 = (f32[4,512,128]{2,1,0:T(8,128)}, f32[4,1,512]{2,1,0:T(1,128)}, f32[4,1,512]{2,1,0:T(1,128)}, f32[4,1,512]{2,1,0:T(1,128)}) custom-call(s32[1]{0:T(128)S(6)} %sub.27.limit_ref, bf16[4,512,128]{2,1,0:T(8,128)(2,1)} %bitcast.73, bf16[1024,512]{1,0:T(8,128)(2,1)} %bitcast.74, bf16[1024,512]{1,0:T(8,128)(2,1)} %bitcast.75, ...), custom_call_target="tpu_custom_call" | custom-call | tf_op jit(solution)/shard_map/pallas_call | solution.py:67
  80.1 0.7 copy.30
  80.8 1.6 %add_convert_fusion = bf16[4,512,128]{2,1,0:T(8,128)(2,1)S(1)} fusion(f32[4,512,128]{2,1,0:T(8,128)} %get-tuple-element.9, f32[4,128]{1,0:T(4,128)S(1)} %bitcast.82, f32[4,512]{1,0:T(4,128)S(1)} %bitcast.80), kind=kLoop, calls=%fused_computation.18 | loop fusion | flops 786432 | bytes 1583104 | tf_op jit(solution)/shard_map/convert_element_type | solution.py:185
  83.1 0.8 convert_element_type.158
  84.8 25.8 %all_to_all.26 = bf16[64,36,128]{2,1,0:T(8,128)(2,1)S(1)} all-to-all(bf16[64,36,128]{2,1,0:T(8,128)(2,1)S(1)} %reshape.277), channel_id=1, replica_groups=mesh['req'=4,'z'=8,'y'=4,'c'=2] {'z','y','c'}, dimensions={0} | all-to-all | bytes 1179648 | tf_op jit(solution)/shard_map/all_to_all | solution.py:104
  111.1 1.1 reshape.279
  112.2 1.6 %fusion.3 = f32[64,1,64]{2,1,0:T(1,128)S(1)} fusion(f32[64,64,1]{0,2,1:T(1,128)S(1)} %copy.16, bf16[64,64,64]{2,1,0:T(8,128)(2,1)S(1)} %reshape.279), kind=kOutput, calls=%fused_computation.13 | convolution fusion | flops 3145728 | bytes 557056 | tf_op jit(solution)/shard_map/st,stc->tc/dot_general | solution.py:199
  114.2 1.1 convert_element_type.173
  115.3 0.7 copy.27
  116.5 23.3 %all_to_all.27 = bf16[64,32,128]{2,1,0:T(8,128)(2,1)S(1)} all-to-all(bf16[64,32,128]{2,1,0:T(8,128)(2,1)S(1)} %convert_element_type.175), channel_id=1, replica_groups=mesh['req'=4,'z'=8,'y'=4,'c'=2] {'z','y','c'}, dimensions={0} | all-to-all | bytes 1048576 | tf_op jit(solution)/shard_map/all_to_all | solution.py:104
  139.9 0.6 fusion.9
  (55 shorter events, 6.5 us)
Async XLA Ops:
  0.0 1.6 %copy-start = (bf16[64,5120]{1,0:T(8,128)(2,1)S(1)}, bf16[64,5120]{1,0:T(8,128)(2,1)}, u32[]{:S(2)}) copy-start(bf16[64,5120]{1,0:T(8,128)(2,1)} %param.11) | copy-start | bytes 1966084
  11.4 12.1 %copy-start.5 = (s32[1,64]{1,0:T(1,128)S(1)}, s32[1,64]{1,0:T(1,128)}, u32[]{:S(2)}) copy-start(s32[1,64]{1,0:T(1,128)} %param.15) | copy-start | bytes 772
  12.8 28.8 %all-to-all-start.1 = ((f32[32,1,5248]{2,1,0:T(1,128)}), f32[32,1,5248]{2,1,0:T(1,128)S(1)}, u32[]{:S(2)}, u32[]{:S(2)}) async-start(f32[32,1,5248]{2,1,0:T(1,128)} %reduce_sum.51), calls=%async_computation.1 | async-start | bytes 1343488 | tf_op jit(solution)/shard_map/all_to_all | solution.py:131
  44.3 25.0 %all-to-all-start.2 = ((bf16[64,32,128]{2,1,0:T(8,128)(2,1)}), bf16[64,32,128]{2,1,0:T(8,128)(2,1)S(1)}, u32[]{:S(2)}, u32[]{:S(2)}) async-start(bf16[64,32,128]{2,1,0:T(8,128)(2,1)} %broadcast_in_dim.24), calls=%async_computation.2 | async-start | bytes 1048576 | tf_op jit(solution)/shard_map/all_to_all | solution.py:104
  82.8 1.1 copy-start.4
  82.8 1.2 copy-start.3
  111.1 2.7 %copy-start.1 = (bf16[64,4096]{1,0:T(8,128)(2,1)S(1)}, bf16[64,4096]{1,0:T(8,128)(2,1)}, u32[]{:S(2)}) copy-start(bf16[64,4096]{1,0:T(8,128)(2,1)} %param.12) | copy-start | bytes 1572868
  116.0 24.0 %copy-start.2 = (bf16[64,64]{1,0:T(8,128)(2,1)S(1)}, bf16[64,64]{1,0:T(8,128)(2,1)}, u32[]{:S(2)}) copy-start(bf16[64,64]{1,0:T(8,128)(2,1)} %param.9) | copy-start | bytes 24580

commit v9 on v8

--- a/solution.py
+++ b/solution.py
@@ -136,9 +136,14 @@
     ).astype(jnp.bfloat16)
     own_queries = own_qkv[:, :model_width]
     lanes = own_count * model_width // 128
-    query = spread(
-        jnp.broadcast_to(own_queries.reshape(1, lanes, 128), (tp_count, lanes, 128))
-    ).reshape(all_rows, model_width)
+    chips = tp_count // cores
+    chip_rows = lax.all_to_all(
+        jnp.broadcast_to(own_queries.reshape(1, lanes, 128), (chips, lanes, 128)), CHIP, 0, 0, tiled=True
+    )
+    core_rows = lax.all_to_all(
+        jnp.broadcast_to(chip_rows[None], (cores, chips, lanes, 128)), "c", 0, 0, tiled=True
+    )
+    query = jnp.swapaxes(core_rows, 0, 1).reshape(all_rows, model_width)
     own_tokens = own_qkv[:, model_width:]
     own_keys = own_tokens[:, :kv_width].reshape(own_count, KV_HEADS, HEAD)
     own_values = own_tokens[:, kv_width:].reshape(own_count, KV_HEADS, HEAD)
@@ -204,8 +209,14 @@
     partial_terms = jnp.dot(attended, w_out, preferred_element_type=jnp.float32)
     out_cols = model_width // tp_count
     owner_terms = jnp.swapaxes(partial_terms.reshape(all_rows, tp_count, out_cols), 0, 1)
-    terms = spread(
-        owner_terms.reshape(tp_count, all_rows * out_cols // 128, 128).astype(jnp.bfloat16)
+    by_core = owner_terms.reshape(chips, cores, all_rows * out_cols)
+    chip_terms = jnp.sum(lax.all_to_all(by_core, "c", 1, 1, tiled=True), axis=1)
+    terms = lax.all_to_all(
+        chip_terms.reshape(chips, all_rows * out_cols // 128, 128).astype(jnp.bfloat16),
+        CHIP,
+        0,
+        0,
+        tiled=True,
     )
     projected = jnp.sum(terms.astype(jnp.float32), axis=0).reshape(all_rows, out_cols)
     return (inputs + projected).astype(jnp.bfloat16)

time: 141 us -> 144 us (1.021)
  waiting for transfers between devices: 34.1 us -> 26.8 us
  local copies, waits for them, and re-layouts: 12.8 us -> 18.3 us
  blocking collectives: 56.7 us -> 60.4 us
  starting transfers between devices: 16.8 us -> 14.9 us
    all_to_all x0 -> x3, blocking collectives: none -> 28.5 us  [the longest x1 16.2 us: on_device(): lax.all_to_all(chip_terms.reshape(chips, all_rows * out_cols // 128, 128)...]
    all_to_all x2 -> x1, blocking collectives: 49.1 us -> 24.3 us  [spread(): return lax.all_to_all(pieces, TP, 0, 0, tiled=True)]
    all_to_all x1, waiting for transfers between devices: 16.9 us -> 8.65 us  [on_device(): lax.all_to_all(jnp.broadcast_to(own_queries.reshape(1, lanes, 128), (chip...]
    reshape x0 -> x4, local copies, waits for them, and re-layouts: none -> 7.62 us  [the longest x2 4.57 us: on_device(): partial_terms.reshape(all_rows, tp_count, out_cols)]
    convert_element_type x3 -> x0, local copies, waits for them, and re-layouts: 2.28 us -> none  [on_device(): owner_terms.reshape(tp_count, all_rows * out_cols // 128, 128)]
    all_to_all x1, starting transfers between devices: 7.35 us -> 5.42 us  [on_device(): lax.all_to_all(jnp.broadcast_to(own_queries.reshape(1, lanes, 128), (chip...]
where the time goes in v9:
time: 144 us; the launch traced here: 143 us
  blocking collectives  60.4 us (42%)
  waiting for transfers between devices  26.8 us (19%)
  local copies, waits for them, and re-layouts  18.3 us (13%)
  starting transfers between devices  14.9 us (10%)
  Pallas kernels  8.57 us (6%)
  other arithmetic  6.3 us (4%)
  matrix products  5.23 us (4%)
  between operations  2.34 us (2%)
    all_to_all x1, blocking collectives, spread(): return lax.all_to_all(pieces, TP, 0, 0, tiled=True)  24.3 us
    all_to_all x1, waiting for transfers between devices, on_device(): gathered = lax.all_to_all(chip_sum, CHIP, 0, 0, tiled=True)  18.2 us
    all_to_all x1, blocking collectives, on_device(): lax.all_to_all(chip_terms.reshape(chips, all_rows * out_cols // 128, 128)...  16.2 us
    all_to_all x1, starting transfers between devices, on_device(): gathered = lax.all_to_all(chip_sum, CHIP, 0, 0, tiled=True)  9.5 us
    all_to_all x1, waiting for transfers between devices, on_device(): lax.all_to_all(jnp.broadcast_to(own_queries.reshape(1, lanes, 128), (chip...  8.65 us
    pallas_call x1, Pallas kernels, local_attention(): pl.pallas_call(attention_kernel, grid_spec=pltpu.PrefetchScalarGridSpec(n...  8.57 us
    all_to_all x1, blocking collectives, on_device(): chip_sum = jnp.sum(lax.all_to_all(by_core, 'c', 1, 1, tiled=True), axis=1)  7.62 us
    all_to_all x1, blocking collectives, on_device(): lax.all_to_all(jnp.broadcast_to(chip_rows[None], (cores, chips, lanes, 12...  7.54 us
  transfers between devices with their start and end apart: 2, of which 2 were waited for; matrix products, arithmetic and copies ran while one was open for 1% of the time, Pallas kernels for 0%

profile of v9, /device:TPU:1, one launch (start us, length us, event | category | flops | bytes accessed | tf_op | source)
XLA Modules:
  0.0 142.8 jit_solution(11393505446640688155)
XLA Ops:
  0.7 0.8 fusion.8
  1.6 1.0 fusion.15
  2.8 0.8 reshape.276
  3.7 7.6 %all_to_all.35 = f32[32,2,1,5248]{3,0,2,1:T(8,128)S(1)} all-to-all(f32[32,2,1,5248]{3,0,2,1:T(8,128)S(1)} %copy.24), channel_id=1, replica_groups=mesh['req'=4,'z'=8,'y'=4,'c'=2] {'c'}, dimensions={1} | all-to-all | bytes 2686976 | tf_op jit(solution)/shard_map/all_to_all | solution.py:130
  11.4 1.3 reduce_sum.60
  12.8 9.5 %all-to-all-start.1 = ((f32[32,1,5248]{2,1,0:T(1,128)}), f32[32,1,5248]{2,1,0:T(1,128)S(1)}, u32[]{:S(2)}, u32[]{:S(2)}) async-start(f32[32,1,5248]{2,1,0:T(1,128)} %reduce_sum.60), calls=%async_computation.1 | async-start | bytes 1343488 | tf_op jit(solution)/shard_map/all_to_all | solution.py:131
  23.4 18.2 %all-to-all-done.1 = f32[32,1,5248]{2,1,0:T(1,128)S(1)} async-done(((f32[32,1,5248]{2,1,0:T(1,128)}), f32[32,1,5248]{2,1,0:T(1,128)S(1)}, u32[]{:S(2)}, u32[]{:S(2)}) %all-to-all-start.1) | async-done | bytes 671776 | tf_op jit(solution)/shard_map/all_to_all | solution.py:131
  43.3 0.7 broadcast_in_dim.26
  44.0 5.4 %all-to-all-start.2 = ((bf16[32,32,128]{2,1,0:T(8,128)(2,1)}), bf16[32,32,128]{2,1,0:T(8,128)(2,1)S(1)}, u32[]{:S(2)}, u32[]{:S(2)}) async-start(bf16[32,32,128]{2,1,0:T(8,128)(2,1)} %broadcast_in_dim.26), calls=%async_computation.2 | async-start | bytes 524288 | tf_op jit(solution)/shard_map/all_to_all | solution.py:140
  51.2 8.7 %all-to-all-done.2 = bf16[32,32,128]{2,1,0:T(8,128)(2,1)S(1)} async-done(((bf16[32,32,128]{2,1,0:T(8,128)(2,1)}), bf16[32,32,128]{2,1,0:T(8,128)(2,1)S(1)}, u32[]{:S(2)}, u32[]{:S(2)}) %all-to-all-start.2) | async-done | bytes 262176 | tf_op jit(solution)/shard_map/all_to_all | solution.py:140
  60.0 7.5 %all_to_all.36 = bf16[2,32,32,128]{3,1,2,0:T(8,128)(2,1)S(1)} all-to-all(bf16[2,32,32,128]{3,1,2,0:T(8,128)(2,1)S(1)} %broadcast_in_dim.27), channel_id=1, replica_groups=mesh['req'=4,'z'=8,'y'=4,'c'=2] {'c'}, dimensions={0} | all-to-all | bytes 1048576 | tf_op jit(solution)/shard_map/all_to_all | solution.py:143
  67.8 1.0 copy.27
  70.0 8.6 %shard_map.94 = (f32[4,512,128]{2,1,0:T(8,128)}, f32[4,1,512]{2,1,0:T(1,128)}, f32[4,1,512]{2,1,0:T(1,128)}, f32[4,1,512]{2,1,0:T(1,128)}) custom-call(s32[1]{0:T(128)S(6)} %sub.27.limit_ref, bf16[4,512,128]{2,1,0:T(8,128)(2,1)} %bitcast.79, bf16[1024,512]{1,0:T(8,128)(2,1)} %bitcast.81, bf16[1024,512]{1,0:T(8,128)(2,1)} %bitcast.82, ...), custom_call_target="tpu_custom_call" | custom-call | tf_op jit(solution)/shard_map/pallas_call | solution.py:67
  80.9 1.6 %add_convert_fusion = bf16[4,512,128]{2,1,0:T(8,128)(2,1)S(1)} fusion(f32[4,512,128]{2,1,0:T(8,128)} %get-tuple-element.9, f32[4,128]{1,0:T(4,128)S(1)} %bitcast.90, f32[4,512]{1,0:T(4,128)S(1)} %bitcast.87), kind=kLoop, calls=%fused_computation.16 | loop fusion | flops 786432 | bytes 1583104 | tf_op jit(solution)/shard_map/convert_element_type | solution.py:190
  83.1 0.8 convert_element_type.152
  84.6 24.3 %all_to_all.37 = bf16[64,36,128]{2,1,0:T(8,128)(2,1)S(1)} all-to-all(bf16[64,36,128]{2,1,0:T(8,128)(2,1)S(1)} %reshape.282), channel_id=1, replica_groups=mesh['req'=4,'z'=8,'y'=4,'c'=2] {'z','y','c'}, dimensions={0} | all-to-all | bytes 1179648 | tf_op jit(solution)/shard_map/all_to_all | solution.py:104
  109.3 1.1 reshape.284
  110.4 1.6 %fusion.3 = f32[64,1,64]{2,1,0:T(1,128)S(1)} fusion(f32[64,64,1]{0,2,1:T(1,128)S(1)} %copy.31, bf16[64,64,64]{2,1,0:T(8,128)(2,1)S(1)} %reshape.284), kind=kOutput, calls=%fused_computation.13 | convolution fusion | flops 3145728 | bytes 557056 | tf_op jit(solution)/shard_map/st,stc->tc/dot_general | solution.py:204
  112.0 1.4 fusion.14
  113.4 2.0 %reshape.285 = f32[64,64,64]{2,1,0:T(8,128)S(1)} reshape(f32[64,4096]{1,0:T(8,128)} %fusion.14) | data formatting | bytes 2097152 | tf_op jit(solution)/shard_map/reshape | solution.py:211
  115.4 2.6 %copy.43 = f32[64,64,64]{2,0,1:T(8,128)} copy(f32[64,64,64]{2,1,0:T(8,128)S(1)} %reshape.285) | data formatting | bytes 2097152 | tf_op jit(solution)/shard_map/reshape | solution.py:211
  118.0 2.4 %reshape.286 = f32[32,2,4096]{2,1,0:T(2,128)S(1)} reshape(f32[64,64,64]{2,1,0:T(8,128)} %bitcast.72) | data formatting | bytes 2097152 | tf_op jit(solution)/shard_map/reshape | solution.py:212
  121.0 4.7 %all_to_all.38 = f32[32,2,4096]{2,0,1:T(8,128)S(1)} all-to-all(f32[32,2,4096]{2,0,1:T(8,128)S(1)} %copy.30), channel_id=1, replica_groups=mesh['req'=4,'z'=8,'y'=4,'c'=2] {'c'}, dimensions={1} | all-to-all | bytes 2097152 | tf_op jit(solution)/shard_map/all_to_all | solution.py:213
  125.9 16.2 %all_to_all.39 = bf16[32,32,128]{2,1,0:T(8,128)(2,1)S(1)} all-to-all(bf16[32,32,128]{2,1,0:T(8,128)(2,1)S(1)} %bitcast.83), channel_id=1, replica_groups=mesh['req'=4,'z'=8,'y'=4,'c'=2] {'z','y'}, dimensions={0} | all-to-all | bytes 524288 | tf_op jit(solution)/shard_map/all_to_all | solution.py:214
  (59 shorter events, 10.7 us)
Async XLA Ops:
  0.0 1.6 %copy-start = (bf16[64,5120]{1,0:T(8,128)(2,1)S(1)}, bf16[64,5120]{1,0:T(8,128)(2,1)}, u32[]{:S(2)}) copy-start(bf16[64,5120]{1,0:T(8,128)(2,1)} %param.11) | copy-start | bytes 1966084
  11.4 10.8 %copy-start.3 = (s32[1,64]{1,0:T(1,128)S(1)}, s32[1,64]{1,0:T(1,128)}, u32[]{:S(2)}) copy-start(s32[1,64]{1,0:T(1,128)} %param.15) | copy-start | bytes 772
  12.8 28.8 %all-to-all-start.1 = ((f32[32,1,5248]{2,1,0:T(1,128)}), f32[32,1,5248]{2,1,0:T(1,128)S(1)}, u32[]{:S(2)}, u32[]{:S(2)}) async-start(f32[32,1,5248]{2,1,0:T(1,128)} %reduce_sum.60), calls=%async_computation.1 | async-start | bytes 1343488 | tf_op jit(solution)/shard_map/all_to_all | solution.py:131
  44.0 15.8 %all-to-all-start.2 = ((bf16[32,32,128]{2,1,0:T(8,128)(2,1)}), bf16[32,32,128]{2,1,0:T(8,128)(2,1)S(1)}, u32[]{:S(2)}, u32[]{:S(2)}) async-start(bf16[32,32,128]{2,1,0:T(8,128)(2,1)} %broadcast_in_dim.26), calls=%async_computation.2 | async-start | bytes 524288 | tf_op jit(solution)/shard_map/all_to_all | solution.py:140
  109.3 2.7 %copy-start.1 = (bf16[64,4096]{1,0:T(8,128)(2,1)S(1)}, bf16[64,4096]{1,0:T(8,128)(2,1)}, u32[]{:S(2)}) copy-start(bf16[64,4096]{1,0:T(8,128)(2,1)} %param.12) | copy-start | bytes 1572868
  125.8 16.4 %copy-start.2 = (bf16[64,64]{1,0:T(8,128)(2,1)S(1)}, bf16[64,64]{1,0:T(8,128)(2,1)}, u32[]{:S(2)}) copy-start(bf16[64,64]{1,0:T(8,128)(2,1)} %param.9) | copy-start | bytes 24580

commit v10 on v9

--- a/solution.py
+++ b/solution.py
@@ -209,14 +209,8 @@
     partial_terms = jnp.dot(attended, w_out, preferred_element_type=jnp.float32)
     out_cols = model_width // tp_count
     owner_terms = jnp.swapaxes(partial_terms.reshape(all_rows, tp_count, out_cols), 0, 1)
-    by_core = owner_terms.reshape(chips, cores, all_rows * out_cols)
-    chip_terms = jnp.sum(lax.all_to_all(by_core, "c", 1, 1, tiled=True), axis=1)
-    terms = lax.all_to_all(
-        chip_terms.reshape(chips, all_rows * out_cols // 128, 128).astype(jnp.bfloat16),
-        CHIP,
-        0,
-        0,
-        tiled=True,
+    terms = spread(
+        owner_terms.reshape(tp_count, all_rows * out_cols // 128, 128).astype(jnp.bfloat16)
     )
     projected = jnp.sum(terms.astype(jnp.float32), axis=0).reshape(all_rows, out_cols)
     return (inputs + projected).astype(jnp.bfloat16)

time: 144 us -> 138 us (0.958)
  local copies, waits for them, and re-layouts: 18.3 us -> 12.9 us
  blocking collectives: 60.4 us -> 62.7 us
    all_to_all x1 -> x2, blocking collectives: 24.3 us -> 47.5 us  [spread(): return lax.all_to_all(pieces, TP, 0, 0, tiled=True)]
    all_to_all x2 -> x0, blocking collectives: 20.9 us -> none  [the longest x1 16.2 us: on_device(): lax.all_to_all(chip_terms.reshape(chips, all_rows * out_cols // 128, 128)...]
    reshape x4 -> x0, local copies, waits for them, and re-layouts: 7.62 us -> none  [the longest x2 4.57 us: on_device(): partial_terms.reshape(all_rows, tp_count, out_cols)]
    convert_element_type x0 -> x3, local copies, waits for them, and re-layouts: none -> 2.28 us  [on_device(): owner_terms.reshape(tp_count, all_rows * out_cols // 128, 128)]
where the time goes in v10:
time: 138 us; the launch traced here: 137 us
  blocking collectives  62.7 us (45%)
  waiting for transfers between devices  26.8 us (19%)
  starting transfers between devices  14.9 us (11%)
  local copies, waits for them, and re-layouts  12.9 us (9%)
  Pallas kernels  8.57 us (6%)
  other arithmetic  4.92 us (4%)
  matrix products  4.22 us (3%)
  between operations  2.35 us (2%)
    all_to_all x2, blocking collectives, spread(): return lax.all_to_all(pieces, TP, 0, 0, tiled=True)  47.5 us
    all_to_all x1, waiting for transfers between devices, on_device(): gathered = lax.all_to_all(chip_sum, CHIP, 0, 0, tiled=True)  18.2 us
    all_to_all x1, starting transfers between devices, on_device(): gathered = lax.all_to_all(chip_sum, CHIP, 0, 0, tiled=True)  9.49 us
    all_to_all x1, waiting for transfers between devices, on_device(): lax.all_to_all(jnp.broadcast_to(own_queries.reshape(1, lanes, 128), (chip...  8.65 us
    pallas_call x1, Pallas kernels, local_attention(): pl.pallas_call(attention_kernel, grid_spec=pltpu.PrefetchScalarGridSpec(n...  8.57 us
    all_to_all x1, blocking collectives, on_device(): chip_sum = jnp.sum(lax.all_to_all(by_core, 'c', 1, 1, tiled=True), axis=1)  7.63 us
    all_to_all x1, blocking collectives, on_device(): lax.all_to_all(jnp.broadcast_to(chip_rows[None], (cores, chips, lanes, 12...  7.54 us
    all_to_all x1, starting transfers between devices, on_device(): lax.all_to_all(jnp.broadcast_to(own_queries.reshape(1, lanes, 128), (chip...  5.42 us
  transfers between devices with their start and end apart: 2, of which 2 were waited for; matrix products, arithmetic and copies ran while one was open for 1% of the time, Pallas kernels for 0%

profile of v10, /device:TPU:1, one launch (start us, length us, event | category | flops | bytes accessed | tf_op | source)
XLA Modules:
  0.0 137.4 jit_solution(1783150242010300413)
XLA Ops:
  0.0 0.9 fusion.8
  0.9 0.7 convert_element_type.147
  1.6 1.0 fusion.14
  2.8 0.8 reshape.272
  3.7 7.6 %all_to_all.30 = f32[32,2,1,5248]{3,0,2,1:T(8,128)S(1)} all-to-all(f32[32,2,1,5248]{3,0,2,1:T(8,128)S(1)} %copy.16), channel_id=1, replica_groups=mesh['req'=4,'z'=8,'y'=4,'c'=2] {'c'}, dimensions={1} | all-to-all | bytes 2686976 | tf_op jit(solution)/shard_map/all_to_all | solution.py:130
  11.4 1.3 reduce_sum.51
  12.8 9.5 %all-to-all-start.1 = ((f32[32,1,5248]{2,1,0:T(1,128)}), f32[32,1,5248]{2,1,0:T(1,128)S(1)}, u32[]{:S(2)}, u32[]{:S(2)}) async-start(f32[32,1,5248]{2,1,0:T(1,128)} %reduce_sum.51), calls=%async_computation.1 | async-start | bytes 1343488 | tf_op jit(solution)/shard_map/all_to_all | solution.py:131
  23.4 18.2 %all-to-all-done.1 = f32[32,1,5248]{2,1,0:T(1,128)S(1)} async-done(((f32[32,1,5248]{2,1,0:T(1,128)}), f32[32,1,5248]{2,1,0:T(1,128)S(1)}, u32[]{:S(2)}, u32[]{:S(2)}) %all-to-all-start.1) | async-done | bytes 671776 | tf_op jit(solution)/shard_map/all_to_all | solution.py:131
  43.3 0.7 broadcast_in_dim.26
  44.0 5.4 %all-to-all-start.2 = ((bf16[32,32,128]{2,1,0:T(8,128)(2,1)}), bf16[32,32,128]{2,1,0:T(8,128)(2,1)S(1)}, u32[]{:S(2)}, u32[]{:S(2)}) async-start(bf16[32,32,128]{2,1,0:T(8,128)(2,1)} %broadcast_in_dim.26), calls=%async_computation.2 | async-start | bytes 524288 | tf_op jit(solution)/shard_map/all_to_all | solution.py:140
  51.2 8.7 %all-to-all-done.2 = bf16[32,32,128]{2,1,0:T(8,128)(2,1)S(1)} async-done(((bf16[32,32,128]{2,1,0:T(8,128)(2,1)}), bf16[32,32,128]{2,1,0:T(8,128)(2,1)S(1)}, u32[]{:S(2)}, u32[]{:S(2)}) %all-to-all-start.2) | async-done | bytes 262176 | tf_op jit(solution)/shard_map/all_to_all | solution.py:140
  60.0 7.5 %all_to_all.31 = bf16[2,32,32,128]{3,1,2,0:T(8,128)(2,1)S(1)} all-to-all(bf16[2,32,32,128]{3,1,2,0:T(8,128)(2,1)S(1)} %broadcast_in_dim.27), channel_id=1, replica_groups=mesh['req'=4,'z'=8,'y'=4,'c'=2] {'c'}, dimensions={0} | all-to-all | bytes 1048576 | tf_op jit(solution)/shard_map/all_to_all | solution.py:143
  67.8 1.0 copy.19
  70.0 8.6 %shard_map.94 = (f32[4,512,128]{2,1,0:T(8,128)}, f32[4,1,512]{2,1,0:T(1,128)}, f32[4,1,512]{2,1,0:T(1,128)}, f32[4,1,512]{2,1,0:T(1,128)}) custom-call(s32[1]{0:T(128)S(6)} %sub.27.limit_ref, bf16[4,512,128]{2,1,0:T(8,128)(2,1)} %bitcast.75, bf16[1024,512]{1,0:T(8,128)(2,1)} %bitcast.76, bf16[1024,512]{1,0:T(8,128)(2,1)} %bitcast.77, ...), custom_call_target="tpu_custom_call" | custom-call | tf_op jit(solution)/shard_map/pallas_call | solution.py:67
  78.6 0.7 copy.36
  79.3 1.6 %add_convert_fusion = bf16[4,512,128]{2,1,0:T(8,128)(2,1)S(1)} fusion(f32[4,512,128]{2,1,0:T(8,128)} %get-tuple-element.9, f32[4,128]{1,0:T(4,128)S(1)} %bitcast.84, f32[4,512]{1,0:T(4,128)S(1)} %bitcast.81), kind=kLoop, calls=%fused_computation.18 | loop fusion | flops 786432 | bytes 1583104 | tf_op jit(solution)/shard_map/convert_element_type | solution.py:190
  81.5 0.8 convert_element_type.158
  83.3 24.3 %all_to_all.32 = bf16[64,36,128]{2,1,0:T(8,128)(2,1)S(1)} all-to-all(bf16[64,36,128]{2,1,0:T(8,128)(2,1)S(1)} %reshape.278), channel_id=1, replica_groups=mesh['req'=4,'z'=8,'y'=4,'c'=2] {'z','y','c'}, dimensions={0} | all-to-all | bytes 1179648 | tf_op jit(solution)/shard_map/all_to_all | solution.py:104
  108.0 1.1 reshape.280
  109.1 1.6 %fusion.3 = f32[64,1,64]{2,1,0:T(1,128)S(1)} fusion(f32[64,64,1]{0,2,1:T(1,128)S(1)} %copy.22, bf16[64,64,64]{2,1,0:T(8,128)(2,1)S(1)} %reshape.280), kind=kOutput, calls=%fused_computation.13 | convolution fusion | flops 3145728 | bytes 557056 | tf_op jit(solution)/shard_map/st,stc->tc/dot_general | solution.py:204
  111.0 1.1 convert_element_type.173
  112.2 0.7 copy.33
  113.4 23.3 %all_to_all.33 = bf16[64,32,128]{2,1,0:T(8,128)(2,1)S(1)} all-to-all(bf16[64,32,128]{2,1,0:T(8,128)(2,1)S(1)} %convert_element_type.175), channel_id=1, replica_groups=mesh['req'=4,'z'=8,'y'=4,'c'=2] {'z','y','c'}, dimensions={0} | all-to-all | bytes 1048576 | tf_op jit(solution)/shard_map/all_to_all | solution.py:104
  136.8 0.6 fusion.9
  (59 shorter events, 7.4 us)
Async XLA Ops:
  0.0 1.6 %copy-start = (bf16[64,5120]{1,0:T(8,128)(2,1)S(1)}, bf16[64,5120]{1,0:T(8,128)(2,1)}, u32[]{:S(2)}) copy-start(bf16[64,5120]{1,0:T(8,128)(2,1)} %param.11) | copy-start | bytes 1966084
  11.4 10.8 %copy-start.5 = (s32[1,64]{1,0:T(1,128)S(1)}, s32[1,64]{1,0:T(1,128)}, u32[]{:S(2)}) copy-start(s32[1,64]{1,0:T(1,128)} %param.15) | copy-start | bytes 772
  12.8 28.8 %all-to-all-start.1 = ((f32[32,1,5248]{2,1,0:T(1,128)}), f32[32,1,5248]{2,1,0:T(1,128)S(1)}, u32[]{:S(2)}, u32[]{:S(2)}) async-start(f32[32,1,5248]{2,1,0:T(1,128)} %reduce_sum.51), calls=%async_computation.1 | async-start | bytes 1343488 | tf_op jit(solution)/shard_map/all_to_all | solution.py:131
  44.0 15.8 %all-to-all-start.2 = ((bf16[32,32,128]{2,1,0:T(8,128)(2,1)}), bf16[32,32,128]{2,1,0:T(8,128)(2,1)S(1)}, u32[]{:S(2)}, u32[]{:S(2)}) async-start(bf16[32,32,128]{2,1,0:T(8,128)(2,1)} %broadcast_in_dim.26), calls=%async_computation.2 | async-start | bytes 524288 | tf_op jit(solution)/shard_map/all_to_all | solution.py:140
  81.3 1.1 copy-start.4
  81.3 1.2 copy-start.3
  107.9 2.7 %copy-start.1 = (bf16[64,4096]{1,0:T(8,128)(2,1)S(1)}, bf16[64,4096]{1,0:T(8,128)(2,1)}, u32[]{:S(2)}) copy-start(bf16[64,4096]{1,0:T(8,128)(2,1)} %param.12) | copy-start | bytes 1572868
  112.9 24.0 %copy-start.2 = (bf16[64,64]{1,0:T(8,128)(2,1)S(1)}, bf16[64,64]{1,0:T(8,128)(2,1)}, u32[]{:S(2)}) copy-start(bf16[64,64]{1,0:T(8,128)(2,1)} %param.9) | copy-start | bytes 24580

commit v11 on v10

--- a/solution.py
+++ b/solution.py
@@ -208,10 +208,11 @@
 
     partial_terms = jnp.dot(attended, w_out, preferred_element_type=jnp.float32)
     out_cols = model_width // tp_count
-    owner_terms = jnp.swapaxes(partial_terms.reshape(all_rows, tp_count, out_cols), 0, 1)
-    terms = spread(
-        owner_terms.reshape(tp_count, all_rows * out_cols // 128, 128).astype(jnp.bfloat16)
-    )
+    by_core = jnp.transpose(
+        partial_terms.reshape(all_rows, chips, cores, out_cols), (2, 1, 0, 3)
+    ).reshape(cores, chips, all_rows * out_cols // 128, 128)
+    chip_terms = jnp.sum(lax.all_to_all(by_core, "c", 0, 0, tiled=True), axis=0)
+    terms = lax.all_to_all(chip_terms.astype(jnp.bfloat16), CHIP, 0, 0, tiled=True)
     projected = jnp.sum(terms.astype(jnp.float32), axis=0).reshape(all_rows, out_cols)
     return (inputs + projected).astype(jnp.bfloat16)
 

time: 138 us -> 144 us (1.043)
  local copies, waits for them, and re-layouts: 12.9 us -> 17.8 us
  blocking collectives: 62.7 us -> 60.4 us
    all_to_all x2 -> x1, blocking collectives: 47.5 us -> 24.3 us  [spread(): return lax.all_to_all(pieces, TP, 0, 0, tiled=True)]
    all_to_all x0 -> x2, blocking collectives: none -> 20.9 us  [the longest x1 16.2 us: on_device(): lax.all_to_all(chip_terms.astype(jnp.bfloat16), CHIP, 0, 0, tiled=True)]
    reshape x0 -> x3, local copies, waits for them, and re-layouts: none -> 7.16 us  [the longest x2 5.36 us: on_device(): partial_terms.reshape(all_rows, chips, cores, out_cols)]
    convert_element_type x3 -> x0, local copies, waits for them, and re-layouts: 2.28 us -> none  [on_device(): owner_terms.reshape(tp_count, all_rows * out_cols // 128, 128)]
where the time goes in v11:
time: 144 us; the launch traced here: 142 us
  blocking collectives  60.4 us (42%)
  waiting for transfers between devices  26.8 us (19%)
  local copies, waits for them, and re-layouts  17.8 us (12%)
  starting transfers between devices  14.9 us (10%)
  Pallas kernels  8.57 us (6%)
  other arithmetic  6.35 us (4%)
  matrix products  5.23 us (4%)
  between operations  2.32 us (2%)
    all_to_all x1, blocking collectives, spread(): return lax.all_to_all(pieces, TP, 0, 0, tiled=True)  24.3 us
    all_to_all x1, waiting for transfers between devices, on_device(): gathered = lax.all_to_all(chip_sum, CHIP, 0, 0, tiled=True)  18.2 us
    all_to_all x1, blocking collectives, on_device(): lax.all_to_all(chip_terms.astype(jnp.bfloat16), CHIP, 0, 0, tiled=True)  16.2 us
    all_to_all x1, starting transfers between devices, on_device(): gathered = lax.all_to_all(chip_sum, CHIP, 0, 0, tiled=True)  9.5 us
    all_to_all x1, waiting for transfers between devices, on_device(): lax.all_to_all(jnp.broadcast_to(own_queries.reshape(1, lanes, 128), (chip...  8.65 us
    pallas_call x1, Pallas kernels, local_attention(): pl.pallas_call(attention_kernel, grid_spec=pltpu.PrefetchScalarGridSpec(n...  8.57 us
    all_to_all x1, blocking collectives, on_device(): chip_sum = jnp.sum(lax.all_to_all(by_core, 'c', 1, 1, tiled=True), axis=1)  7.62 us
    all_to_all x1, blocking collectives, on_device(): lax.all_to_all(jnp.broadcast_to(chip_rows[None], (cores, chips, lanes, 12...  7.54 us
  transfers between devices with their start and end apart: 2, of which 2 were waited for; matrix products, arithmetic and copies ran while one was open for 1% of the time, Pallas kernels for 0%

profile of v11, /device:TPU:1, one launch (start us, length us, event | category | flops | bytes accessed | tf_op | source)
XLA Modules:
  0.0 142.4 jit_solution(1362514474767852173)
XLA Ops:
  0.7 0.8 fusion.8
  1.6 1.0 fusion.15
  2.8 0.8 reshape.274
  3.7 7.6 %all_to_all.35 = f32[32,2,1,5248]{3,0,2,1:T(8,128)S(1)} all-to-all(f32[32,2,1,5248]{3,0,2,1:T(8,128)S(1)} %copy.22), channel_id=1, replica_groups=mesh['req'=4,'z'=8,'y'=4,'c'=2] {'c'}, dimensions={1} | all-to-all | bytes 2686976 | tf_op jit(solution)/shard_map/all_to_all | solution.py:130
  11.4 1.3 reduce_sum.60
  12.8 9.5 %all-to-all-start.1 = ((f32[32,1,5248]{2,1,0:T(1,128)}), f32[32,1,5248]{2,1,0:T(1,128)S(1)}, u32[]{:S(2)}, u32[]{:S(2)}) async-start(f32[32,1,5248]{2,1,0:T(1,128)} %reduce_sum.60), calls=%async_computation.1 | async-start | bytes 1343488 | tf_op jit(solution)/shard_map/all_to_all | solution.py:131
  23.4 18.2 %all-to-all-done.1 = f32[32,1,5248]{2,1,0:T(1,128)S(1)} async-done(((f32[32,1,5248]{2,1,0:T(1,128)}), f32[32,1,5248]{2,1,0:T(1,128)S(1)}, u32[]{:S(2)}, u32[]{:S(2)}) %all-to-all-start.1) | async-done | bytes 671776 | tf_op jit(solution)/shard_map/all_to_all | solution.py:131
  43.3 0.7 broadcast_in_dim.26
  44.0 5.4 %all-to-all-start.2 = ((bf16[32,32,128]{2,1,0:T(8,128)(2,1)}), bf16[32,32,128]{2,1,0:T(8,128)(2,1)S(1)}, u32[]{:S(2)}, u32[]{:S(2)}) async-start(bf16[32,32,128]{2,1,0:T(8,128)(2,1)} %broadcast_in_dim.26), calls=%async_computation.2 | async-start | bytes 524288 | tf_op jit(solution)/shard_map/all_to_all | solution.py:140
  51.2 8.7 %all-to-all-done.2 = bf16[32,32,128]{2,1,0:T(8,128)(2,1)S(1)} async-done(((bf16[32,32,128]{2,1,0:T(8,128)(2,1)}), bf16[32,32,128]{2,1,0:T(8,128)(2,1)S(1)}, u32[]{:S(2)}, u32[]{:S(2)}) %all-to-all-start.2) | async-done | bytes 262176 | tf_op jit(solution)/shard_map/all_to_all | solution.py:140
  60.0 7.5 %all_to_all.36 = bf16[2,32,32,128]{3,1,2,0:T(8,128)(2,1)S(1)} all-to-all(bf16[2,32,32,128]{3,1,2,0:T(8,128)(2,1)S(1)} %broadcast_in_dim.27), channel_id=1, replica_groups=mesh['req'=4,'z'=8,'y'=4,'c'=2] {'c'}, dimensions={0} | all-to-all | bytes 1048576 | tf_op jit(solution)/shard_map/all_to_all | solution.py:143
  67.8 1.0 copy.25
  70.0 8.6 %shard_map.94 = (f32[4,512,128]{2,1,0:T(8,128)}, f32[4,1,512]{2,1,0:T(1,128)}, f32[4,1,512]{2,1,0:T(1,128)}, f32[4,1,512]{2,1,0:T(1,128)}) custom-call(s32[1]{0:T(128)S(6)} %sub.27.limit_ref, bf16[4,512,128]{2,1,0:T(8,128)(2,1)} %bitcast.77, bf16[1024,512]{1,0:T(8,128)(2,1)} %bitcast.78, bf16[1024,512]{1,0:T(8,128)(2,1)} %bitcast.79, ...), custom_call_target="tpu_custom_call" | custom-call | tf_op jit(solution)/shard_map/pallas_call | solution.py:67
  80.9 1.6 %add_convert_fusion = bf16[4,512,128]{2,1,0:T(8,128)(2,1)S(1)} fusion(f32[4,512,128]{2,1,0:T(8,128)} %get-tuple-element.9, f32[4,128]{1,0:T(4,128)S(1)} %bitcast.86, f32[4,512]{1,0:T(4,128)S(1)} %bitcast.83), kind=kLoop, calls=%fused_computation.16 | loop fusion | flops 786432 | bytes 1583104 | tf_op jit(solution)/shard_map/convert_element_type | solution.py:190
  83.1 0.8 convert_element_type.149
  84.6 24.3 %all_to_all.37 = bf16[64,36,128]{2,1,0:T(8,128)(2,1)S(1)} all-to-all(bf16[64,36,128]{2,1,0:T(8,128)(2,1)S(1)} %reshape.280), channel_id=1, replica_groups=mesh['req'=4,'z'=8,'y'=4,'c'=2] {'z','y','c'}, dimensions={0} | all-to-all | bytes 1179648 | tf_op jit(solution)/shard_map/all_to_all | solution.py:104
  109.3 1.1 reshape.282
  110.4 1.6 %fusion.3 = f32[64,1,64]{2,1,0:T(1,128)S(1)} fusion(f32[64,64,1]{0,2,1:T(1,128)S(1)} %copy.28, bf16[64,64,64]{2,1,0:T(8,128)(2,1)S(1)} %reshape.282), kind=kOutput, calls=%fused_computation.13 | convolution fusion | flops 3145728 | bytes 557056 | tf_op jit(solution)/shard_map/st,stc->tc/dot_general | solution.py:204
  112.0 1.4 fusion.14
  113.4 2.8 %reshape.283 = f32[64,32,2,64]{3,2,1,0:T(2,128)S(1)} reshape(f32[64,4096]{1,0:T(8,128)} %fusion.14) | data formatting | bytes 2097152 | tf_op jit(solution)/shard_map/reshape | solution.py:212
  116.2 2.6 %copy.39 = f32[64,32,2,64]{3,0,1,2:T(8,128)} copy(f32[64,32,2,64]{3,2,1,0:T(2,128)S(1)} %reshape.283) | data formatting | bytes 2097152 | tf_op jit(solution)/shard_map/reshape | solution.py:212
  118.8 1.8 %reshape.284 = f32[2,32,32,128]{3,2,1,0:T(8,128)S(1)} reshape(f32[2,32,64,64]{3,2,1,0:T(8,128)} %bitcast.70) | data formatting | bytes 2097152 | tf_op jit(solution)/shard_map/reshape | solution.py:213
  120.6 4.7 %all_to_all.38 = f32[2,32,32,128]{3,2,1,0:T(8,128)S(1)} all-to-all(f32[2,32,32,128]{3,2,1,0:T(8,128)S(1)} %reshape.284), channel_id=1, replica_groups=mesh['req'=4,'z'=8,'y'=4,'c'=2] {'c'}, dimensions={0} | all-to-all | bytes 2097152 | tf_op jit(solution)/shard_map/all_to_all | solution.py:214
  125.4 16.2 %all_to_all.39 = bf16[32,32,128]{2,1,0:T(8,128)(2,1)S(1)} all-to-all(bf16[32,32,128]{2,1,0:T(8,128)(2,1)S(1)} %reduce_sum.64), channel_id=1, replica_groups=mesh['req'=4,'z'=8,'y'=4,'c'=2] {'z','y'}, dimensions={0} | all-to-all | bytes 524288 | tf_op jit(solution)/shard_map/all_to_all | solution.py:215
  (57 shorter events, 10.1 us)
Async XLA Ops:
  0.0 1.6 %copy-start = (bf16[64,5120]{1,0:T(8,128)(2,1)S(1)}, bf16[64,5120]{1,0:T(8,128)(2,1)}, u32[]{:S(2)}) copy-start(bf16[64,5120]{1,0:T(8,128)(2,1)} %param.11) | copy-start | bytes 1966084
  11.4 10.8 %copy-start.3 = (s32[1,64]{1,0:T(1,128)S(1)}, s32[1,64]{1,0:T(1,128)}, u32[]{:S(2)}) copy-start(s32[1,64]{1,0:T(1,128)} %param.15) | copy-start | bytes 772
  12.8 28.8 %all-to-all-start.1 = ((f32[32,1,5248]{2,1,0:T(1,128)}), f32[32,1,5248]{2,1,0:T(1,128)S(1)}, u32[]{:S(2)}, u32[]{:S(2)}) async-start(f32[32,1,5248]{2,1,0:T(1,128)} %reduce_sum.60), calls=%async_computation.1 | async-start | bytes 1343488 | tf_op jit(solution)/shard_map/all_to_all | solution.py:131
  44.0 15.8 %all-to-all-start.2 = ((bf16[32,32,128]{2,1,0:T(8,128)(2,1)}), bf16[32,32,128]{2,1,0:T(8,128)(2,1)S(1)}, u32[]{:S(2)}, u32[]{:S(2)}) async-start(bf16[32,32,128]{2,1,0:T(8,128)(2,1)} %broadcast_in_dim.26), calls=%async_computation.2 | async-start | bytes 524288 | tf_op jit(solution)/shard_map/all_to_all | solution.py:140
  109.3 2.7 %copy-start.1 = (bf16[64,4096]{1,0:T(8,128)(2,1)S(1)}, bf16[64,4096]{1,0:T(8,128)(2,1)}, u32[]{:S(2)}) copy-start(bf16[64,4096]{1,0:T(8,128)(2,1)} %param.12) | copy-start | bytes 1572868
  125.3 16.4 %copy-start.2 = (bf16[64,64]{1,0:T(8,128)(2,1)S(1)}, bf16[64,64]{1,0:T(8,128)(2,1)}, u32[]{:S(2)}) copy-start(bf16[64,64]{1,0:T(8,128)(2,1)} %param.9) | copy-start | bytes 24580

commit v12 on v10

--- a/solution.py
+++ b/solution.py
@@ -30,9 +30,9 @@
 
 
 def attention_kernel(limit_ref, q_ref, k_ref, v_ref, tk_ref, tb_ref, o_ref, m_ref, l_ref, w_ref):
-    rows, places = q_ref.shape[1], k_ref.shape[0]
+    rows, places = q_ref.shape[0] * q_ref.shape[1], k_ref.shape[0]
     scale = HEAD ** (-0.5)
-    query = q_ref[0]
+    query = q_ref[...].reshape(rows, HEAD)
     scores = (
         lax.dot_general(
             k_ref[...], query, (((1,), (1,)), ((), ())), preferred_element_type=jnp.float32
@@ -61,7 +61,8 @@
 
 
 def local_attention(limit, query, keys, values, tree_keys, tree_valid):
-    rows = query.shape[1]
+    tokens, groups = query.shape[0], HEADS // KV_HEADS
+    rows = tokens * groups
     places = keys.shape[0]
     lane_row = pl.BlockSpec((1, 1, rows), lambda k, lim: (k, 0, 0))
     return pl.pallas_call(
@@ -70,7 +71,7 @@
             num_scalar_prefetch=1,
             grid=(KV_HEADS,),
             in_specs=[
-                pl.BlockSpec((1, rows, HEAD), lambda k, lim: (k, 0, 0)),
+                pl.BlockSpec((tokens, groups, HEAD), lambda k, lim: (0, k, 0)),
                 pl.BlockSpec((places, HEAD), lambda k, lim: (0, k)),
                 pl.BlockSpec((places, HEAD), lambda k, lim: (0, k)),
                 pl.BlockSpec((1, 8, HEAD), lambda k, lim: (k, 0, 0)),
@@ -143,7 +144,7 @@
     core_rows = lax.all_to_all(
         jnp.broadcast_to(chip_rows[None], (cores, chips, lanes, 128)), "c", 0, 0, tiled=True
     )
-    query = jnp.swapaxes(core_rows, 0, 1).reshape(all_rows, model_width)
+    query = core_rows.reshape(all_rows, HEADS, HEAD)
     own_tokens = own_qkv[:, model_width:]
     own_keys = own_tokens[:, :kv_width].reshape(own_count, KV_HEADS, HEAD)
     own_values = own_tokens[:, kv_width:].reshape(own_count, KV_HEADS, HEAD)
@@ -158,25 +159,31 @@
     on_path = jnp.dot(reached, column_pick, precision=lax.Precision.HIGHEST) > 0.5
     tree_mask = on_path & (key_place < draft_counts[0])[None, :]
 
-    query_heads = query.reshape(all_rows, KV_HEADS, groups, HEAD)
     limit = (cache_lengths[:1] - tp_rank * places_dev).astype(jnp.int32)
-    head_rows = jnp.transpose(query_heads, (1, 2, 0, 3)).reshape(KV_HEADS, groups * all_rows, HEAD)
+    valid_rows = jnp.swapaxes(tree_mask[:, 0].astype(jnp.float32).reshape(chips, cores), 0, 1)
     tree_valid = jnp.broadcast_to(
-        tree_mask[:, 0].astype(jnp.float32)[None, None, None, :], (KV_HEADS, 1, groups, all_rows)
+        valid_rows[None, None, :, :, None], (KV_HEADS, 1, cores, chips, groups)
     ).reshape(KV_HEADS, 1, groups * all_rows)
     cache_mixed, top_parts, total_parts, tree_weight = local_attention(
         limit,
-        head_rows,
+        query,
         cache_keys[0],
         cache_values[0],
         jnp.broadcast_to(own_keys[0][:, None, :], (KV_HEADS, 8, HEAD)),
         tree_valid,
     )
-    head_mixed = cache_mixed + jnp.swapaxes(tree_weight, 1, 2) * own_values[0].reshape(
+    row_mixed = cache_mixed + jnp.swapaxes(tree_weight, 1, 2) * own_values[0].reshape(
         KV_HEADS, 1, HEAD
     ).astype(jnp.float32)
-    local_top = top_parts.reshape(HEADS, all_rows)
-    totals = total_parts.reshape(HEADS, all_rows)
+    head_mixed = jnp.transpose(
+        row_mixed.reshape(KV_HEADS, cores, chips, groups, HEAD), (0, 3, 2, 1, 4)
+    ).reshape(HEADS, all_rows, HEAD)
+    local_top = jnp.transpose(
+        top_parts.reshape(KV_HEADS, cores, chips, groups), (0, 3, 2, 1)
+    ).reshape(HEADS, all_rows)
+    totals = jnp.transpose(
+        total_parts.reshape(KV_HEADS, cores, chips, groups), (0, 3, 2, 1)
+    ).reshape(HEADS, all_rows)
 
     columns = w_out.shape[0]
     per_head = HEAD // columns

time: 138 us -> 139 us (level)
    convert_element_type x2 -> x1, other arithmetic: 1.61 us -> 0.02 us  [on_device(): row_mixed = cache_mixed + jnp.swapaxes(tree_weight, 1, 2) * own_values[0]...]
    another operation x0 -> x1, other arithmetic: none -> 1.56 us
where the time goes in v12:
time: 139 us
  blocking collectives  63.5 us (46%)
  waiting for transfers between devices  26.5 us (19%)
  starting transfers between devices  14.9 us (11%)
  local copies, waits for them, and re-layouts  13.6 us (10%)
  Pallas kernels  8.58 us (6%)
  other arithmetic  4.9 us (4%)
  matrix products  4.23 us (3%)
  between operations  2.4 us (2%)
    all_to_all x2, blocking collectives, spread(): return lax.all_to_all(pieces, TP, 0, 0, tiled=True)  47.5 us
    all_to_all x1, waiting for transfers between devices, on_device(): gathered = lax.all_to_all(chip_sum, CHIP, 0, 0, tiled=True)  18.2 us
    all_to_all x1, starting transfers between devices, on_device(): gathered = lax.all_to_all(chip_sum, CHIP, 0, 0, tiled=True)  9.49 us
    pallas_call x1, Pallas kernels, local_attention(): pl.pallas_call(attention_kernel, grid_spec=pltpu.PrefetchScalarGridSpec(n...  8.58 us
    all_to_all x1, waiting for transfers between devices, on_device(): lax.all_to_all(jnp.broadcast_to(own_queries.reshape(1, lanes, 128), (chip...  8.36 us
    all_to_all x1, blocking collectives, on_device(): lax.all_to_all(jnp.broadcast_to(chip_rows[None], (cores, chips, lanes, 12...  8.3 us
    all_to_all x1, blocking collectives, on_device(): chip_sum = jnp.sum(lax.all_to_all(by_core, 'c', 1, 1, tiled=True), axis=1)  7.63 us
    all_to_all x1, starting transfers between devices, on_device(): lax.all_to_all(jnp.broadcast_to(own_queries.reshape(1, lanes, 128), (chip...  5.42 us
  transfers between devices with their start and end apart: 2, of which 2 were waited for; matrix products, arithmetic and copies ran while one was open for 1% of the time, Pallas kernels for 0%

profile of v12, /device:TPU:1, one launch (start us, length us, event | category | flops | bytes accessed | tf_op | source)
XLA Modules:
  0.0 138.6 jit_solution(13971976663623409403)
XLA Ops:
  0.0 0.9 fusion.8
  0.9 0.7 convert_element_type.148
  1.6 1.0 fusion.14
  2.8 0.8 reshape.283
  3.7 7.6 %all_to_all.30 = f32[32,2,1,5248]{3,0,2,1:T(8,128)S(1)} all-to-all(f32[32,2,1,5248]{3,0,2,1:T(8,128)S(1)} %copy.19), channel_id=1, replica_groups=mesh['req'=4,'z'=8,'y'=4,'c'=2] {'c'}, dimensions={1} | all-to-all | bytes 2686976 | tf_op jit(solution)/shard_map/all_to_all | solution.py:131
  11.4 1.3 reduce_sum.51
  12.8 9.5 %all-to-all-start.1 = ((f32[32,1,5248]{2,1,0:T(1,128)}), f32[32,1,5248]{2,1,0:T(1,128)S(1)}, u32[]{:S(2)}, u32[]{:S(2)}) async-start(f32[32,1,5248]{2,1,0:T(1,128)} %reduce_sum.51), calls=%async_computation.1 | async-start | bytes 1343488 | tf_op jit(solution)/shard_map/all_to_all | solution.py:132
  23.4 18.2 %all-to-all-done.1 = f32[32,1,5248]{2,1,0:T(1,128)S(1)} async-done(((f32[32,1,5248]{2,1,0:T(1,128)}), f32[32,1,5248]{2,1,0:T(1,128)S(1)}, u32[]{:S(2)}, u32[]{:S(2)}) %all-to-all-start.1) | async-done | bytes 671776 | tf_op jit(solution)/shard_map/all_to_all | solution.py:132
  43.3 0.7 broadcast_in_dim.26
  44.0 5.4 %all-to-all-start.2 = ((bf16[32,32,128]{2,1,0:T(8,128)(2,1)}), bf16[32,32,128]{2,1,0:T(8,128)(2,1)S(1)}, u32[]{:S(2)}, u32[]{:S(2)}) async-start(bf16[32,32,128]{2,1,0:T(8,128)(2,1)} %broadcast_in_dim.26), calls=%async_computation.2 | async-start | bytes 524288 | tf_op jit(solution)/shard_map/all_to_all | solution.py:141
  51.5 8.4 %all-to-all-done.2 = bf16[32,32,128]{2,1,0:T(8,128)(2,1)S(1)} async-done(((bf16[32,32,128]{2,1,0:T(8,128)(2,1)}), bf16[32,32,128]{2,1,0:T(8,128)(2,1)S(1)}, u32[]{:S(2)}, u32[]{:S(2)}) %all-to-all-start.2) | async-done | bytes 262176 | tf_op jit(solution)/shard_map/all_to_all | solution.py:141
  59.9 8.3 %all_to_all.31 = bf16[2,32,32,128]{3,2,1,0:T(8,128)(2,1)} all-to-all(bf16[2,32,32,128]{3,2,1,0:T(8,128)(2,1)S(1)} %broadcast_in_dim.27), channel_id=1, replica_groups=mesh['req'=4,'z'=8,'y'=4,'c'=2] {'c'}, dimensions={0} | all-to-all | bytes 1048576 | tf_op jit(solution)/shard_map/all_to_all | solution.py:144
  69.4 8.6 %shard_map.94 = (f32[4,512,128]{2,1,0:T(8,128)}, f32[4,1,512]{2,1,0:T(1,128)}, f32[4,1,512]{2,1,0:T(1,128)}, f32[4,1,512]{2,1,0:T(1,128)}) custom-call(s32[1]{0:T(128)S(6)} %sub.27.limit_ref, bf16[64,32,128]{2,1,0:T(8,128)(2,1)} %bitcast.84, bf16[1024,512]{1,0:T(8,128)(2,1)} %bitcast.85, bf16[1024,512]{1,0:T(8,128)(2,1)} %bitcast.86, ...), custom_call_target="tpu_custom_call" | custom-call | tf_op jit(solution)/shard_map/pallas_call | solution.py:68
  78.0 0.7 copy.42
  78.7 1.6 %add_convert_fusion = bf16[4,512,128]{2,1,0:T(8,128)(2,1)S(1)} fusion(f32[4,512,128]{2,1,0:T(8,128)} %get-tuple-element.9, f32[4,128]{1,0:T(4,128)S(1)} %bitcast.96, f32[4,512]{1,0:T(4,128)S(1)} %bitcast.93), kind=kLoop, calls=%fused_computation.17 | loop fusion | flops 786432 | bytes 1583104 | tf_op jit(solution)/shard_map/convert.3
  80.8 1.2 copy.22
  82.1 0.8 convert_element_type.159
  84.5 24.3 %all_to_all.32 = bf16[64,36,128]{2,1,0:T(8,128)(2,1)S(1)} all-to-all(bf16[64,36,128]{2,1,0:T(8,128)(2,1)S(1)} %reshape.292), channel_id=1, replica_groups=mesh['req'=4,'z'=8,'y'=4,'c'=2] {'z','y','c'}, dimensions={0} | all-to-all | bytes 1179648 | tf_op jit(solution)/shard_map/all_to_all | solution.py:105
  109.1 1.1 reshape.294
  110.3 1.6 %fusion.3 = f32[64,1,64]{2,1,0:T(1,128)S(1)} fusion(f32[64,64,1]{0,2,1:T(1,128)S(1)} %copy.28, bf16[64,64,64]{2,1,0:T(8,128)(2,1)S(1)} %reshape.294), kind=kOutput, calls=%fused_computation.13 | convolution fusion | flops 3145728 | bytes 557056 | tf_op jit(solution)/shard_map/st,stc->tc/dot_general | solution.py:211
  112.2 1.1 convert_element_type.174
  113.4 0.7 copy.39
  114.5 23.3 %all_to_all.33 = bf16[64,32,128]{2,1,0:T(8,128)(2,1)S(1)} all-to-all(bf16[64,32,128]{2,1,0:T(8,128)(2,1)S(1)} %convert_element_type.176), channel_id=1, replica_groups=mesh['req'=4,'z'=8,'y'=4,'c'=2] {'z','y','c'}, dimensions={0} | all-to-all | bytes 1048576 | tf_op jit(solution)/shard_map/all_to_all | solution.py:105
  138.0 0.6 fusion.9
  (65 shorter events, 7.9 us)
Async XLA Ops:
  0.0 1.6 %copy-start = (bf16[64,5120]{1,0:T(8,128)(2,1)S(1)}, bf16[64,5120]{1,0:T(8,128)(2,1)}, u32[]{:S(2)}) copy-start(bf16[64,5120]{1,0:T(8,128)(2,1)} %param.11) | copy-start | bytes 1966084
  11.4 10.8 %copy-start.5 = (s32[1,64]{1,0:T(1,128)S(1)}, s32[1,64]{1,0:T(1,128)}, u32[]{:S(2)}) copy-start(s32[1,64]{1,0:T(1,128)} %param.15) | copy-start | bytes 772
  12.8 28.8 %all-to-all-start.1 = ((f32[32,1,5248]{2,1,0:T(1,128)}), f32[32,1,5248]{2,1,0:T(1,128)S(1)}, u32[]{:S(2)}, u32[]{:S(2)}) async-start(f32[32,1,5248]{2,1,0:T(1,128)} %reduce_sum.51), calls=%async_computation.1 | async-start | bytes 1343488 | tf_op jit(solution)/shard_map/all_to_all | solution.py:132
  44.0 15.8 %all-to-all-start.2 = ((bf16[32,32,128]{2,1,0:T(8,128)(2,1)}), bf16[32,32,128]{2,1,0:T(8,128)(2,1)S(1)}, u32[]{:S(2)}, u32[]{:S(2)}) async-start(bf16[32,32,128]{2,1,0:T(8,128)(2,1)} %broadcast_in_dim.26), calls=%async_computation.2 | async-start | bytes 524288 | tf_op jit(solution)/shard_map/all_to_all | solution.py:141
  80.8 2.1 %copy-start.4 = (f32[4,1,512]{2,1,0:T(1,128)S(1)}, f32[4,1,512]{2,1,0:T(1,128)}, u32[]{:S(2)}) copy-start(f32[4,1,512]{2,1,0:T(1,128)} %get-tuple-element.11) | copy-start | bytes 24580
  82.1 1.3 copy-start.3
  109.1 2.7 %copy-start.1 = (bf16[64,4096]{1,0:T(8,128)(2,1)S(1)}, bf16[64,4096]{1,0:T(8,128)(2,1)}, u32[]{:S(2)}) copy-start(bf16[64,4096]{1,0:T(8,128)(2,1)} %param.12) | copy-start | bytes 1572868
  114.0 24.0 %copy-start.2 = (bf16[64,64]{1,0:T(8,128)(2,1)S(1)}, bf16[64,64]{1,0:T(8,128)(2,1)}, u32[]{:S(2)}) copy-start(bf16[64,64]{1,0:T(8,128)(2,1)} %param.9) | copy-start | bytes 24580

commit v13 on v10

--- a/solution.py
+++ b/solution.py
@@ -94,6 +94,11 @@
     middle = lax.reduce_precision(rest, exponent_bits=8, mantissa_bits=7)
     low = rest - middle
     return [high.astype(jnp.bfloat16), middle.astype(jnp.bfloat16), low.astype(jnp.bfloat16)]
+
+
+def split2(values):
+    high = lax.reduce_precision(values, exponent_bits=8, mantissa_bits=7)
+    return [high.astype(jnp.bfloat16), (values - high).astype(jnp.bfloat16)]
 
 
 def join3(high, middle, low):
@@ -188,18 +193,17 @@
     owner_totals = jnp.repeat(totals, per_head, 0)
     packed = jnp.concatenate(
         [owner_mixed.astype(jnp.bfloat16)]
-        + split3(owner_top)
-        + split3(owner_totals)
-        + [jnp.zeros((tp_count, 128 - (6 * all_rows) % 128), jnp.bfloat16)],
+        + split2(owner_top)
+        + split2(owner_totals),
         axis=1,
     )
     got = spread(packed.reshape(tp_count, -1, 128)).reshape(tp_count, -1)
     flat = all_rows * columns
-    piece = [got[:, flat + i * all_rows : flat + (i + 1) * all_rows] for i in range(6)]
-    source_top = join3(*piece[:3])
+    piece = [got[:, flat + i * all_rows : flat + (i + 1) * all_rows].astype(jnp.float32) for i in range(4)]
+    source_top = piece[0] + piece[1]
     top = jnp.max(source_top, axis=0)
     rescale = jnp.exp(source_top - top[None])
-    total = jnp.sum(rescale * join3(*piece[3:]), axis=0)
+    total = jnp.sum(rescale * (piece[2] + piece[3]), axis=0)
     source_mixed = got[:, :flat].reshape(tp_count, all_rows, columns).astype(jnp.float32)
     mixed_cols = jnp.einsum(
         "st,stc->tc", rescale, source_mixed, precision=lax.Precision.HIGHEST

time: 138 us -> 138 us (level)
  no operation moved by 1% of the time
where the time goes in v13:
time: 138 us; the launch traced here: 137 us
  blocking collectives  62.7 us (45%)
  waiting for transfers between devices  26.8 us (19%)
  starting transfers between devices  14.9 us (11%)
  local copies, waits for them, and re-layouts  12.9 us (9%)
  Pallas kernels  8.57 us (6%)
  other arithmetic  4.91 us (4%)
  matrix products  4.23 us (3%)
  between operations  2.35 us (2%)
    all_to_all x2, blocking collectives, spread(): return lax.all_to_all(pieces, TP, 0, 0, tiled=True)  47.5 us
    all_to_all x1, waiting for transfers between devices, on_device(): gathered = lax.all_to_all(chip_sum, CHIP, 0, 0, tiled=True)  18.2 us
    all_to_all x1, starting transfers between devices, on_device(): gathered = lax.all_to_all(chip_sum, CHIP, 0, 0, tiled=True)  9.49 us
    all_to_all x1, waiting for transfers between devices, on_device(): lax.all_to_all(jnp.broadcast_to(own_queries.reshape(1, lanes, 128), (chip...  8.65 us
    pallas_call x1, Pallas kernels, local_attention(): pl.pallas_call(attention_kernel, grid_spec=pltpu.PrefetchScalarGridSpec(n...  8.57 us
    all_to_all x1, blocking collectives, on_device(): chip_sum = jnp.sum(lax.all_to_all(by_core, 'c', 1, 1, tiled=True), axis=1)  7.63 us
    all_to_all x1, blocking collectives, on_device(): lax.all_to_all(jnp.broadcast_to(chip_rows[None], (cores, chips, lanes, 12...  7.54 us
    all_to_all x1, starting transfers between devices, on_device(): lax.all_to_all(jnp.broadcast_to(own_queries.reshape(1, lanes, 128), (chip...  5.42 us
  transfers between devices with their start and end apart: 2, of which 2 were waited for; matrix products, arithmetic and copies ran while one was open for 1% of the time, Pallas kernels for 0%

profile of v13, /device:TPU:1, one launch (start us, length us, event | category | flops | bytes accessed | tf_op | source)
XLA Modules:
  0.0 137.3 jit_solution(11229471876812938371)
XLA Ops:
  0.0 0.9 fusion.8
  0.9 0.7 convert_element_type.135
  1.6 1.0 fusion.15
  2.8 0.8 reshape.272
  3.7 7.6 %all_to_all.30 = f32[32,2,1,5248]{3,0,2,1:T(8,128)S(1)} all-to-all(f32[32,2,1,5248]{3,0,2,1:T(8,128)S(1)} %copy.16), channel_id=1, replica_groups=mesh['req'=4,'z'=8,'y'=4,'c'=2] {'c'}, dimensions={1} | all-to-all | bytes 2686976 | tf_op jit(solution)/shard_map/all_to_all | solution.py:135
  11.4 1.3 reduce_sum.51
  12.8 9.5 %all-to-all-start.1 = ((f32[32,1,5248]{2,1,0:T(1,128)}), f32[32,1,5248]{2,1,0:T(1,128)S(1)}, u32[]{:S(2)}, u32[]{:S(2)}) async-start(f32[32,1,5248]{2,1,0:T(1,128)} %reduce_sum.51), calls=%async_computation.1 | async-start | bytes 1343488 | tf_op jit(solution)/shard_map/all_to_all | solution.py:136
  23.4 18.2 %all-to-all-done.1 = f32[32,1,5248]{2,1,0:T(1,128)S(1)} async-done(((f32[32,1,5248]{2,1,0:T(1,128)}), f32[32,1,5248]{2,1,0:T(1,128)S(1)}, u32[]{:S(2)}, u32[]{:S(2)}) %all-to-all-start.1) | async-done | bytes 671776 | tf_op jit(solution)/shard_map/all_to_all | solution.py:136
  43.3 0.7 broadcast_in_dim.24
  44.0 5.4 %all-to-all-start.2 = ((bf16[32,32,128]{2,1,0:T(8,128)(2,1)}), bf16[32,32,128]{2,1,0:T(8,128)(2,1)S(1)}, u32[]{:S(2)}, u32[]{:S(2)}) async-start(bf16[32,32,128]{2,1,0:T(8,128)(2,1)} %broadcast_in_dim.24), calls=%async_computation.2 | async-start | bytes 524288 | tf_op jit(solution)/shard_map/all_to_all | solution.py:145
  51.2 8.7 %all-to-all-done.2 = bf16[32,32,128]{2,1,0:T(8,128)(2,1)S(1)} async-done(((bf16[32,32,128]{2,1,0:T(8,128)(2,1)}), bf16[32,32,128]{2,1,0:T(8,128)(2,1)S(1)}, u32[]{:S(2)}, u32[]{:S(2)}) %all-to-all-start.2) | async-done | bytes 262176 | tf_op jit(solution)/shard_map/all_to_all | solution.py:145
  60.0 7.5 %all_to_all.31 = bf16[2,32,32,128]{3,1,2,0:T(8,128)(2,1)S(1)} all-to-all(bf16[2,32,32,128]{3,1,2,0:T(8,128)(2,1)S(1)} %broadcast_in_dim.25), channel_id=1, replica_groups=mesh['req'=4,'z'=8,'y'=4,'c'=2] {'c'}, dimensions={0} | all-to-all | bytes 1048576 | tf_op jit(solution)/shard_map/all_to_all | solution.py:148
  67.8 1.0 copy.19
  70.0 8.6 %shard_map.94 = (f32[4,512,128]{2,1,0:T(8,128)}, f32[4,1,512]{2,1,0:T(1,128)}, f32[4,1,512]{2,1,0:T(1,128)}, f32[4,1,512]{2,1,0:T(1,128)}) custom-call(s32[1]{0:T(128)S(6)} %sub.21.limit_ref, bf16[4,512,128]{2,1,0:T(8,128)(2,1)} %bitcast.75, bf16[1024,512]{1,0:T(8,128)(2,1)} %bitcast.76, bf16[1024,512]{1,0:T(8,128)(2,1)} %bitcast.77, ...), custom_call_target="tpu_custom_call" | custom-call | tf_op jit(solution)/shard_map/pallas_call | solution.py:67
  78.6 0.7 copy.36
  79.3 1.6 %add_convert_fusion = bf16[4,512,128]{2,1,0:T(8,128)(2,1)S(1)} fusion(f32[4,512,128]{2,1,0:T(8,128)} %get-tuple-element.9, f32[4,128]{1,0:T(4,128)S(1)} %bitcast.84, f32[4,512]{1,0:T(4,128)S(1)} %bitcast.81), kind=kLoop, calls=%fused_computation.18 | loop fusion | flops 786432 | bytes 1583104 | tf_op jit(solution)/shard_map/convert_element_type | solution.py:195
  81.5 0.8 convert_element_type.146
  83.2 24.3 %all_to_all.32 = bf16[64,34,128]{2,1,0:T(8,128)(2,1)S(1)} all-to-all(bf16[64,34,128]{2,1,0:T(8,128)(2,1)S(1)} %reshape.278), channel_id=1, replica_groups=mesh['req'=4,'z'=8,'y'=4,'c'=2] {'z','y','c'}, dimensions={0} | all-to-all | bytes 1114112 | tf_op jit(solution)/shard_map/all_to_all | solution.py:109
  107.9 1.1 reshape.280
  109.0 1.6 %fusion.3 = f32[64,1,64]{2,1,0:T(1,128)S(1)} fusion(f32[64,64,1]{0,2,1:T(1,128)S(1)} %copy.22, bf16[64,64,64]{2,1,0:T(8,128)(2,1)S(1)} %reshape.280), kind=kOutput, calls=%fused_computation.13 | convolution fusion | flops 3145728 | bytes 557056 | tf_op jit(solution)/shard_map/st,stc->tc/dot_general | solution.py:208
  111.0 1.1 convert_element_type.157
  112.1 0.7 copy.33
  113.3 23.3 %all_to_all.33 = bf16[64,32,128]{2,1,0:T(8,128)(2,1)S(1)} all-to-all(bf16[64,32,128]{2,1,0:T(8,128)(2,1)S(1)} %convert_element_type.159), channel_id=1, replica_groups=mesh['req'=4,'z'=8,'y'=4,'c'=2] {'z','y','c'}, dimensions={0} | all-to-all | bytes 1048576 | tf_op jit(solution)/shard_map/all_to_all | solution.py:109
  136.7 0.6 fusion.9
  (58 shorter events, 7.3 us)
Async XLA Ops:
  0.0 1.6 %copy-start = (bf16[64,5120]{1,0:T(8,128)(2,1)S(1)}, bf16[64,5120]{1,0:T(8,128)(2,1)}, u32[]{:S(2)}) copy-start(bf16[64,5120]{1,0:T(8,128)(2,1)} %param.11) | copy-start | bytes 1966084
  11.4 10.8 %copy-start.5 = (s32[1,64]{1,0:T(1,128)S(1)}, s32[1,64]{1,0:T(1,128)}, u32[]{:S(2)}) copy-start(s32[1,64]{1,0:T(1,128)} %param.15) | copy-start | bytes 772
  12.8 28.8 %all-to-all-start.1 = ((f32[32,1,5248]{2,1,0:T(1,128)}), f32[32,1,5248]{2,1,0:T(1,128)S(1)}, u32[]{:S(2)}, u32[]{:S(2)}) async-start(f32[32,1,5248]{2,1,0:T(1,128)} %reduce_sum.51), calls=%async_computation.1 | async-start | bytes 1343488 | tf_op jit(solution)/shard_map/all_to_all | solution.py:136
  44.0 15.8 %all-to-all-start.2 = ((bf16[32,32,128]{2,1,0:T(8,128)(2,1)}), bf16[32,32,128]{2,1,0:T(8,128)(2,1)S(1)}, u32[]{:S(2)}, u32[]{:S(2)}) async-start(bf16[32,32,128]{2,1,0:T(8,128)(2,1)} %broadcast_in_dim.24), calls=%async_computation.2 | async-start | bytes 524288 | tf_op jit(solution)/shard_map/all_to_all | solution.py:145
  81.3 1.1 copy-start.4
  81.3 1.2 copy-start.3
  107.8 2.7 %copy-start.1 = (bf16[64,4096]{1,0:T(8,128)(2,1)S(1)}, bf16[64,4096]{1,0:T(8,128)(2,1)}, u32[]{:S(2)}) copy-start(bf16[64,4096]{1,0:T(8,128)(2,1)} %param.12) | copy-start | bytes 1572868
  112.8 24.0 %copy-start.2 = (bf16[64,64]{1,0:T(8,128)(2,1)S(1)}, bf16[64,64]{1,0:T(8,128)(2,1)}, u32[]{:S(2)}) copy-start(bf16[64,64]{1,0:T(8,128)(2,1)} %param.9) | copy-start | bytes 24580
